TPU v7x, 512 devices: a whole 4x8x8 slice. The times are simulated.
512 devices in a mesh: row: 16 (over y, z_hi), col: 32 (over x, z_lo, core).
Axes of the slice: x: 4, y: 8, z: 8 (z_hi: 2, z_lo: 4; z = z_hi * 4 + z_lo), core: 2. Of those that a mesh axis runs over, the one named last changes fastest.
Arguments:
- points: bfloat16 [81920, 128], P(('row', 'col')), may hold values from -6 to 6
- w_in: bfloat16 [128, 1024], replicated, may hold values from -0.5 to 0.5
- w_mid: bfloat16 [1024, 1024], replicated, may hold values from -0.1875 to 0.1875
- w_out: bfloat16 [1024, 32], replicated, may hold values from -0.1875 to 0.1875
- lengthscale: float32 [32], replicated, may hold values from 1 to 10
- probes: bfloat16 [8, 81920], P(None, ('row', 'col')), may hold values from -0.0546875 to 0.0546875
Outputs:
- kv: float32 [8, 81920], P(None, ('row', 'col'))
All inputs are finite; a program needn't handle non-finite values.
Results may differ from a plain program's by a relative error of at most 0.0055.
Values may be sent and summed in bfloat16 or wider, within the bound.
No kernel may reach another device: no remote copies, remote signals or barrier semaphores. Data moves between devices by JAX's collectives and lax.ppermute only.
A program may use at most 64 MiB of HBM per device.

v0:
```python
import jax
import jax.numpy as jnp
from jax import lax
from jax.sharding import PartitionSpec as P


def wide_general(left, right, dims):
    return lax.dot_general(
        left.astype(jnp.float32),
        right.astype(jnp.float32),
        (dims, ((), ())),
        precision=lax.Precision.HIGHEST,
    )


def matern_tile(left_feats, left_sq, right_feats):
    cross_term = wide_general(left_feats, right_feats, ((0,), (0,)))
    right_wide = right_feats.astype(jnp.float32)
    right_sq = jnp.sum(right_wide * right_wide, axis=0)
    dist_sq = jnp.maximum(left_sq[:, None] + right_sq[None, :] - 2.0 * cross_term, 0.0)
    scaled_dist = jnp.sqrt(5.0 * dist_sq)
    values = (1.0 + scaled_dist + scaled_dist * scaled_dist / 3.0) * jnp.exp(-scaled_dist)
    return values.astype(jnp.bfloat16)


def block_width(columns):
    for candidate in (256, 384, 128):
        return candidate
    return columns


def on_device(points, w_in, w_mid, w_out, lengthscale, probes):
    hidden_one = jax.nn.relu(wide_general(points, w_in, ((1,), (0,)))).astype(jnp.bfloat16)
    hidden_two = jax.nn.relu(wide_general(hidden_one, w_mid, ((1,), (0,)))).astype(jnp.bfloat16)
    features = wide_general(w_out, hidden_two, ((0,), (1,)))
    scaled = (features / lengthscale[:, None]).astype(jnp.bfloat16)
    probe_rows = probes.shape[0]
    row_feats = lax.all_gather(scaled, "col", axis=1, tiled=True)
    row_wide = row_feats.astype(jnp.float32)
    row_sq = jnp.sum(row_wide * row_wide, axis=0)
    initial = jnp.zeros((probe_rows, row_feats.shape[1]), jnp.float32)
    piece_feats = lax.all_gather(scaled, "row", axis=1, tiled=True)
    piece_probes = lax.all_gather(probes, "row", axis=1, tiled=True)
    block_cols = block_width(piece_feats.shape[1])

    def advance(position, row_acc):
        column_start = position * block_cols
        feats_block = lax.dynamic_slice_in_dim(piece_feats, column_start, block_cols, 1)
        probes_block = lax.dynamic_slice_in_dim(piece_probes, column_start, block_cols, 1)
        kernel_tile = matern_tile(row_feats, row_sq, feats_block)
        return row_acc + wide_general(probes_block, kernel_tile, ((1,), (1,)))

    folded = lax.fori_loop(0, piece_feats.shape[1] // block_cols, advance, initial)
    column_sums = 0.0
    row_sums = lax.psum_scatter(folded, "col", scatter_dimension=1, tiled=True)
    return row_sums + column_sums


def solution(mesh):
    in_specs = (P(("row", "col"), None), P(), P(), P(), P(), P(None, ("row", "col")))
    out_specs = P(None, ("row", "col"))
    return jax.shard_map(
        on_device, mesh=mesh, in_specs=in_specs, out_specs=out_specs, check_vma=False
    )
```

profile of v0, /device:TPU:1, one launch (start us, length us, event | category | flops | bytes accessed | tf_op | source)
XLA Modules:
  0.0 361.6 jit_solution(8537713413298541568)
XLA Ops:
  6.6 1.3 fusion.9
  8.2 0.5 fusion.10
  9.0 53.4 %all-gather.2 = bf16[16,160,32]{1,2,0:T(8,128)(2,1)S(1)} all-gather(bf16[1,160,32]{1,2,0:T(8,128)(2,1)S(1)} %fusion.12), channel_id=1, replica_groups=mesh['row'=16,'col'=32] {'row'}, dimensions={0}, use_global_device_ids=true | all-gather | bytes 174080 | tf_op jit(solution)/shard_map/all_gather | solution.py:42
  62.4 52.0 %all-gather.1 = bf16[32,160,32]{1,2,0:T(8,128)(2,1)S(1)} all-gather(bf16[1,160,32]{1,2,0:T(8,128)(2,1)S(1)} %fusion.12), channel_id=1, replica_groups=mesh['row'=16,'col'=32] {'col'}, dimensions={0}, use_global_device_ids=true | all-gather | bytes 337920 | tf_op jit(solution)/shard_map/all_gather | solution.py:38
  114.4 38.5 %all-gather = bf16[16,160,8]{1,2,0:T(8,128)(2,1)S(1)} all-gather(bf16[1,160,8]{1,2,0:T(8,128)(2,1)S(1)} %bitcast.48), channel_id=1, replica_groups=mesh['row'=16,'col'=32] {'row'}, dimensions={0}, use_global_device_ids=true | all-gather | bytes 43520 | tf_op jit(solution)/shard_map/all_gather | solution.py:43
  153.3 0.3 reshape.8
  153.6 0.3 copy.14
  153.9 0.7 reshape.6
  154.8 44.2 %while.14 = (s32[]{:T(128)}, f32[8,5120]{1,0:T(8,128)S(1)}, bf16[8,2560]{1,0:T(8,128)(2,1)S(1)}, f32[5120]{0:T(1024)S(1)}, bf16[32,2560]{1,0:T(8,128)(2,1)S(1)},...) while((s32[]{:T(128)}, f32[8,5120]{1,0:T(8,128)S(1)}, ...), condition=%wide.region_3.4_spmd.clone, body=%wide.region_1.3_spmd.clone.sunk | while | flops 120692488 | bytes 5957809 | solution.py:53
  154.8 3.9 %multiply_convert_fusion.2 = bf16[5120,256]{0,1:T(8,128)(2,1)S(1)} fusion(bf16[32,5120]{1,0:T(8,128)(2,1)S(1)} %get-tuple-element.210, f32[256]{0:T(256)S(1)} %multiply_reduce_fusion.3, f32[5120]{0:T(1024)S(1)} %get-tuple-element.208, bf16[32,2560]{1,0:T(8,128)(2,1)S(1)} %get-tuple-element.209, s32[]{:T(128)S(6)} %select_n.10), kind=kOutput, calls=%fused_computation.7.clone.1 | convolution fusion | flops 99614720 | bytes 2987012 | tf_op jit(solution)/shard_map/while/body/eval_jaxpr/dot_general | solution.py:8
  158.7 0.4 convolution_add_fusion.2
  159.2 3.9 %multiply_convert_fusion.2 = bf16[5120,256]{0,1:T(8,128)(2,1)S(1)} fusion(bf16[32,5120]{1,0:T(8,128)(2,1)S(1)} %get-tuple-element.210, f32[256]{0:T(256)S(1)} %multiply_reduce_fusion.3, f32[5120]{0:T(1024)S(1)} %get-tuple-element.208, bf16[32,2560]{1,0:T(8,128)(2,1)S(1)} %get-tuple-element.209, s32[]{:T(128)S(6)} %select_n.10), kind=kOutput, calls=%fused_computation.7.clone.1 | convolution fusion | flops 99614720 | bytes 2987012 | tf_op jit(solution)/shard_map/while/body/eval_jaxpr/dot_general | solution.py:8
  163.2 0.4 convolution_add_fusion.2
  163.6 3.9 %multiply_convert_fusion.2 = bf16[5120,256]{0,1:T(8,128)(2,1)S(1)} fusion(bf16[32,5120]{1,0:T(8,128)(2,1)S(1)} %get-tuple-element.210, f32[256]{0:T(256)S(1)} %multiply_reduce_fusion.3, f32[5120]{0:T(1024)S(1)} %get-tuple-element.208, bf16[32,2560]{1,0:T(8,128)(2,1)S(1)} %get-tuple-element.209, s32[]{:T(128)S(6)} %select_n.10), kind=kOutput, calls=%fused_computation.7.clone.1 | convolution fusion | flops 99614720 | bytes 2987012 | tf_op jit(solution)/shard_map/while/body/eval_jaxpr/dot_general | solution.py:8
  167.6 0.4 convolution_add_fusion.2
  168.1 3.9 %multiply_convert_fusion.2 = bf16[5120,256]{0,1:T(8,128)(2,1)S(1)} fusion(bf16[32,5120]{1,0:T(8,128)(2,1)S(1)} %get-tuple-element.210, f32[256]{0:T(256)S(1)} %multiply_reduce_fusion.3, f32[5120]{0:T(1024)S(1)} %get-tuple-element.208, bf16[32,2560]{1,0:T(8,128)(2,1)S(1)} %get-tuple-element.209, s32[]{:T(128)S(6)} %select_n.10), kind=kOutput, calls=%fused_computation.7.clone.1 | convolution fusion | flops 99614720 | bytes 2987012 | tf_op jit(solution)/shard_map/while/body/eval_jaxpr/dot_general | solution.py:8
  172.0 0.4 convolution_add_fusion.2
  172.5 3.9 %multiply_convert_fusion.2 = bf16[5120,256]{0,1:T(8,128)(2,1)S(1)} fusion(bf16[32,5120]{1,0:T(8,128)(2,1)S(1)} %get-tuple-element.210, f32[256]{0:T(256)S(1)} %multiply_reduce_fusion.3, f32[5120]{0:T(1024)S(1)} %get-tuple-element.208, bf16[32,2560]{1,0:T(8,128)(2,1)S(1)} %get-tuple-element.209, s32[]{:T(128)S(6)} %select_n.10), kind=kOutput, calls=%fused_computation.7.clone.1 | convolution fusion | flops 99614720 | bytes 2987012 | tf_op jit(solution)/shard_map/while/body/eval_jaxpr/dot_general | solution.py:8
  176.4 0.4 convolution_add_fusion.2
  176.9 3.9 %multiply_convert_fusion.2 = bf16[5120,256]{0,1:T(8,128)(2,1)S(1)} fusion(bf16[32,5120]{1,0:T(8,128)(2,1)S(1)} %get-tuple-element.210, f32[256]{0:T(256)S(1)} %multiply_reduce_fusion.3, f32[5120]{0:T(1024)S(1)} %get-tuple-element.208, bf16[32,2560]{1,0:T(8,128)(2,1)S(1)} %get-tuple-element.209, s32[]{:T(128)S(6)} %select_n.10), kind=kOutput, calls=%fused_computation.7.clone.1 | convolution fusion | flops 99614720 | bytes 2987012 | tf_op jit(solution)/shard_map/while/body/eval_jaxpr/dot_general | solution.py:8
  180.8 0.4 convolution_add_fusion.2
  181.3 3.9 %multiply_convert_fusion.2 = bf16[5120,256]{0,1:T(8,128)(2,1)S(1)} fusion(bf16[32,5120]{1,0:T(8,128)(2,1)S(1)} %get-tuple-element.210, f32[256]{0:T(256)S(1)} %multiply_reduce_fusion.3, f32[5120]{0:T(1024)S(1)} %get-tuple-element.208, bf16[32,2560]{1,0:T(8,128)(2,1)S(1)} %get-tuple-element.209, s32[]{:T(128)S(6)} %select_n.10), kind=kOutput, calls=%fused_computation.7.clone.1 | convolution fusion | flops 99614720 | bytes 2987012 | tf_op jit(solution)/shard_map/while/body/eval_jaxpr/dot_general | solution.py:8
  185.3 0.4 convolution_add_fusion.2
  185.7 3.9 %multiply_convert_fusion.2 = bf16[5120,256]{0,1:T(8,128)(2,1)S(1)} fusion(bf16[32,5120]{1,0:T(8,128)(2,1)S(1)} %get-tuple-element.210, f32[256]{0:T(256)S(1)} %multiply_reduce_fusion.3, f32[5120]{0:T(1024)S(1)} %get-tuple-element.208, bf16[32,2560]{1,0:T(8,128)(2,1)S(1)} %get-tuple-element.209, s32[]{:T(128)S(6)} %select_n.10), kind=kOutput, calls=%fused_computation.7.clone.1 | convolution fusion | flops 99614720 | bytes 2987012 | tf_op jit(solution)/shard_map/while/body/eval_jaxpr/dot_general | solution.py:8
  189.7 0.4 convolution_add_fusion.2
  190.2 3.9 %multiply_convert_fusion.2 = bf16[5120,256]{0,1:T(8,128)(2,1)S(1)} fusion(bf16[32,5120]{1,0:T(8,128)(2,1)S(1)} %get-tuple-element.210, f32[256]{0:T(256)S(1)} %multiply_reduce_fusion.3, f32[5120]{0:T(1024)S(1)} %get-tuple-element.208, bf16[32,2560]{1,0:T(8,128)(2,1)S(1)} %get-tuple-element.209, s32[]{:T(128)S(6)} %select_n.10), kind=kOutput, calls=%fused_computation.7.clone.1 | convolution fusion | flops 99614720 | bytes 2987012 | tf_op jit(solution)/shard_map/while/body/eval_jaxpr/dot_general | solution.py:8
  194.1 0.4 convolution_add_fusion.2
  194.6 3.9 %multiply_convert_fusion.2 = bf16[5120,256]{0,1:T(8,128)(2,1)S(1)} fusion(bf16[32,5120]{1,0:T(8,128)(2,1)S(1)} %get-tuple-element.210, f32[256]{0:T(256)S(1)} %multiply_reduce_fusion.3, f32[5120]{0:T(1024)S(1)} %get-tuple-element.208, bf16[32,2560]{1,0:T(8,128)(2,1)S(1)} %get-tuple-element.209, s32[]{:T(128)S(6)} %select_n.10), kind=kOutput, calls=%fused_computation.7.clone.1 | convolution fusion | flops 99614720 | bytes 2987012 | tf_op jit(solution)/shard_map/while/body/eval_jaxpr/dot_general | solution.py:8
  198.5 0.4 convolution_add_fusion.2
  199.0 2.3 copy.16
  201.2 152.0 %reduce-scatter.4.cloned.1.call-done = f32[160,8]{1,0:T(8,128)} async-done(((f32[5120,8]{1,0:T(8,128)}), f32[160,8]{1,0:T(8,128)}) %reduce-scatter.4.cloned.1.call-update) | async-done | bytes 5136
  353.2 1.6 copy.17
  (26 shorter events, 1.2 us)
Async XLA Ops:
  6.5 1.7 copy-start
  6.5 2.2 copy-start.3
  6.5 2.2 copy-start.2
  6.5 107.9 %copy-start.1 = (bf16[8,160]{1,0:T(8,128)(2,1)S(1)}, bf16[8,160]{1,0:T(8,128)(2,1)}, u32[]{:S(2)}) copy-start(bf16[8,160]{1,0:T(8,128)(2,1)} %param.13) | copy-start | bytes 7684
  6.5 346.7 %reduce-scatter.4.cloned.1.call-start = ((), (), s32[]{:S(2)}) async-start(), calls=%async_computation.1 | async-start | bytes 2703360
Sparse Core Ops, SparseCore 0:
  201.4 151.8 reduce-scatter.3
where the time goes:
time: 365 us; the launch traced here: 362 us
  waiting for transfers between devices  152 us (42%)
  blocking collectives  144 us (39%)
  matrix products  45.8 us (13%)
  between operations  13.5 us (4%)
  local copies, waits for them, and re-layouts  5.77 us (2%)
    unnamed x2, waiting for transfers between devices  152 us
    all_gather x1, blocking collectives, on_device(): piece_feats = lax.all_gather(scaled, 'row', axis=1, tiled=True)  53.4 us
    all_gather x1, blocking collectives, on_device(): row_feats = lax.all_gather(scaled, 'col', axis=1, tiled=True)  52 us
    dot_general x23, matrix products, wide_general(): lax.dot_general(left.astype(jnp.float32), right.astype(jnp.float32), (dim...  45.8 us
    all_gather x1, blocking collectives, on_device(): piece_probes = lax.all_gather(probes, 'row', axis=1, tiled=True)  38.5 us
  transfers between devices with their start and end apart: 1, of which 1 were waited for; matrix products, arithmetic and copies ran while one was open for 0% of the time, Pallas kernels for 0%

commit v1 on v0

v1 whole, which is shorter than its diff:
```python
import jax
import jax.numpy as jnp
from jax import lax
from jax.sharding import PartitionSpec as P


def dot_f32(left, right, dims):
    return lax.dot_general(
        left, right, (dims, ((), ())), preferred_element_type=jnp.float32
    )


def matern_tile(left_feats, left_sq, right_feats):
    cross_term = dot_f32(left_feats, right_feats, ((0,), (0,)))
    right_wide = right_feats.astype(jnp.float32)
    right_sq = jnp.sum(right_wide * right_wide, axis=0)
    dist_sq = jnp.maximum(left_sq[:, None] + right_sq[None, :] - 2.0 * cross_term, 0.0)
    scaled_dist = jnp.sqrt(5.0 * dist_sq)
    values = (1.0 + scaled_dist + scaled_dist * scaled_dist / 3.0) * jnp.exp(-scaled_dist)
    return values.astype(jnp.bfloat16)


def gather_peers(block, axis, peers):
    spread = jnp.broadcast_to(block[None], (peers,) + block.shape)
    arrived = lax.all_to_all(spread, axis, 0, 0, tiled=False)
    rows = block.shape[0]
    return jnp.transpose(arrived, (1, 0, 2)).reshape(rows, peers * block.shape[1])


def on_device(points, w_in, w_mid, w_out, lengthscale, probes):
    hidden_one = jax.nn.relu(dot_f32(points, w_in, ((1,), (0,)))).astype(jnp.bfloat16)
    hidden_two = jax.nn.relu(dot_f32(hidden_one, w_mid, ((1,), (0,)))).astype(jnp.bfloat16)
    features = dot_f32(w_out, hidden_two, ((0,), (1,)))
    scaled = (features / lengthscale[:, None]).astype(jnp.bfloat16)
    col_peers = lax.axis_size("col")
    row_peers = lax.axis_size("row")
    local = scaled.shape[1]
    feat_dim = scaled.shape[0]
    probe_rows = probes.shape[0]
    row_feats = gather_peers(scaled, "col", col_peers)
    row_wide = row_feats.astype(jnp.float32)
    row_sq = jnp.sum(row_wide * row_wide, axis=0)
    joined = jnp.concatenate([scaled, probes], axis=0)
    piece = gather_peers(joined, "row", row_peers)
    piece_feats = piece[:feat_dim]
    piece_probes = piece[feat_dim:]
    block_cols = 256
    initial = jnp.zeros((probe_rows, row_feats.shape[1]), jnp.float32)

    def advance(position, row_acc):
        column_start = position * block_cols
        feats_block = lax.dynamic_slice_in_dim(piece_feats, column_start, block_cols, 1)
        probes_block = lax.dynamic_slice_in_dim(piece_probes, column_start, block_cols, 1)
        kernel_tile = matern_tile(row_feats, row_sq, feats_block)
        return row_acc + dot_f32(probes_block, kernel_tile, ((1,), (1,)))

    folded = lax.fori_loop(0, piece_feats.shape[1] // block_cols, advance, initial)
    parts = jnp.transpose(folded.reshape(probe_rows, col_peers, local), (1, 0, 2))
    arrived = lax.all_to_all(parts, "col", 0, 0, tiled=False)
    return jnp.sum(arrived, axis=0)


def solution(mesh):
    in_specs = (P(("row", "col"), None), P(), P(), P(), P(), P(None, ("row", "col")))
    out_specs = P(None, ("row", "col"))
    return jax.shard_map(
        on_device, mesh=mesh, in_specs=in_specs, out_specs=out_specs, check_vma=False
    )
```

time: 365 us -> 117 us (0.32)
  waiting for transfers between devices: 152 us -> 16.1 us
  blocking collectives: 144 us -> 46.8 us
  between operations: 13.5 us -> 0.15 us
  starting transfers between devices: 0.03 us -> 9.14 us
  matrix products: 45.8 us -> 39.2 us
    unnamed x2 -> x0, waiting for transfers between devices: 152 us -> none
    all_gather x3 -> x0, blocking collectives: 144 us -> none  [the longest x1 53.4 us: on_device(): piece_feats = lax.all_gather(scaled, 'row', axis=1, tiled=True)]
    all_to_all x0 -> x2, blocking collectives: none -> 46.8 us  [the longest x1 32.1 us: gather_peers(): arrived = lax.all_to_all(spread, axis, 0, 0, tiled=False)]
    all_to_all x0 -> x1, waiting for transfers between devices: none -> 16.1 us  [gather_peers(): arrived = lax.all_to_all(spread, axis, 0, 0, tiled=False)]
    all_to_all x0 -> x1, starting transfers between devices: none -> 9.14 us  [gather_peers(): arrived = lax.all_to_all(spread, axis, 0, 0, tiled=False)]
    dot_general x23 -> x12, matrix products: 45.8 us -> 39.2 us  [dot_f32(): lax.dot_general(left, right, (dims, ((), ())), preferred_element_type=jnp...]
    unnamed x13 -> x8, local copies, waits for them, and re-layouts: 5.31 us -> 1.6 us
  transfers between devices with their start and end apart: 1 -> 1, of which waited for: 1 -> 1; matrix products, arithmetic and copies ran while one was open for 0% -> 1% of each run, Pallas kernels for 0% -> 0%
where the time goes in v1:
time: 117 us
  blocking collectives  46.8 us (40%)
  matrix products  39.2 us (34%)
  waiting for transfers between devices  16.1 us (14%)
  starting transfers between devices  9.14 us (8%)
  local copies, waits for them, and re-layouts  4.53 us (4%)
    dot_general x12, matrix products, dot_f32(): lax.dot_general(left, right, (dims, ((), ())), preferred_element_type=jnp...  39.2 us
    all_to_all x1, blocking collectives, gather_peers(): arrived = lax.all_to_all(spread, axis, 0, 0, tiled=False)  32.1 us
    all_to_all x1, waiting for transfers between devices, gather_peers(): arrived = lax.all_to_all(spread, axis, 0, 0, tiled=False)  16.1 us
    all_to_all x1, blocking collectives, on_device(): arrived = lax.all_to_all(parts, 'col', 0, 0, tiled=False)  14.7 us
    all_to_all x1, starting transfers between devices, gather_peers(): arrived = lax.all_to_all(spread, axis, 0, 0, tiled=False)  9.14 us
  transfers between devices with their start and end apart: 1, of which 1 were waited for; matrix products, arithmetic and copies ran while one was open for 1% of the time, Pallas kernels for 0%

profile of v1, /device:TPU:1, one launch (start us, length us, event | category | flops | bytes accessed | tf_op | source)
XLA Modules:
  0.0 117.0 jit_solution(2839393019887244514)
XLA Ops:
  0.0 0.0 copy-start
  0.0 1.6 %copy-done = bf16[1024,1024]{1,0:T(8,128)(2,1)S(1)} copy-done((bf16[1024,1024]{1,0:T(8,128)(2,1)S(1)}, bf16[1024,1024]{1,0:T(8,128)(2,1)}, u32[]{:S(2)}) %copy-start) | copy-done | bytes 2097176
  1.6 1.6 %fusion.16 = bf16[160,1024]{1,0:T(8,128)(2,1)S(1)} fusion(bf16[1024,1024]{1,0:T(8,128)(2,1)S(1)} %copy-done, bf16[160,128]{1,0:T(8,128)(2,1)} %param.8, bf16[128,1024]{1,0:T(8,128)(2,1)} %param.9), kind=kOutput, calls=%fused_computation.20 | convolution fusion | flops 378142720 | bytes 2727936 | tf_op jit(solution)/shard_map/dot_general | solution.py:8
  3.2 0.0 copy-done.3
  3.2 0.2 fusion.18
  3.4 0.0 copy-done.1
  3.5 32.1 %all_to_all.15 = bf16[16,40,160]{2,1,0:T(8,128)(2,1)S(1)} all-to-all(bf16[16,40,160]{2,1,0:T(8,128)(2,1)S(1)} %broadcast_in_dim.11), channel_id=1, replica_groups=mesh['row'=16,'col'=32] {'row'}, dimensions={0} | all-to-all | bytes 409600 | tf_op jit(solution)/shard_map/all_to_all | solution.py:25
  35.6 0.8 broadcast_in_dim.24
  36.4 9.1 %all-to-all-start.1 = ((bf16[32,32,160]{2,1,0:T(8,128)(2,1)}), bf16[32,32,160]{2,1,0:T(8,128)(2,1)S(1)}, u32[]{:S(2)}, u32[]{:S(2)}) async-start(bf16[32,32,160]{2,1,0:T(8,128)(2,1)} %broadcast_in_dim.24), calls=%async_computation.1 | async-start | bytes 1048576 | tf_op jit(solution)/shard_map/all_to_all | solution.py:25
  45.6 0.2 copy.8
  45.8 0.3 slice.15
  46.2 0.1 slice.13
  46.3 16.1 %all-to-all-done.1 = bf16[32,32,160]{2,1,0:T(8,128)(2,1)S(1)} async-done(((bf16[32,32,160]{2,1,0:T(8,128)(2,1)}), bf16[32,32,160]{2,1,0:T(8,128)(2,1)S(1)}, u32[]{:S(2)}, u32[]{:S(2)}) %all-to-all-start.1) | async-done | bytes 327712 | tf_op jit(solution)/shard_map/all_to_all | solution.py:25
  62.4 0.2 multiply_reduce_fusion.1
  62.6 0.1 reduce_sum.34
  62.6 0.3 copy.9
  62.9 0.7 reshape.15
  63.7 37.7 %while.14 = (s32[]{:T(128)}, f32[8,5120]{1,0:T(8,128)S(1)}, bf16[8,2560]{1,0:T(8,128)(2,1)S(1)}, f32[5120]{0:T(1024)S(1)}, bf16[32,2560]{1,0:T(8,128)(2,1)S(1)},...) while((s32[]{:T(128)}, f32[8,5120]{1,0:T(8,128)S(1)}, ...), condition=%wide.region_3.4_spmd.clone, body=%wide.region_1.3_spmd.clone.sunk | while | flops 120692488 | bytes 716456 | solution.py:57
  63.7 3.7 %convolution_add_fusion.2 = f32[8,5120]{1,0:T(8,128)S(1)} fusion(bf16[32,5120]{1,0:T(8,128)(2,1)S(1)} %get-tuple-element.210, f32[256]{0:T(256)S(1)} %multiply_reduce_fusion.3, f32[5120]{0:T(1024)S(1)} %get-tuple-element.208, f32[8,5120]{1,0:T(8,128)S(1)} %get-tuple-element.196, pred[]{:T(512)S(6)} %compare.3, ...), kind=kOutput, calls=%fused_computation.6.clone.1 | convolution fusion | flops 120668160 | bytes 698880 | tf_op jit(solution)/shard_map/while/body/eval_jaxpr/dot_general | solution.py:8
  67.5 3.7 %convolution_add_fusion.2 = f32[8,5120]{1,0:T(8,128)S(1)} fusion(bf16[32,5120]{1,0:T(8,128)(2,1)S(1)} %get-tuple-element.210, f32[256]{0:T(256)S(1)} %multiply_reduce_fusion.3, f32[5120]{0:T(1024)S(1)} %get-tuple-element.208, f32[8,5120]{1,0:T(8,128)S(1)} %get-tuple-element.196, pred[]{:T(512)S(6)} %compare.3, ...), kind=kOutput, calls=%fused_computation.6.clone.1 | convolution fusion | flops 120668160 | bytes 698880 | tf_op jit(solution)/shard_map/while/body/eval_jaxpr/dot_general | solution.py:8
  71.3 3.7 %convolution_add_fusion.2 = f32[8,5120]{1,0:T(8,128)S(1)} fusion(bf16[32,5120]{1,0:T(8,128)(2,1)S(1)} %get-tuple-element.210, f32[256]{0:T(256)S(1)} %multiply_reduce_fusion.3, f32[5120]{0:T(1024)S(1)} %get-tuple-element.208, f32[8,5120]{1,0:T(8,128)S(1)} %get-tuple-element.196, pred[]{:T(512)S(6)} %compare.3, ...), kind=kOutput, calls=%fused_computation.6.clone.1 | convolution fusion | flops 120668160 | bytes 698880 | tf_op jit(solution)/shard_map/while/body/eval_jaxpr/dot_general | solution.py:8
  75.0 3.7 %convolution_add_fusion.2 = f32[8,5120]{1,0:T(8,128)S(1)} fusion(bf16[32,5120]{1,0:T(8,128)(2,1)S(1)} %get-tuple-element.210, f32[256]{0:T(256)S(1)} %multiply_reduce_fusion.3, f32[5120]{0:T(1024)S(1)} %get-tuple-element.208, f32[8,5120]{1,0:T(8,128)S(1)} %get-tuple-element.196, pred[]{:T(512)S(6)} %compare.3, ...), kind=kOutput, calls=%fused_computation.6.clone.1 | convolution fusion | flops 120668160 | bytes 698880 | tf_op jit(solution)/shard_map/while/body/eval_jaxpr/dot_general | solution.py:8
  78.8 3.7 %convolution_add_fusion.2 = f32[8,5120]{1,0:T(8,128)S(1)} fusion(bf16[32,5120]{1,0:T(8,128)(2,1)S(1)} %get-tuple-element.210, f32[256]{0:T(256)S(1)} %multiply_reduce_fusion.3, f32[5120]{0:T(1024)S(1)} %get-tuple-element.208, f32[8,5120]{1,0:T(8,128)S(1)} %get-tuple-element.196, pred[]{:T(512)S(6)} %compare.3, ...), kind=kOutput, calls=%fused_computation.6.clone.1 | convolution fusion | flops 120668160 | bytes 698880 | tf_op jit(solution)/shard_map/while/body/eval_jaxpr/dot_general | solution.py:8
  82.6 3.7 %convolution_add_fusion.2 = f32[8,5120]{1,0:T(8,128)S(1)} fusion(bf16[32,5120]{1,0:T(8,128)(2,1)S(1)} %get-tuple-element.210, f32[256]{0:T(256)S(1)} %multiply_reduce_fusion.3, f32[5120]{0:T(1024)S(1)} %get-tuple-element.208, f32[8,5120]{1,0:T(8,128)S(1)} %get-tuple-element.196, pred[]{:T(512)S(6)} %compare.3, ...), kind=kOutput, calls=%fused_computation.6.clone.1 | convolution fusion | flops 120668160 | bytes 698880 | tf_op jit(solution)/shard_map/while/body/eval_jaxpr/dot_general | solution.py:8
  86.3 3.7 %convolution_add_fusion.2 = f32[8,5120]{1,0:T(8,128)S(1)} fusion(bf16[32,5120]{1,0:T(8,128)(2,1)S(1)} %get-tuple-element.210, f32[256]{0:T(256)S(1)} %multiply_reduce_fusion.3, f32[5120]{0:T(1024)S(1)} %get-tuple-element.208, f32[8,5120]{1,0:T(8,128)S(1)} %get-tuple-element.196, pred[]{:T(512)S(6)} %compare.3, ...), kind=kOutput, calls=%fused_computation.6.clone.1 | convolution fusion | flops 120668160 | bytes 698880 | tf_op jit(solution)/shard_map/while/body/eval_jaxpr/dot_general | solution.py:8
  90.1 3.7 %convolution_add_fusion.2 = f32[8,5120]{1,0:T(8,128)S(1)} fusion(bf16[32,5120]{1,0:T(8,128)(2,1)S(1)} %get-tuple-element.210, f32[256]{0:T(256)S(1)} %multiply_reduce_fusion.3, f32[5120]{0:T(1024)S(1)} %get-tuple-element.208, f32[8,5120]{1,0:T(8,128)S(1)} %get-tuple-element.196, pred[]{:T(512)S(6)} %compare.3, ...), kind=kOutput, calls=%fused_computation.6.clone.1 | convolution fusion | flops 120668160 | bytes 698880 | tf_op jit(solution)/shard_map/while/body/eval_jaxpr/dot_general | solution.py:8
  93.9 3.7 %convolution_add_fusion.2 = f32[8,5120]{1,0:T(8,128)S(1)} fusion(bf16[32,5120]{1,0:T(8,128)(2,1)S(1)} %get-tuple-element.210, f32[256]{0:T(256)S(1)} %multiply_reduce_fusion.3, f32[5120]{0:T(1024)S(1)} %get-tuple-element.208, f32[8,5120]{1,0:T(8,128)S(1)} %get-tuple-element.196, pred[]{:T(512)S(6)} %compare.3, ...), kind=kOutput, calls=%fused_computation.6.clone.1 | convolution fusion | flops 120668160 | bytes 698880 | tf_op jit(solution)/shard_map/while/body/eval_jaxpr/dot_general | solution.py:8
  97.6 3.7 %convolution_add_fusion.2 = f32[8,5120]{1,0:T(8,128)S(1)} fusion(bf16[32,5120]{1,0:T(8,128)(2,1)S(1)} %get-tuple-element.210, f32[256]{0:T(256)S(1)} %multiply_reduce_fusion.3, f32[5120]{0:T(1024)S(1)} %get-tuple-element.208, f32[8,5120]{1,0:T(8,128)S(1)} %get-tuple-element.196, pred[]{:T(512)S(6)} %compare.3, ...), kind=kOutput, calls=%fused_computation.6.clone.1 | convolution fusion | flops 120668160 | bytes 698880 | tf_op jit(solution)/shard_map/while/body/eval_jaxpr/dot_general | solution.py:8
  101.4 0.1 reshape.16
  101.5 0.2 copy.10
  101.7 14.7 %all_to_all.16 = f32[32,8,160]{2,1,0:T(8,128)S(1)} all-to-all(f32[32,8,160]{2,1,0:T(8,128)S(1)} %copy.10), channel_id=1, replica_groups=mesh['row'=16,'col'=32] {'col'}, dimensions={0} | all-to-all | bytes 327680 | tf_op jit(solution)/shard_map/all_to_all | solution.py:59
  116.4 0.6 reduce_sum.35
  (20 shorter events, 0.3 us)
Async XLA Ops:
  0.0 1.6 %copy-start = (bf16[1024,1024]{1,0:T(8,128)(2,1)S(1)}, bf16[1024,1024]{1,0:T(8,128)(2,1)}, u32[]{:S(2)}) copy-start(bf16[1024,1024]{1,0:T(8,128)(2,1)} %param.10) | copy-start | bytes 6291460
  0.0 3.2 %copy-start.3 = (f32[32]{0:T(128)S(1)}, f32[32]{0:T(128)}, u32[]{:S(2)}) copy-start(f32[32]{0:T(128)} %param.12) | copy-start | bytes 388
  0.0 3.2 %copy-start.2 = (bf16[1024,32]{0,1:T(8,128)(2,1)S(1)}, bf16[1024,32]{0,1:T(8,128)(2,1)}, u32[]{:S(2)}) copy-start(bf16[1024,32]{0,1:T(8,128)(2,1)} %param.11) | copy-start | bytes 196612
  1.6 1.8 %copy-start.1 = (bf16[8,160]{1,0:T(8,128)(2,1)S(1)}, bf16[8,160]{1,0:T(8,128)(2,1)}, u32[]{:S(2)}) copy-start(bf16[8,160]{1,0:T(8,128)(2,1)} %param.13) | copy-start | bytes 7684
  36.4 25.9 %all-to-all-start.1 = ((bf16[32,32,160]{2,1,0:T(8,128)(2,1)}), bf16[32,32,160]{2,1,0:T(8,128)(2,1)S(1)}, u32[]{:S(2)}, u32[]{:S(2)}) async-start(bf16[32,32,160]{2,1,0:T(8,128)(2,1)} %broadcast_in_dim.24), calls=%async_computation.1 | async-start | bytes 1048576 | tf_op jit(solution)/shard_map/all_to_all | solution.py:25

commit v2 on v1

--- a/solution.py
+++ b/solution.py
@@ -27,6 +27,17 @@
     return jnp.transpose(arrived, (1, 0, 2)).reshape(rows, peers * block.shape[1])
 
 
+def fold_columns(row_feats, row_sq, feats, probes, acc, block_cols):
+    def advance(position, row_acc):
+        column_start = position * block_cols
+        feats_block = lax.dynamic_slice_in_dim(feats, column_start, block_cols, 1)
+        probes_block = lax.dynamic_slice_in_dim(probes, column_start, block_cols, 1)
+        kernel_tile = matern_tile(row_feats, row_sq, feats_block)
+        return row_acc + dot_f32(probes_block, kernel_tile, ((1,), (1,)))
+
+    return lax.fori_loop(0, feats.shape[1] // block_cols, advance, acc)
+
+
 def on_device(points, w_in, w_mid, w_out, lengthscale, probes):
     hidden_one = jax.nn.relu(dot_f32(points, w_in, ((1,), (0,)))).astype(jnp.bfloat16)
     hidden_two = jax.nn.relu(dot_f32(hidden_one, w_mid, ((1,), (0,)))).astype(jnp.bfloat16)
@@ -37,27 +48,32 @@
     local = scaled.shape[1]
     feat_dim = scaled.shape[0]
     probe_rows = probes.shape[0]
-    row_feats = gather_peers(scaled, "col", col_peers)
+    joined = jnp.concatenate([scaled, probes], axis=0)
+    block = gather_peers(joined, "col", col_peers)
+    row_feats = block[:feat_dim]
     row_wide = row_feats.astype(jnp.float32)
     row_sq = jnp.sum(row_wide * row_wide, axis=0)
-    joined = jnp.concatenate([scaled, probes], axis=0)
-    piece = gather_peers(joined, "row", row_peers)
-    piece_feats = piece[:feat_dim]
-    piece_probes = piece[feat_dim:]
-    block_cols = 256
-    initial = jnp.zeros((probe_rows, row_feats.shape[1]), jnp.float32)
-
-    def advance(position, row_acc):
-        column_start = position * block_cols
-        feats_block = lax.dynamic_slice_in_dim(piece_feats, column_start, block_cols, 1)
-        probes_block = lax.dynamic_slice_in_dim(piece_probes, column_start, block_cols, 1)
-        kernel_tile = matern_tile(row_feats, row_sq, feats_block)
-        return row_acc + dot_f32(probes_block, kernel_tile, ((1,), (1,)))
-
-    folded = lax.fori_loop(0, piece_feats.shape[1] // block_cols, advance, initial)
-    parts = jnp.transpose(folded.reshape(probe_rows, col_peers, local), (1, 0, 2))
-    arrived = lax.all_to_all(parts, "col", 0, 0, tiled=False)
-    return jnp.sum(arrived, axis=0)
+    halves = col_peers // row_peers
+    span = block.shape[1] // halves
+    col = lax.axis_index("col")
+    mine = lax.dynamic_slice_in_dim(block, (col % halves) * span, span, 1)
+    pairs = []
+    for r in range(row_peers):
+        for c in range(col_peers):
+            target = (r - c // halves) % row_peers
+            pairs.append((r * col_peers + c, target * col_peers + c))
+    chunks = 2
+    width = span // chunks
+    arrived = [
+        lax.ppermute(mine[:, k * width:(k + 1) * width], ("row", "col"), pairs)
+        for k in range(chunks)
+    ]
+    acc = jnp.zeros((probe_rows, block.shape[1]), jnp.float32)
+    for piece in arrived:
+        acc = fold_columns(row_feats, row_sq, piece[:feat_dim], piece[feat_dim:], acc, 256)
+    parts = jnp.transpose(acc.reshape(probe_rows, col_peers, local), (1, 0, 2))
+    summed = lax.all_to_all(parts, "col", 0, 0, tiled=False)
+    return jnp.sum(summed, axis=0)
 
 
 def solution(mesh):

time: 117 us -> 113 us (0.966)
  blocking collectives: 46.8 us -> 31.1 us
  local copies, waits for them, and re-layouts: 4.53 us -> 8.7 us
  starting transfers between devices: 9.14 us -> 12.7 us
  waiting for transfers between devices: 16.1 us -> 19.5 us
    all_to_all x2 -> x1, blocking collectives: 46.8 us -> 31.1 us  [on_device(): summed = lax.all_to_all(parts, 'col', 0, 0, tiled=False)]
    all_to_all x1, waiting for transfers between devices: 16.1 us -> 19.5 us  [gather_peers(): arrived = lax.all_to_all(spread, axis, 0, 0, tiled=False)]
    slice x6 -> x8, local copies, waits for them, and re-layouts: 0.65 us -> 3.95 us  [the longest x3 2.93 us: on_device(): row_feats = block[:feat_dim]]
    all_to_all x1, starting transfers between devices: 9.14 us -> 11.4 us  [gather_peers(): arrived = lax.all_to_all(spread, axis, 0, 0, tiled=False)]
    ppermute x0 -> x2, starting transfers between devices: none -> 1.33 us  [on_device(): lax.ppermute(mine[:, k * width:(k + 1) * width], ('row', 'col'), pairs)]
  transfers between devices with their start and end apart: 1 -> 3, of which waited for: 1 -> 1; matrix products, arithmetic and copies ran while one was open for 1% -> 19% of each run, Pallas kernels for 0% -> 0%
where the time goes in v2:
time: 113 us
  matrix products  39.2 us (35%)
  blocking collectives  31.1 us (28%)
  waiting for transfers between devices  19.5 us (17%)
  starting transfers between devices  12.7 us (11%)
  local copies, waits for them, and re-layouts  8.7 us (8%)
    dot_general x12, matrix products, dot_f32(): lax.dot_general(left, right, (dims, ((), ())), preferred_element_type=jnp...  39.2 us
    all_to_all x1, blocking collectives, on_device(): summed = lax.all_to_all(parts, 'col', 0, 0, tiled=False)  31.1 us
    all_to_all x1, waiting for transfers between devices, gather_peers(): arrived = lax.all_to_all(spread, axis, 0, 0, tiled=False)  19.5 us
    all_to_all x1, starting transfers between devices, gather_peers(): arrived = lax.all_to_all(spread, axis, 0, 0, tiled=False)  11.4 us
    slice x3, local copies, waits for them, and re-layouts, on_device(): row_feats = block[:feat_dim]  2.93 us
  transfers between devices with their start and end apart: 3, of which 1 were waited for; matrix products, arithmetic and copies ran while one was open for 19% of the time, Pallas kernels for 0%

profile of v2, /device:TPU:1, one launch (start us, length us, event | category | flops | bytes accessed | tf_op | source)
XLA Modules:
  0.0 112.5 jit_solution(899810420433188477)
XLA Ops:
  0.0 1.6 %copy-done = bf16[1024,1024]{1,0:T(8,128)(2,1)S(1)} copy-done((bf16[1024,1024]{1,0:T(8,128)(2,1)S(1)}, bf16[1024,1024]{1,0:T(8,128)(2,1)}, u32[]{:S(2)}) %copy-start) | copy-done | bytes 2097176
  1.6 1.6 %fusion.31 = bf16[160,1024]{1,0:T(8,128)(2,1)S(1)} fusion(bf16[1024,1024]{1,0:T(8,128)(2,1)S(1)} %copy-done, bf16[160,128]{1,0:T(8,128)(2,1)} %param.10, bf16[128,1024]{1,0:T(8,128)(2,1)} %param.11), kind=kOutput, calls=%fused_computation.37 | convolution fusion | flops 378142720 | bytes 2727936 | tf_op jit(solution)/shard_map/dot_general | solution.py:8
  3.2 0.2 fusion.33
  3.5 0.9 broadcast_in_dim.23
  4.4 11.4 %all-to-all-start = ((bf16[32,40,160]{2,1,0:T(8,128)(2,1)}), bf16[32,40,160]{2,1,0:T(8,128)(2,1)S(1)}, u32[]{:S(2)}, u32[]{:S(2)}) async-start(bf16[32,40,160]{2,1,0:T(8,128)(2,1)} %broadcast_in_dim.23), calls=%async_computation | async-start | bytes 1310720 | tf_op jit(solution)/shard_map/all_to_all | solution.py:25
  15.8 19.5 %all-to-all-done = bf16[32,40,160]{2,1,0:T(8,128)(2,1)S(1)} async-done(((bf16[32,40,160]{2,1,0:T(8,128)(2,1)}), bf16[32,40,160]{2,1,0:T(8,128)(2,1)S(1)}, u32[]{:S(2)}, u32[]{:S(2)}) %all-to-all-start) | async-done | bytes 409632 | tf_op jit(solution)/shard_map/all_to_all | solution.py:25
  35.3 0.1 copy.7
  35.4 0.8 slice.33
  36.3 1.7 %reshape.14 = bf16[40,5120]{1,0:T(8,128)(2,1)} reshape(bf16[40,32,160]{2,1,0:T(8,128)(2,1)S(1)} %copy.7) | data formatting | bytes 819200 | tf_op jit(solution)/shard_map/reshape | solution.py:27
  38.0 1.0 constant_dynamic-slice_fusion.1
  39.0 0.7 collective-permute-start
  39.7 0.2 multiply_reduce_fusion.2
  39.9 0.1 reduce_sum.47
  40.0 1.3 %copy.8 = bf16[32,32,160]{2,1,0:T(8,128)(2,1)S(1)} copy(bf16[32,32,160]{2,0,1:T(8,128)(2,1)} %slice.33) | data formatting | bytes 655360 | tf_op jit(solution)/shard_map/slice | solution.py:53
  41.3 0.7 slice.28
  42.1 0.7 collective-permute-start.1
  42.8 18.9 %while.28 = (s32[]{:T(128)}, f32[8,5120]{1,0:T(8,128)S(1)}, bf16[8,1280]{1,0:T(8,128)(2,1)S(1)}, f32[5120]{0:T(1024)S(1)}, bf16[32,1280]{1,0:T(8,128)(2,1)S(1)},...) while((s32[]{:T(128)}, f32[8,5120]{1,0:T(8,128)S(1)}, ...), condition=%wide.region_3.4_spmd.clone, body=%wide.region_1.3_spmd.clone.sunk | while | flops 120692488 | bytes 716456 | solution.py:38
  42.8 3.7 %convolution_add_fusion.5 = f32[8,5120]{1,0:T(8,128)S(1)} fusion(bf16[32,5120]{1,0:T(8,128)(2,1)S(1)} %get-tuple-element.371, f32[256]{0:T(256)S(1)} %multiply_reduce_fusion.6, f32[5120]{0:T(1024)S(1)} %get-tuple-element.369, f32[8,5120]{1,0:T(8,128)S(1)} %get-tuple-element.357, pred[]{:T(512)S(6)} %compare.4, ...), kind=kOutput, calls=%fused_computation.23.clone.1 | convolution fusion | flops 120668160 | bytes 698880 | tf_op jit(solution)/shard_map/while/body/eval_jaxpr/dot_general | solution.py:8
  46.6 3.7 %convolution_add_fusion.5 = f32[8,5120]{1,0:T(8,128)S(1)} fusion(bf16[32,5120]{1,0:T(8,128)(2,1)S(1)} %get-tuple-element.371, f32[256]{0:T(256)S(1)} %multiply_reduce_fusion.6, f32[5120]{0:T(1024)S(1)} %get-tuple-element.369, f32[8,5120]{1,0:T(8,128)S(1)} %get-tuple-element.357, pred[]{:T(512)S(6)} %compare.4, ...), kind=kOutput, calls=%fused_computation.23.clone.1 | convolution fusion | flops 120668160 | bytes 698880 | tf_op jit(solution)/shard_map/while/body/eval_jaxpr/dot_general | solution.py:8
  50.4 3.7 %convolution_add_fusion.5 = f32[8,5120]{1,0:T(8,128)S(1)} fusion(bf16[32,5120]{1,0:T(8,128)(2,1)S(1)} %get-tuple-element.371, f32[256]{0:T(256)S(1)} %multiply_reduce_fusion.6, f32[5120]{0:T(1024)S(1)} %get-tuple-element.369, f32[8,5120]{1,0:T(8,128)S(1)} %get-tuple-element.357, pred[]{:T(512)S(6)} %compare.4, ...), kind=kOutput, calls=%fused_computation.23.clone.1 | convolution fusion | flops 120668160 | bytes 698880 | tf_op jit(solution)/shard_map/while/body/eval_jaxpr/dot_general | solution.py:8
  54.1 3.7 %convolution_add_fusion.5 = f32[8,5120]{1,0:T(8,128)S(1)} fusion(bf16[32,5120]{1,0:T(8,128)(2,1)S(1)} %get-tuple-element.371, f32[256]{0:T(256)S(1)} %multiply_reduce_fusion.6, f32[5120]{0:T(1024)S(1)} %get-tuple-element.369, f32[8,5120]{1,0:T(8,128)S(1)} %get-tuple-element.357, pred[]{:T(512)S(6)} %compare.4, ...), kind=kOutput, calls=%fused_computation.23.clone.1 | convolution fusion | flops 120668160 | bytes 698880 | tf_op jit(solution)/shard_map/while/body/eval_jaxpr/dot_general | solution.py:8
  57.9 3.7 %convolution_add_fusion.5 = f32[8,5120]{1,0:T(8,128)S(1)} fusion(bf16[32,5120]{1,0:T(8,128)(2,1)S(1)} %get-tuple-element.371, f32[256]{0:T(256)S(1)} %multiply_reduce_fusion.6, f32[5120]{0:T(1024)S(1)} %get-tuple-element.369, f32[8,5120]{1,0:T(8,128)S(1)} %get-tuple-element.357, pred[]{:T(512)S(6)} %compare.4, ...), kind=kOutput, calls=%fused_computation.23.clone.1 | convolution fusion | flops 120668160 | bytes 698880 | tf_op jit(solution)/shard_map/while/body/eval_jaxpr/dot_general | solution.py:8
  61.7 18.8 %while.27 = (s32[]{:T(128)}, f32[8,5120]{1,0:T(8,128)S(1)}, bf16[8,1280]{1,0:T(8,128)(2,1)S(1)}, f32[5120]{0:T(1024)S(1)}, bf16[32,1280]{1,0:T(8,128)(2,1)S(1)},...) while((s32[]{:T(128)}, f32[8,5120]{1,0:T(8,128)S(1)}, ...), condition=%wide.region_6.7_spmd, body=%wide.region_4.6_spmd.sunk | while | flops 120651528 | bytes 715935 | solution.py:38
  61.7 3.7 %convolution_add_fusion.4 = f32[8,5120]{1,0:T(8,128)S(1)} fusion(f32[8,5120]{1,0:T(8,128)S(1)} %get-tuple-element.387, bf16[32,5120]{1,0:T(8,128)(2,1)S(1)} %get-tuple-element.401, f32[256]{0:T(256)S(1)} %multiply_reduce_fusion.5, f32[5120]{0:T(1024)S(1)} %get-tuple-element.399, bf16[32,1280]{1,0:T(8,128)(2,1)S(1)} %get-tuple-element.400, ...), kind=kOutput, calls=%fused_computation.6.clone.1 | convolution fusion | flops 120627200 | bytes 698368 | tf_op jit(solution)/shard_map/while/body/eval_jaxpr/dot_general | solution.py:8
  65.5 3.7 %convolution_add_fusion.4 = f32[8,5120]{1,0:T(8,128)S(1)} fusion(f32[8,5120]{1,0:T(8,128)S(1)} %get-tuple-element.387, bf16[32,5120]{1,0:T(8,128)(2,1)S(1)} %get-tuple-element.401, f32[256]{0:T(256)S(1)} %multiply_reduce_fusion.5, f32[5120]{0:T(1024)S(1)} %get-tuple-element.399, bf16[32,1280]{1,0:T(8,128)(2,1)S(1)} %get-tuple-element.400, ...), kind=kOutput, calls=%fused_computation.6.clone.1 | convolution fusion | flops 120627200 | bytes 698368 | tf_op jit(solution)/shard_map/while/body/eval_jaxpr/dot_general | solution.py:8
  69.3 3.7 %convolution_add_fusion.4 = f32[8,5120]{1,0:T(8,128)S(1)} fusion(f32[8,5120]{1,0:T(8,128)S(1)} %get-tuple-element.387, bf16[32,5120]{1,0:T(8,128)(2,1)S(1)} %get-tuple-element.401, f32[256]{0:T(256)S(1)} %multiply_reduce_fusion.5, f32[5120]{0:T(1024)S(1)} %get-tuple-element.399, bf16[32,1280]{1,0:T(8,128)(2,1)S(1)} %get-tuple-element.400, ...), kind=kOutput, calls=%fused_computation.6.clone.1 | convolution fusion | flops 120627200 | bytes 698368 | tf_op jit(solution)/shard_map/while/body/eval_jaxpr/dot_general | solution.py:8
  73.0 3.7 %convolution_add_fusion.4 = f32[8,5120]{1,0:T(8,128)S(1)} fusion(f32[8,5120]{1,0:T(8,128)S(1)} %get-tuple-element.387, bf16[32,5120]{1,0:T(8,128)(2,1)S(1)} %get-tuple-element.401, f32[256]{0:T(256)S(1)} %multiply_reduce_fusion.5, f32[5120]{0:T(1024)S(1)} %get-tuple-element.399, bf16[32,1280]{1,0:T(8,128)(2,1)S(1)} %get-tuple-element.400, ...), kind=kOutput, calls=%fused_computation.6.clone.1 | convolution fusion | flops 120627200 | bytes 698368 | tf_op jit(solution)/shard_map/while/body/eval_jaxpr/dot_general | solution.py:8
  76.8 3.7 %convolution_add_fusion.4 = f32[8,5120]{1,0:T(8,128)S(1)} fusion(f32[8,5120]{1,0:T(8,128)S(1)} %get-tuple-element.387, bf16[32,5120]{1,0:T(8,128)(2,1)S(1)} %get-tuple-element.401, f32[256]{0:T(256)S(1)} %multiply_reduce_fusion.5, f32[5120]{0:T(1024)S(1)} %get-tuple-element.399, bf16[32,1280]{1,0:T(8,128)(2,1)S(1)} %get-tuple-element.400, ...), kind=kOutput, calls=%fused_computation.6.clone.1 | convolution fusion | flops 120627200 | bytes 698368 | tf_op jit(solution)/shard_map/while/body/eval_jaxpr/dot_general | solution.py:8
  80.5 0.1 reshape.15
  80.7 0.2 copy.9
  80.8 31.1 %all_to_all.10 = f32[32,8,160]{2,1,0:T(8,128)S(1)} all-to-all(f32[32,8,160]{2,1,0:T(8,128)S(1)} %copy.9), channel_id=1, replica_groups=mesh['row'=16,'col'=32] {'col'}, dimensions={0} | all-to-all | bytes 327680 | tf_op jit(solution)/shard_map/all_to_all | solution.py:75
  111.9 0.6 reduce_sum.48
  (27 shorter events, 0.3 us)
Async XLA Ops:
  0.0 1.6 %copy-start = (bf16[1024,1024]{1,0:T(8,128)(2,1)S(1)}, bf16[1024,1024]{1,0:T(8,128)(2,1)}, u32[]{:S(2)}) copy-start(bf16[1024,1024]{1,0:T(8,128)(2,1)} %param.12) | copy-start | bytes 6291460
  0.0 3.2 %copy-start.3 = (bf16[1024,32]{0,1:T(8,128)(2,1)S(1)}, bf16[1024,32]{0,1:T(8,128)(2,1)}, u32[]{:S(2)}) copy-start(bf16[1024,32]{0,1:T(8,128)(2,1)} %param.13) | copy-start | bytes 196612
  0.0 3.2 %copy-start.4 = (f32[32]{0:T(128)S(1)}, f32[32]{0:T(128)}, u32[]{:S(2)}) copy-start(f32[32]{0:T(128)} %param.14) | copy-start | bytes 388
  1.6 1.8 %copy-start.2 = (bf16[8,160]{1,0:T(8,128)(2,1)S(1)}, bf16[8,160]{1,0:T(8,128)(2,1)}, u32[]{:S(2)}) copy-start(bf16[8,160]{1,0:T(8,128)(2,1)} %param.15) | copy-start | bytes 7684
  4.4 30.9 %all-to-all-start = ((bf16[32,40,160]{2,1,0:T(8,128)(2,1)}), bf16[32,40,160]{2,1,0:T(8,128)(2,1)S(1)}, u32[]{:S(2)}, u32[]{:S(2)}) async-start(bf16[32,40,160]{2,1,0:T(8,128)(2,1)} %broadcast_in_dim.23), calls=%async_computation | async-start | bytes 1310720 | tf_op jit(solution)/shard_map/all_to_all | solution.py:25
  38.0 4.7 %copy-start.1 = (f32[8,5120]{1,0:T(8,128)S(1)}, f32[8,5120]{1,0:T(8,128)}, u32[]{:S(2)}) copy-start(f32[8,5120]{1,0:T(8,128)} %custom-call) | copy-start | bytes 491524
  39.0 3.7 %collective-permute-start = (bf16[40,1280]{1,0:T(8,128)(2,1)S(1)}, bf16[40,1280]{1,0:T(8,128)(2,1)S(1)}, u32[]{:S(2)}, u32[]{:S(2)}) collective-permute-start(bf16[40,1280]{1,0:T(8,128)(2,1)S(1)} %get-tuple-element.271), channel_id=1, source_target_pairs={{0,0},{1,1},{2,482},{3,483},{4,452},{5,453},{6,422},{7,423},{8,392... | collective-permute-start | bytes 307208 | tf_op jit(solution)/shard_map/ppermute | solution.py:68
  42.1 19.6 %collective-permute-start.1 = (bf16[40,1280]{1,0:T(8,128)(2,1)S(1)}, bf16[40,1280]{1,0:T(8,128)(2,1)S(1)}, u32[]{:S(2)}, u32[]{:S(2)}) collective-permute-start(bf16[40,1280]{1,0:T(8,128)(2,1)S(1)} %get-tuple-element.270), channel_id=1, source_target_pairs={{0,0},{1,1},{2,482},{3,483},{4,452},{5,453},{6,422},{7,423},{8,392... | collective-permute-start | bytes 307208 | tf_op jit(solution)/shard_map/ppermute | solution.py:68

commit v3 on v2

--- a/solution.py
+++ b/solution.py
@@ -10,13 +10,35 @@
     )
 
 
-def matern_tile(left_feats, left_sq, right_feats):
-    cross_term = dot_f32(left_feats, right_feats, ((0,), (0,)))
-    right_wide = right_feats.astype(jnp.float32)
-    right_sq = jnp.sum(right_wide * right_wide, axis=0)
-    dist_sq = jnp.maximum(left_sq[:, None] + right_sq[None, :] - 2.0 * cross_term, 0.0)
-    scaled_dist = jnp.sqrt(5.0 * dist_sq)
-    values = (1.0 + scaled_dist + scaled_dist * scaled_dist / 3.0) * jnp.exp(-scaled_dist)
+def split_three(value):
+    high = value.astype(jnp.bfloat16)
+    rest = value - high.astype(jnp.float32)
+    middle = rest.astype(jnp.bfloat16)
+    low = (rest - middle.astype(jnp.float32)).astype(jnp.bfloat16)
+    return [high, middle, low]
+
+
+def row_side(feats):
+    wide = feats.astype(jnp.float32)
+    five_sq = 5.0 * jnp.sum(wide * wide, axis=0)
+    ones = jnp.ones((3, feats.shape[1]), jnp.bfloat16)
+    return jnp.concatenate([jnp.stack(split_three(five_sq)), ones, feats, feats], axis=0)
+
+
+def column_side(feats):
+    wide = feats.astype(jnp.float32)
+    five_sq = 5.0 * jnp.sum(wide * wide, axis=0)
+    ones = jnp.ones((3, feats.shape[1]), jnp.bfloat16)
+    scaled = -10.0 * wide
+    high = scaled.astype(jnp.bfloat16)
+    low = (scaled - high.astype(jnp.float32)).astype(jnp.bfloat16)
+    return jnp.concatenate([ones, jnp.stack(split_three(five_sq)), high, low], axis=0)
+
+
+def matern_tile(left_side, right_side):
+    five_dist = jnp.maximum(dot_f32(left_side, right_side, ((0,), (0,))), 0.0)
+    scaled_dist = jnp.sqrt(five_dist)
+    values = (1.0 + scaled_dist + five_dist * (1.0 / 3.0)) * jnp.exp(-scaled_dist)
     return values.astype(jnp.bfloat16)
 
 
@@ -27,15 +49,15 @@
     return jnp.transpose(arrived, (1, 0, 2)).reshape(rows, peers * block.shape[1])
 
 
-def fold_columns(row_feats, row_sq, feats, probes, acc, block_cols):
+def fold_columns(left_side, right_side, probes, acc, block_cols):
     def advance(position, row_acc):
         column_start = position * block_cols
-        feats_block = lax.dynamic_slice_in_dim(feats, column_start, block_cols, 1)
+        side_block = lax.dynamic_slice_in_dim(right_side, column_start, block_cols, 1)
         probes_block = lax.dynamic_slice_in_dim(probes, column_start, block_cols, 1)
-        kernel_tile = matern_tile(row_feats, row_sq, feats_block)
+        kernel_tile = matern_tile(left_side, side_block)
         return row_acc + dot_f32(probes_block, kernel_tile, ((1,), (1,)))
 
-    return lax.fori_loop(0, feats.shape[1] // block_cols, advance, acc)
+    return lax.fori_loop(0, right_side.shape[1] // block_cols, advance, acc)
 
 
 def on_device(points, w_in, w_mid, w_out, lengthscale, probes):
@@ -50,9 +72,7 @@
     probe_rows = probes.shape[0]
     joined = jnp.concatenate([scaled, probes], axis=0)
     block = gather_peers(joined, "col", col_peers)
-    row_feats = block[:feat_dim]
-    row_wide = row_feats.astype(jnp.float32)
-    row_sq = jnp.sum(row_wide * row_wide, axis=0)
+    left_side = row_side(block[:feat_dim])
     halves = col_peers // row_peers
     span = block.shape[1] // halves
     col = lax.axis_index("col")
@@ -70,7 +90,8 @@
     ]
     acc = jnp.zeros((probe_rows, block.shape[1]), jnp.float32)
     for piece in arrived:
-        acc = fold_columns(row_feats, row_sq, piece[:feat_dim], piece[feat_dim:], acc, 256)
+        right_side = column_side(piece[:feat_dim])
+        acc = fold_columns(left_side, right_side, piece[feat_dim:], acc, 256)
     parts = jnp.transpose(acc.reshape(probe_rows, col_peers, local), (1, 0, 2))
     summed = lax.all_to_all(parts, "col", 0, 0, tiled=False)
     return jnp.sum(summed, axis=0)

time: 113 us -> 120 us (1.062); the launches traced: 113 us -> 118 us
  matrix products: 39.2 us -> 32.1 us
  local copies, waits for them, and re-layouts: 8.7 us -> 15.7 us
  starting transfers between devices: 12.7 us -> 15 us
  blocking collectives: 31.1 us -> 33.1 us
    dot_general x12, matrix products: 39.2 us -> 32.1 us  [dot_f32(): lax.dot_general(left, right, (dims, ((), ())), preferred_element_type=jnp...]
    concatenate x0 -> x3, local copies, waits for them, and re-layouts: none -> 6.21 us  [the longest x1 4.62 us: row_side(): jnp.concatenate([jnp.stack(split_three(five_sq)), ones, feats, feats], ax...]
    ppermute x2, starting transfers between devices: 1.33 us -> 3.66 us  [on_device(): lax.ppermute(mine[:, k * width:(k + 1) * width], ('row', 'col'), pairs)]
    all_to_all x1, blocking collectives: 31.1 us -> 33.1 us  [on_device(): summed = lax.all_to_all(parts, 'col', 0, 0, tiled=False)]
    mul x0 -> x3, local copies, waits for them, and re-layouts: none -> 1.3 us  [the longest x2 1.2 us: column_side(): five_sq = 5.0 * jnp.sum(wide * wide, axis=0)]
    slice x7 -> x6, local copies, waits for them, and re-layouts: 2.95 us -> 1.83 us  [the longest x3 1.1 us: on_device(): left_side = row_side(block[:feat_dim])]
  transfers between devices with their start and end apart: 3 -> 3, of which waited for: 1 -> 1; matrix products, arithmetic and copies ran while one was open for 19% -> 6% of each run, Pallas kernels for 0% -> 0%
where the time goes in v3:
time: 120 us; the launch traced here: 118 us
  blocking collectives  33.1 us (28%)
  matrix products  32.1 us (27%)
  waiting for transfers between devices  19.5 us (16%)
  local copies, waits for them, and re-layouts  15.7 us (13%)
  starting transfers between devices  15 us (12%)
  other arithmetic  1.87 us (2%)
    all_to_all x1, blocking collectives, on_device(): summed = lax.all_to_all(parts, 'col', 0, 0, tiled=False)  33.1 us
    dot_general x12, matrix products, dot_f32(): lax.dot_general(left, right, (dims, ((), ())), preferred_element_type=jnp...  32.1 us
    all_to_all x1, waiting for transfers between devices, gather_peers(): arrived = lax.all_to_all(spread, axis, 0, 0, tiled=False)  19.5 us
    all_to_all x1, starting transfers between devices, gather_peers(): arrived = lax.all_to_all(spread, axis, 0, 0, tiled=False)  11.4 us
    concatenate x1, local copies, waits for them, and re-layouts, row_side(): jnp.concatenate([jnp.stack(split_three(five_sq)), ones, feats, feats], ax...  4.62 us
    ppermute x2, starting transfers between devices, on_device(): lax.ppermute(mine[:, k * width:(k + 1) * width], ('row', 'col'), pairs)  3.66 us
  transfers between devices with their start and end apart: 3, of which 1 were waited for; matrix products, arithmetic and copies ran while one was open for 6% of the time, Pallas kernels for 0%

profile of v3, /device:TPU:1, one launch (start us, length us, event | category | flops | bytes accessed | tf_op | source)
XLA Modules:
  0.0 117.6 jit_solution(3199435070466765985)
XLA Ops:
  0.0 1.6 %copy-done = bf16[1024,1024]{1,0:T(8,128)(2,1)S(1)} copy-done((bf16[1024,1024]{1,0:T(8,128)(2,1)S(1)}, bf16[1024,1024]{1,0:T(8,128)(2,1)}, u32[]{:S(2)}) %copy-start) | copy-done | bytes 2097176
  1.6 1.6 %fusion.17 = bf16[160,1024]{1,0:T(8,128)(2,1)S(1)} fusion(bf16[1024,1024]{1,0:T(8,128)(2,1)S(1)} %copy-done, bf16[160,128]{1,0:T(8,128)(2,1)} %param.10, bf16[128,1024]{1,0:T(8,128)(2,1)} %param.11), kind=kOutput, calls=%fused_computation.21 | convolution fusion | flops 378142720 | bytes 2727936 | tf_op jit(solution)/shard_map/dot_general | solution.py:8
  3.5 0.9 broadcast_in_dim.14
  4.3 11.4 %all-to-all-start = ((bf16[32,40,160]{2,1,0:T(8,128)(2,1)}), bf16[32,40,160]{2,1,0:T(8,128)(2,1)S(1)}, u32[]{:S(2)}, u32[]{:S(2)}) async-start(bf16[32,40,160]{2,1,0:T(8,128)(2,1)} %broadcast_in_dim.14), calls=%async_computation | async-start | bytes 1310720 | tf_op jit(solution)/shard_map/all_to_all | solution.py:47
  15.8 19.5 %all-to-all-done = bf16[32,40,160]{2,1,0:T(8,128)(2,1)S(1)} async-done(((bf16[32,40,160]{2,1,0:T(8,128)(2,1)}), bf16[32,40,160]{2,1,0:T(8,128)(2,1)S(1)}, u32[]{:S(2)}, u32[]{:S(2)}) %all-to-all-start) | async-done | bytes 409632 | tf_op jit(solution)/shard_map/all_to_all | solution.py:47
  35.6 1.7 %reshape.130 = bf16[40,5120]{1,0:T(8,128)(2,1)} reshape(bf16[40,32,160]{2,1,0:T(8,128)(2,1)S(1)} %copy.7) | data formatting | bytes 819200 | tf_op jit(solution)/shard_map/reshape | solution.py:49
  37.3 1.6 %constant_dynamic-slice_fusion.1 = (bf16[40,1280]{1,0:T(8,128)(2,1)}, bf16[40,1280]{1,0:T(8,128)(2,1)}) fusion(bf16[40,5120]{1,0:T(8,128)(2,1)} %reshape.130, s32[]{:T(128)S(6)} %add.112, s32[]{:T(128)S(6)} %select_n.27), kind=kLoop, calls=%fused_computation.53 | loop fusion | bytes 409608 | tf_op jit(solution)/shard_map/slice | solution.py:88
  39.0 1.5 %collective-permute-start.1 = (bf16[40,1280]{1,0:T(8,128)(2,1)}, bf16[40,1280]{1,0:T(8,128)(2,1)S(1)}, u32[]{:S(2)}, u32[]{:S(2)}) collective-permute-start(bf16[40,1280]{1,0:T(8,128)(2,1)} %get-tuple-element.233), channel_id=1, source_target_pairs={{0,0},{1,1},{2,482},{3,483},{4,452},{5,453},{6,422},{7,423},{8,392... | collective-permute-start | bytes 307208 | tf_op jit(solution)/shard_map/ppermute | solution.py:88
  40.5 2.1 %collective-permute-start = (bf16[40,1280]{1,0:T(8,128)(2,1)}, bf16[40,1280]{1,0:T(8,128)(2,1)}, u32[]{:S(2)}, u32[]{:S(2)}) collective-permute-start(bf16[40,1280]{1,0:T(8,128)(2,1)} %get-tuple-element.234), channel_id=1, source_target_pairs={{0,0},{1,1},{2,482},{3,483},{4,452},{5,453},{6,422},{7,423},{8,392... | collective-permute-start | bytes 307208 | tf_op jit(solution)/shard_map/ppermute | solution.py:88
  42.9 0.3 copy.8
  43.2 0.7 slice.28
  43.9 4.6 %concatenate.14 = bf16[70,5120]{1,0:T(8,128)(2,1)S(1)} concatenate(bf16[1,5120]{1,0:T(2,128)(2,1)S(1)} %get-tuple-element.243, bf16[1,5120]{1,0:T(2,128)(2,1)S(1)} %get-tuple-element.242, bf16[1,5120]{1,0:T(2,128)(2,1)S(1)} %get-tuple-element.241, bf16[3,5120]{1,0:T(4,128)(2,1)S(1)} %broadcast_in_dim.15, bf16[32,5120]{1,0:T(8,128)(2,1)S(1)} %slice.28, bf16[32,5120]{1,0:T(8,128)(2,1)S(1)} %slice.28), dimensions={0} | concatenate | bytes 1433600 | tf_op jit(solution)/shard_map/concatenate | solution.py:25
  48.7 0.6 mul.208
  49.3 0.9 fusion.26
  50.2 0.6 mul.209
  50.8 1.1 concatenate.13
  52.0 0.7 slice.32
  52.7 15.2 %while.28 = (s32[]{:T(128)}, f32[8,5120]{1,0:T(8,128)S(1)}, bf16[8,1280]{1,0:T(8,128)(2,1)S(1)}, bf16[70,1280]{1,0:T(8,128)(2,1)S(1)}, bf16[70,5120]{1,0:T(8,128...) while((s32[]{:T(128)}, f32[8,5120]{1,0:T(8,128)S(1)}, ...), condition=%wide.region_3.4_spmd.clone, body=%wide.region_2.3_spmd.clone.sunk | while | flops 213729280 | bytes 1107604 | solution.py:60
  52.8 3.0 %convolution_add_fusion.5 = f32[8,5120]{1,0:T(8,128)S(1)} fusion(bf16[70,5120]{1,0:T(8,128)(2,1)S(1)} %get-tuple-element.332, f32[8,5120]{1,0:T(8,128)S(1)} %get-tuple-element.320, pred[]{:T(512)S(6)} %compare.4, bf16[70,1280]{1,0:T(8,128)(2,1)S(1)} %get-tuple-element.331, s32[]{:T(128)S(6)} %select_n.32, bf16[8,1280]{1,0:T(8,128)(2,1)S(1)} %get-tuple-element.330), kind=kOutput, calls=%fused_computation.10.clone.1 | convolution fusion | flops 213729280 | bytes 1107456 | tf_op jit(solution)/shard_map/while/body/eval_jaxpr/dot_general | solution.py:8
  55.8 3.0 %convolution_add_fusion.5 = f32[8,5120]{1,0:T(8,128)S(1)} fusion(bf16[70,5120]{1,0:T(8,128)(2,1)S(1)} %get-tuple-element.332, f32[8,5120]{1,0:T(8,128)S(1)} %get-tuple-element.320, pred[]{:T(512)S(6)} %compare.4, bf16[70,1280]{1,0:T(8,128)(2,1)S(1)} %get-tuple-element.331, s32[]{:T(128)S(6)} %select_n.32, bf16[8,1280]{1,0:T(8,128)(2,1)S(1)} %get-tuple-element.330), kind=kOutput, calls=%fused_computation.10.clone.1 | convolution fusion | flops 213729280 | bytes 1107456 | tf_op jit(solution)/shard_map/while/body/eval_jaxpr/dot_general | solution.py:8
  58.8 3.0 %convolution_add_fusion.5 = f32[8,5120]{1,0:T(8,128)S(1)} fusion(bf16[70,5120]{1,0:T(8,128)(2,1)S(1)} %get-tuple-element.332, f32[8,5120]{1,0:T(8,128)S(1)} %get-tuple-element.320, pred[]{:T(512)S(6)} %compare.4, bf16[70,1280]{1,0:T(8,128)(2,1)S(1)} %get-tuple-element.331, s32[]{:T(128)S(6)} %select_n.32, bf16[8,1280]{1,0:T(8,128)(2,1)S(1)} %get-tuple-element.330), kind=kOutput, calls=%fused_computation.10.clone.1 | convolution fusion | flops 213729280 | bytes 1107456 | tf_op jit(solution)/shard_map/while/body/eval_jaxpr/dot_general | solution.py:8
  61.9 3.0 %convolution_add_fusion.5 = f32[8,5120]{1,0:T(8,128)S(1)} fusion(bf16[70,5120]{1,0:T(8,128)(2,1)S(1)} %get-tuple-element.332, f32[8,5120]{1,0:T(8,128)S(1)} %get-tuple-element.320, pred[]{:T(512)S(6)} %compare.4, bf16[70,1280]{1,0:T(8,128)(2,1)S(1)} %get-tuple-element.331, s32[]{:T(128)S(6)} %select_n.32, bf16[8,1280]{1,0:T(8,128)(2,1)S(1)} %get-tuple-element.330), kind=kOutput, calls=%fused_computation.10.clone.1 | convolution fusion | flops 213729280 | bytes 1107456 | tf_op jit(solution)/shard_map/while/body/eval_jaxpr/dot_general | solution.py:8
  64.9 3.0 %convolution_add_fusion.5 = f32[8,5120]{1,0:T(8,128)S(1)} fusion(bf16[70,5120]{1,0:T(8,128)(2,1)S(1)} %get-tuple-element.332, f32[8,5120]{1,0:T(8,128)S(1)} %get-tuple-element.320, pred[]{:T(512)S(6)} %compare.4, bf16[70,1280]{1,0:T(8,128)(2,1)S(1)} %get-tuple-element.331, s32[]{:T(128)S(6)} %select_n.32, bf16[8,1280]{1,0:T(8,128)(2,1)S(1)} %get-tuple-element.330), kind=kOutput, calls=%fused_computation.10.clone.1 | convolution fusion | flops 213729280 | bytes 1107456 | tf_op jit(solution)/shard_map/while/body/eval_jaxpr/dot_general | solution.py:8
  67.9 0.5 concatenate.15
  68.4 15.2 %while.27 = (s32[]{:T(128)}, f32[8,5120]{1,0:T(8,128)S(1)}, bf16[8,1280]{1,0:T(8,128)(2,1)S(1)}, bf16[70,1280]{1,0:T(8,128)(2,1)S(1)}, bf16[70,5120]{1,0:T(8,128...) while((s32[]{:T(128)}, f32[8,5120]{1,0:T(8,128)S(1)}, bf16[8,1280]{1,0:T(8,128)(2,1)S(1)}, ...), condition=%wide.region_6.7_spmd, body=%wide.region_5.6_spmd.sunk | while | flops 213688320 | bytes 1107083 | solution.py:60
  68.4 3.0 %convolution_add_fusion.4 = f32[8,5120]{1,0:T(8,128)S(1)} fusion(f32[8,5120]{1,0:T(8,128)S(1)} %get-tuple-element.347, bf16[70,5120]{1,0:T(8,128)(2,1)S(1)} %get-tuple-element.359, bf16[70,1280]{1,0:T(8,128)(2,1)S(1)} %get-tuple-element.358, s32[]{:T(128)S(6)} %select_n.31, bf16[8,1280]{1,0:T(8,128)(2,1)S(1)} %get-tuple-element.357), kind=kOutput, calls=%fused_computation.1.clone.1 | convolution fusion | flops 213688320 | bytes 1106944 | tf_op jit(solution)/shard_map/while/body/eval_jaxpr/dot_general | solution.py:8
  71.5 3.0 %convolution_add_fusion.4 = f32[8,5120]{1,0:T(8,128)S(1)} fusion(f32[8,5120]{1,0:T(8,128)S(1)} %get-tuple-element.347, bf16[70,5120]{1,0:T(8,128)(2,1)S(1)} %get-tuple-element.359, bf16[70,1280]{1,0:T(8,128)(2,1)S(1)} %get-tuple-element.358, s32[]{:T(128)S(6)} %select_n.31, bf16[8,1280]{1,0:T(8,128)(2,1)S(1)} %get-tuple-element.357), kind=kOutput, calls=%fused_computation.1.clone.1 | convolution fusion | flops 213688320 | bytes 1106944 | tf_op jit(solution)/shard_map/while/body/eval_jaxpr/dot_general | solution.py:8
  74.5 3.0 %convolution_add_fusion.4 = f32[8,5120]{1,0:T(8,128)S(1)} fusion(f32[8,5120]{1,0:T(8,128)S(1)} %get-tuple-element.347, bf16[70,5120]{1,0:T(8,128)(2,1)S(1)} %get-tuple-element.359, bf16[70,1280]{1,0:T(8,128)(2,1)S(1)} %get-tuple-element.358, s32[]{:T(128)S(6)} %select_n.31, bf16[8,1280]{1,0:T(8,128)(2,1)S(1)} %get-tuple-element.357), kind=kOutput, calls=%fused_computation.1.clone.1 | convolution fusion | flops 213688320 | bytes 1106944 | tf_op jit(solution)/shard_map/while/body/eval_jaxpr/dot_general | solution.py:8
  77.5 3.0 %convolution_add_fusion.4 = f32[8,5120]{1,0:T(8,128)S(1)} fusion(f32[8,5120]{1,0:T(8,128)S(1)} %get-tuple-element.347, bf16[70,5120]{1,0:T(8,128)(2,1)S(1)} %get-tuple-element.359, bf16[70,1280]{1,0:T(8,128)(2,1)S(1)} %get-tuple-element.358, s32[]{:T(128)S(6)} %select_n.31, bf16[8,1280]{1,0:T(8,128)(2,1)S(1)} %get-tuple-element.357), kind=kOutput, calls=%fused_computation.1.clone.1 | convolution fusion | flops 213688320 | bytes 1106944 | tf_op jit(solution)/shard_map/while/body/eval_jaxpr/dot_general | solution.py:8
  80.5 3.0 %convolution_add_fusion.4 = f32[8,5120]{1,0:T(8,128)S(1)} fusion(f32[8,5120]{1,0:T(8,128)S(1)} %get-tuple-element.347, bf16[70,5120]{1,0:T(8,128)(2,1)S(1)} %get-tuple-element.359, bf16[70,1280]{1,0:T(8,128)(2,1)S(1)} %get-tuple-element.358, s32[]{:T(128)S(6)} %select_n.31, bf16[8,1280]{1,0:T(8,128)(2,1)S(1)} %get-tuple-element.357), kind=kOutput, calls=%fused_computation.1.clone.1 | convolution fusion | flops 213688320 | bytes 1106944 | tf_op jit(solution)/shard_map/while/body/eval_jaxpr/dot_general | solution.py:8
  83.9 33.1 %all_to_all.10 = f32[32,8,160]{2,1,0:T(8,128)S(1)} all-to-all(f32[32,8,160]{2,1,0:T(8,128)S(1)} %copy.9), channel_id=1, replica_groups=mesh['row'=16,'col'=32] {'col'}, dimensions={0} | all-to-all | bytes 327680 | tf_op jit(solution)/shard_map/all_to_all | solution.py:96
  117.0 0.6 reduce_sum.39
  (35 shorter events, 1.2 us)
Async XLA Ops:
  0.0 1.6 %copy-start = (bf16[1024,1024]{1,0:T(8,128)(2,1)S(1)}, bf16[1024,1024]{1,0:T(8,128)(2,1)}, u32[]{:S(2)}) copy-start(bf16[1024,1024]{1,0:T(8,128)(2,1)} %param.12) | copy-start | bytes 6291460
  0.0 3.2 %copy-start.5 = (bf16[1024,32]{0,1:T(8,128)(2,1)S(1)}, bf16[1024,32]{0,1:T(8,128)(2,1)}, u32[]{:S(2)}) copy-start(bf16[1024,32]{0,1:T(8,128)(2,1)} %param.13) | copy-start | bytes 196612
  0.0 3.2 %copy-start.6 = (f32[32]{0:T(128)S(1)}, f32[32]{0:T(128)}, u32[]{:S(2)}) copy-start(f32[32]{0:T(128)} %param.14) | copy-start | bytes 388
  1.6 1.8 %copy-start.4 = (bf16[8,160]{1,0:T(8,128)(2,1)S(1)}, bf16[8,160]{1,0:T(8,128)(2,1)}, u32[]{:S(2)}) copy-start(bf16[8,160]{1,0:T(8,128)(2,1)} %param.15) | copy-start | bytes 7684
  4.3 30.9 %all-to-all-start = ((bf16[32,40,160]{2,1,0:T(8,128)(2,1)}), bf16[32,40,160]{2,1,0:T(8,128)(2,1)S(1)}, u32[]{:S(2)}, u32[]{:S(2)}) async-start(bf16[32,40,160]{2,1,0:T(8,128)(2,1)} %broadcast_in_dim.14), calls=%async_computation | async-start | bytes 1310720 | tf_op jit(solution)/shard_map/all_to_all | solution.py:47
  39.0 9.6 %collective-permute-start.1 = (bf16[40,1280]{1,0:T(8,128)(2,1)}, bf16[40,1280]{1,0:T(8,128)(2,1)S(1)}, u32[]{:S(2)}, u32[]{:S(2)}) collective-permute-start(bf16[40,1280]{1,0:T(8,128)(2,1)} %get-tuple-element.233), channel_id=1, source_target_pairs={{0,0},{1,1},{2,482},{3,483},{4,452},{5,453},{6,422},{7,423},{8,392... | collective-permute-start | bytes 307208 | tf_op jit(solution)/shard_map/ppermute | solution.py:88
  40.5 8.8 %collective-permute-start = (bf16[40,1280]{1,0:T(8,128)(2,1)}, bf16[40,1280]{1,0:T(8,128)(2,1)}, u32[]{:S(2)}, u32[]{:S(2)}) collective-permute-start(bf16[40,1280]{1,0:T(8,128)(2,1)} %get-tuple-element.234), channel_id=1, source_target_pairs={{0,0},{1,1},{2,482},{3,483},{4,452},{5,453},{6,422},{7,423},{8,392... | collective-permute-start | bytes 307208 | tf_op jit(solution)/shard_map/ppermute | solution.py:88
  42.9 9.9 %copy-start.1 = (f32[8,5120]{1,0:T(8,128)S(1)}, f32[8,5120]{1,0:T(8,128)}, u32[]{:S(2)}) copy-start(f32[8,5120]{1,0:T(8,128)} %custom-call) | copy-start | bytes 491524
  48.6 2.3 %copy-start.2 = (bf16[40,1280]{1,0:T(8,128)(2,1)}, bf16[40,1280]{1,0:T(8,128)(2,1)S(1)}, u32[]{:S(2)}) copy-start(bf16[40,1280]{1,0:T(8,128)(2,1)S(1)} %collective-permute-done.1) | copy-start | bytes 307204
  52.7 15.2 %copy-start.3 = (bf16[1,1280]{1,0:T(2,128)(2,1)S(1)}, bf16[1,1280]{1,0:T(2,128)(2,1)}, u32[]{:S(2)}) copy-start(bf16[1,1280]{1,0:T(2,128)(2,1)} %mul.208) | copy-start | bytes 7684
  52.7 15.7 %slice-start = ((bf16[40,1280]{1,0:T(8,128)(2,1)}), bf16[8,1280]{1,0:T(8,128)(2,1)S(1)}, s32[]{:S(2)}) async-start(bf16[40,1280]{1,0:T(8,128)(2,1)} %copy-done.2), calls=%async_computation.2 | async-start | bytes 40960 | tf_op jit(solution)/shard_map/slice | solution.py:94

commit v4 on v2

--- a/solution.py
+++ b/solution.py
@@ -10,13 +10,23 @@
     )
 
 
-def matern_tile(left_feats, left_sq, right_feats):
-    cross_term = dot_f32(left_feats, right_feats, ((0,), (0,)))
-    right_wide = right_feats.astype(jnp.float32)
-    right_sq = jnp.sum(right_wide * right_wide, axis=0)
-    dist_sq = jnp.maximum(left_sq[:, None] + right_sq[None, :] - 2.0 * cross_term, 0.0)
-    scaled_dist = jnp.sqrt(5.0 * dist_sq)
-    values = (1.0 + scaled_dist + scaled_dist * scaled_dist / 3.0) * jnp.exp(-scaled_dist)
+def five_sq_norm(feats):
+    wide = feats.astype(jnp.float32)
+    return 5.0 * jnp.sum(wide * wide, axis=0)
+
+
+def minus_ten(feats):
+    scaled = -10.0 * feats.astype(jnp.float32)
+    high = lax.reduce_precision(scaled, exponent_bits=8, mantissa_bits=7)
+    low = scaled - high
+    return jnp.concatenate([high.astype(jnp.bfloat16), low.astype(jnp.bfloat16)], axis=0)
+
+
+def matern_tile(left_feats, left_sq5, right_side, right_sq5):
+    cross_term = dot_f32(left_feats, right_side, ((0,), (0,)))
+    five_dist = jnp.maximum(left_sq5[:, None] + right_sq5[None, :] + cross_term, 0.0)
+    scaled_dist = jnp.sqrt(five_dist)
+    values = (1.0 + scaled_dist + five_dist * (1.0 / 3.0)) * jnp.exp(-scaled_dist)
     return values.astype(jnp.bfloat16)
 
 
@@ -27,15 +37,18 @@
     return jnp.transpose(arrived, (1, 0, 2)).reshape(rows, peers * block.shape[1])
 
 
-def fold_columns(row_feats, row_sq, feats, probes, acc, block_cols):
+def fold_columns(left_feats, left_sq5, right_side, right_sq5, probes, acc, block_cols):
+    doubled = jnp.concatenate([left_feats, left_feats], axis=0)
+
     def advance(position, row_acc):
         column_start = position * block_cols
-        feats_block = lax.dynamic_slice_in_dim(feats, column_start, block_cols, 1)
+        side_block = lax.dynamic_slice_in_dim(right_side, column_start, block_cols, 1)
+        sq_block = lax.dynamic_slice_in_dim(right_sq5, column_start, block_cols, 0)
         probes_block = lax.dynamic_slice_in_dim(probes, column_start, block_cols, 1)
-        kernel_tile = matern_tile(row_feats, row_sq, feats_block)
+        kernel_tile = matern_tile(doubled, left_sq5, side_block, sq_block)
         return row_acc + dot_f32(probes_block, kernel_tile, ((1,), (1,)))
 
-    return lax.fori_loop(0, feats.shape[1] // block_cols, advance, acc)
+    return lax.fori_loop(0, right_side.shape[1] // block_cols, advance, acc)
 
 
 def on_device(points, w_in, w_mid, w_out, lengthscale, probes):
@@ -51,8 +64,7 @@
     joined = jnp.concatenate([scaled, probes], axis=0)
     block = gather_peers(joined, "col", col_peers)
     row_feats = block[:feat_dim]
-    row_wide = row_feats.astype(jnp.float32)
-    row_sq = jnp.sum(row_wide * row_wide, axis=0)
+    row_sq5 = five_sq_norm(row_feats)
     halves = col_peers // row_peers
     span = block.shape[1] // halves
     col = lax.axis_index("col")
@@ -62,7 +74,7 @@
         for c in range(col_peers):
             target = (r - c // halves) % row_peers
             pairs.append((r * col_peers + c, target * col_peers + c))
-    chunks = 2
+    chunks = 1
     width = span // chunks
     arrived = [
         lax.ppermute(mine[:, k * width:(k + 1) * width], ("row", "col"), pairs)
@@ -70,7 +82,11 @@
     ]
     acc = jnp.zeros((probe_rows, block.shape[1]), jnp.float32)
     for piece in arrived:
-        acc = fold_columns(row_feats, row_sq, piece[:feat_dim], piece[feat_dim:], acc, 256)
+        col_feats = piece[:feat_dim]
+        acc = fold_columns(
+            row_feats, row_sq5, minus_ten(col_feats), five_sq_norm(col_feats),
+            piece[feat_dim:], acc, 256,
+        )
     parts = jnp.transpose(acc.reshape(probe_rows, col_peers, local), (1, 0, 2))
     summed = lax.all_to_all(parts, "col", 0, 0, tiled=False)
     return jnp.sum(summed, axis=0)

time: 113 us -> 124 us (1.097)
  matrix products: 39.2 us -> 45.4 us
  blocking collectives: 31.1 us -> 36.5 us
    dot_general x12, matrix products: 39.2 us -> 45.4 us  [dot_f32(): lax.dot_general(left, right, (dims, ((), ())), preferred_element_type=jnp...]
    all_to_all x1, blocking collectives: 31.1 us -> 36.5 us  [on_device(): summed = lax.all_to_all(parts, 'col', 0, 0, tiled=False)]
  transfers between devices with their start and end apart: 3 -> 2, of which waited for: 1 -> 1; matrix products, arithmetic and copies ran while one was open for 19% -> 2% of each run, Pallas kernels for 0% -> 0%
where the time goes in v4:
time: 124 us; the launch traced here: 123 us
  matrix products  45.4 us (37%)
  blocking collectives  36.5 us (29%)
  waiting for transfers between devices  19.5 us (16%)
  starting transfers between devices  12.2 us (10%)
  local copies, waits for them, and re-layouts  7.68 us (6%)
  other arithmetic  1.83 us (1%)
    dot_general x12, matrix products, dot_f32(): lax.dot_general(left, right, (dims, ((), ())), preferred_element_type=jnp...  45.4 us
    all_to_all x1, blocking collectives, on_device(): summed = lax.all_to_all(parts, 'col', 0, 0, tiled=False)  36.5 us
    all_to_all x1, waiting for transfers between devices, gather_peers(): arrived = lax.all_to_all(spread, axis, 0, 0, tiled=False)  19.5 us
    all_to_all x1, starting transfers between devices, gather_peers(): arrived = lax.all_to_all(spread, axis, 0, 0, tiled=False)  11.4 us
    slice x3, local copies, waits for them, and re-layouts, on_device(): row_feats = block[:feat_dim]  2.92 us
  transfers between devices with their start and end apart: 2, of which 1 were waited for; matrix products, arithmetic and copies ran while one was open for 2% of the time, Pallas kernels for 0%

profile of v4, /device:TPU:1, one launch (start us, length us, event | category | flops | bytes accessed | tf_op | source)
XLA Modules:
  0.0 123.4 jit_solution(1879913002895834313)
XLA Ops:
  0.0 1.6 %copy-done = bf16[1024,1024]{1,0:T(8,128)(2,1)S(1)} copy-done((bf16[1024,1024]{1,0:T(8,128)(2,1)S(1)}, bf16[1024,1024]{1,0:T(8,128)(2,1)}, u32[]{:S(2)}) %copy-start) | copy-done | bytes 2097176
  1.6 1.6 %fusion.11 = bf16[160,1024]{1,0:T(8,128)(2,1)S(1)} fusion(bf16[1024,1024]{1,0:T(8,128)(2,1)S(1)} %copy-done, bf16[160,128]{1,0:T(8,128)(2,1)} %param.8, bf16[128,1024]{1,0:T(8,128)(2,1)} %param.9), kind=kOutput, calls=%fused_computation.14 | convolution fusion | flops 378142720 | bytes 2727936 | tf_op jit(solution)/shard_map/dot_general | solution.py:8
  3.2 0.2 fusion.13
  3.5 0.9 broadcast_in_dim.17
  4.3 11.4 %all-to-all-start = ((bf16[32,40,160]{2,1,0:T(8,128)(2,1)}), bf16[32,40,160]{2,1,0:T(8,128)(2,1)S(1)}, u32[]{:S(2)}, u32[]{:S(2)}) async-start(bf16[32,40,160]{2,1,0:T(8,128)(2,1)} %broadcast_in_dim.17), calls=%async_computation | async-start | bytes 1310720 | tf_op jit(solution)/shard_map/all_to_all | solution.py:35
  15.8 19.5 %all-to-all-done = bf16[32,40,160]{2,1,0:T(8,128)(2,1)S(1)} async-done(((bf16[32,40,160]{2,1,0:T(8,128)(2,1)}), bf16[32,40,160]{2,1,0:T(8,128)(2,1)S(1)}, u32[]{:S(2)}, u32[]{:S(2)}) %all-to-all-start) | async-done | bytes 409632 | tf_op jit(solution)/shard_map/all_to_all | solution.py:35
  35.3 0.1 copy.7
  35.4 0.2 multiply_reduce_fusion
  35.6 0.8 slice.17
  36.4 1.0 reshape.14
  37.5 0.8 collective-permute-start
  38.3 1.3 %copy.8 = bf16[32,32,160]{2,1,0:T(8,128)(2,1)S(1)} copy(bf16[32,32,160]{2,0,1:T(8,128)(2,1)} %slice.17) | data formatting | bytes 655360 | tf_op jit(solution)/shard_map/slice | solution.py:66
  39.6 0.7 slice.15
  40.4 0.9 pad_maximum_fusion
  41.3 0.1 mul.56
  41.4 0.1 reduce-precision_convert_fusion
  41.5 44.4 %while.14 = (s32[]{:T(128)}, f32[8,5120]{1,0:T(8,128)S(1)}, bf16[8,2560]{1,0:T(8,128)(2,1)S(1)}, f32[5120]{0:T(1024)S(1)}, f32[2560]{0:T(1024)S(1)}, /*index=5*/...) while((s32[]{:T(128)}, f32[8,5120]{1,0:T(8,128)S(1)}, ...), condition=%wide.region_3.4_spmd.clone, body=%wide.region_2.3_spmd.clone.sunk | while | flops 200622080 | bytes 1045168 | solution.py:51
  41.6 0.1 dynamic_slice.39
  41.6 4.4 %convolution_add_fusion.2 = f32[8,5120]{1,0:T(8,128)S(1)} fusion(bf16[64,5120]{1,0:T(8,128)(2,1)} %get-tuple-element.242, f32[256]{0:T(256)S(1)} %dynamic_slice.39, f32[5120]{0:T(1024)S(1)} %get-tuple-element.239, f32[8,5120]{1,0:T(8,128)S(1)} %get-tuple-element.226, pred[]{:T(512)S(6)} %compare.4, bf16[64,2560]{1,0:T(8,128)(2,1)S(1)} %get-tuple-element.241, ...), kind=kOutput, calls=%fused_computation.3.clone.1 | convolution fusion | flops 200622080 | bytes 1042944 | tf_op jit(solution)/shard_map/while/body/eval_jaxpr/dot_general | solution.py:8
  46.1 4.4 %convolution_add_fusion.2 = f32[8,5120]{1,0:T(8,128)S(1)} fusion(bf16[64,5120]{1,0:T(8,128)(2,1)} %get-tuple-element.242, f32[256]{0:T(256)S(1)} %dynamic_slice.39, f32[5120]{0:T(1024)S(1)} %get-tuple-element.239, f32[8,5120]{1,0:T(8,128)S(1)} %get-tuple-element.226, pred[]{:T(512)S(6)} %compare.4, bf16[64,2560]{1,0:T(8,128)(2,1)S(1)} %get-tuple-element.241, ...), kind=kOutput, calls=%fused_computation.3.clone.1 | convolution fusion | flops 200622080 | bytes 1042944 | tf_op jit(solution)/shard_map/while/body/eval_jaxpr/dot_general | solution.py:8
  50.5 4.4 %convolution_add_fusion.2 = f32[8,5120]{1,0:T(8,128)S(1)} fusion(bf16[64,5120]{1,0:T(8,128)(2,1)} %get-tuple-element.242, f32[256]{0:T(256)S(1)} %dynamic_slice.39, f32[5120]{0:T(1024)S(1)} %get-tuple-element.239, f32[8,5120]{1,0:T(8,128)S(1)} %get-tuple-element.226, pred[]{:T(512)S(6)} %compare.4, bf16[64,2560]{1,0:T(8,128)(2,1)S(1)} %get-tuple-element.241, ...), kind=kOutput, calls=%fused_computation.3.clone.1 | convolution fusion | flops 200622080 | bytes 1042944 | tf_op jit(solution)/shard_map/while/body/eval_jaxpr/dot_general | solution.py:8
  54.9 4.4 %convolution_add_fusion.2 = f32[8,5120]{1,0:T(8,128)S(1)} fusion(bf16[64,5120]{1,0:T(8,128)(2,1)} %get-tuple-element.242, f32[256]{0:T(256)S(1)} %dynamic_slice.39, f32[5120]{0:T(1024)S(1)} %get-tuple-element.239, f32[8,5120]{1,0:T(8,128)S(1)} %get-tuple-element.226, pred[]{:T(512)S(6)} %compare.4, bf16[64,2560]{1,0:T(8,128)(2,1)S(1)} %get-tuple-element.241, ...), kind=kOutput, calls=%fused_computation.3.clone.1 | convolution fusion | flops 200622080 | bytes 1042944 | tf_op jit(solution)/shard_map/while/body/eval_jaxpr/dot_general | solution.py:8
  59.4 4.4 %convolution_add_fusion.2 = f32[8,5120]{1,0:T(8,128)S(1)} fusion(bf16[64,5120]{1,0:T(8,128)(2,1)} %get-tuple-element.242, f32[256]{0:T(256)S(1)} %dynamic_slice.39, f32[5120]{0:T(1024)S(1)} %get-tuple-element.239, f32[8,5120]{1,0:T(8,128)S(1)} %get-tuple-element.226, pred[]{:T(512)S(6)} %compare.4, bf16[64,2560]{1,0:T(8,128)(2,1)S(1)} %get-tuple-element.241, ...), kind=kOutput, calls=%fused_computation.3.clone.1 | convolution fusion | flops 200622080 | bytes 1042944 | tf_op jit(solution)/shard_map/while/body/eval_jaxpr/dot_general | solution.py:8
  63.8 4.4 %convolution_add_fusion.2 = f32[8,5120]{1,0:T(8,128)S(1)} fusion(bf16[64,5120]{1,0:T(8,128)(2,1)} %get-tuple-element.242, f32[256]{0:T(256)S(1)} %dynamic_slice.39, f32[5120]{0:T(1024)S(1)} %get-tuple-element.239, f32[8,5120]{1,0:T(8,128)S(1)} %get-tuple-element.226, pred[]{:T(512)S(6)} %compare.4, bf16[64,2560]{1,0:T(8,128)(2,1)S(1)} %get-tuple-element.241, ...), kind=kOutput, calls=%fused_computation.3.clone.1 | convolution fusion | flops 200622080 | bytes 1042944 | tf_op jit(solution)/shard_map/while/body/eval_jaxpr/dot_general | solution.py:8
  68.3 4.4 %convolution_add_fusion.2 = f32[8,5120]{1,0:T(8,128)S(1)} fusion(bf16[64,5120]{1,0:T(8,128)(2,1)} %get-tuple-element.242, f32[256]{0:T(256)S(1)} %dynamic_slice.39, f32[5120]{0:T(1024)S(1)} %get-tuple-element.239, f32[8,5120]{1,0:T(8,128)S(1)} %get-tuple-element.226, pred[]{:T(512)S(6)} %compare.4, bf16[64,2560]{1,0:T(8,128)(2,1)S(1)} %get-tuple-element.241, ...), kind=kOutput, calls=%fused_computation.3.clone.1 | convolution fusion | flops 200622080 | bytes 1042944 | tf_op jit(solution)/shard_map/while/body/eval_jaxpr/dot_general | solution.py:8
  72.7 4.4 %convolution_add_fusion.2 = f32[8,5120]{1,0:T(8,128)S(1)} fusion(bf16[64,5120]{1,0:T(8,128)(2,1)} %get-tuple-element.242, f32[256]{0:T(256)S(1)} %dynamic_slice.39, f32[5120]{0:T(1024)S(1)} %get-tuple-element.239, f32[8,5120]{1,0:T(8,128)S(1)} %get-tuple-element.226, pred[]{:T(512)S(6)} %compare.4, bf16[64,2560]{1,0:T(8,128)(2,1)S(1)} %get-tuple-element.241, ...), kind=kOutput, calls=%fused_computation.3.clone.1 | convolution fusion | flops 200622080 | bytes 1042944 | tf_op jit(solution)/shard_map/while/body/eval_jaxpr/dot_general | solution.py:8
  77.1 4.4 %convolution_add_fusion.2 = f32[8,5120]{1,0:T(8,128)S(1)} fusion(bf16[64,5120]{1,0:T(8,128)(2,1)} %get-tuple-element.242, f32[256]{0:T(256)S(1)} %dynamic_slice.39, f32[5120]{0:T(1024)S(1)} %get-tuple-element.239, f32[8,5120]{1,0:T(8,128)S(1)} %get-tuple-element.226, pred[]{:T(512)S(6)} %compare.4, bf16[64,2560]{1,0:T(8,128)(2,1)S(1)} %get-tuple-element.241, ...), kind=kOutput, calls=%fused_computation.3.clone.1 | convolution fusion | flops 200622080 | bytes 1042944 | tf_op jit(solution)/shard_map/while/body/eval_jaxpr/dot_general | solution.py:8
  81.6 4.4 %convolution_add_fusion.2 = f32[8,5120]{1,0:T(8,128)S(1)} fusion(bf16[64,5120]{1,0:T(8,128)(2,1)} %get-tuple-element.242, f32[256]{0:T(256)S(1)} %dynamic_slice.39, f32[5120]{0:T(1024)S(1)} %get-tuple-element.239, f32[8,5120]{1,0:T(8,128)S(1)} %get-tuple-element.226, pred[]{:T(512)S(6)} %compare.4, bf16[64,2560]{1,0:T(8,128)(2,1)S(1)} %get-tuple-element.241, ...), kind=kOutput, calls=%fused_computation.3.clone.1 | convolution fusion | flops 200622080 | bytes 1042944 | tf_op jit(solution)/shard_map/while/body/eval_jaxpr/dot_general | solution.py:8
  85.9 0.1 reshape.15
  86.1 0.2 copy.9
  86.2 36.5 %all_to_all.10 = f32[32,8,160]{2,1,0:T(8,128)S(1)} all-to-all(f32[32,8,160]{2,1,0:T(8,128)S(1)} %copy.9), channel_id=1, replica_groups=mesh['row'=16,'col'=32] {'col'}, dimensions={0} | all-to-all | bytes 327680 | tf_op jit(solution)/shard_map/all_to_all | solution.py:91
  122.8 0.6 reduce_sum.29
  (26 shorter events, 0.8 us)
Async XLA Ops:
  0.0 1.6 %copy-start = (bf16[1024,1024]{1,0:T(8,128)(2,1)S(1)}, bf16[1024,1024]{1,0:T(8,128)(2,1)}, u32[]{:S(2)}) copy-start(bf16[1024,1024]{1,0:T(8,128)(2,1)} %param.10) | copy-start | bytes 6291460
  0.0 3.2 %copy-start.3 = (bf16[1024,32]{0,1:T(8,128)(2,1)S(1)}, bf16[1024,32]{0,1:T(8,128)(2,1)}, u32[]{:S(2)}) copy-start(bf16[1024,32]{0,1:T(8,128)(2,1)} %param.11) | copy-start | bytes 196612
  0.0 3.2 %copy-start.4 = (f32[32]{0:T(128)S(1)}, f32[32]{0:T(128)}, u32[]{:S(2)}) copy-start(f32[32]{0:T(128)} %param.12) | copy-start | bytes 388
  1.6 1.8 %copy-start.2 = (bf16[8,160]{1,0:T(8,128)(2,1)S(1)}, bf16[8,160]{1,0:T(8,128)(2,1)}, u32[]{:S(2)}) copy-start(bf16[8,160]{1,0:T(8,128)(2,1)} %param.13) | copy-start | bytes 7684
  4.3 30.9 %all-to-all-start = ((bf16[32,40,160]{2,1,0:T(8,128)(2,1)}), bf16[32,40,160]{2,1,0:T(8,128)(2,1)S(1)}, u32[]{:S(2)}, u32[]{:S(2)}) async-start(bf16[32,40,160]{2,1,0:T(8,128)(2,1)} %broadcast_in_dim.17), calls=%async_computation | async-start | bytes 1310720 | tf_op jit(solution)/shard_map/all_to_all | solution.py:35
  37.5 4.1 %copy-start.1 = (f32[8,5120]{1,0:T(8,128)S(1)}, f32[8,5120]{1,0:T(8,128)}, u32[]{:S(2)}) copy-start(f32[8,5120]{1,0:T(8,128)} %custom-call) | copy-start | bytes 491524
  37.5 3.9 %collective-permute-start = (bf16[40,2560]{1,0:T(8,128)(2,1)S(1)}, bf16[40,2560]{1,0:T(8,128)(2,1)S(1)}, u32[]{:S(2)}, u32[]{:S(2)}) collective-permute-start(bf16[40,2560]{1,0:T(8,128)(2,1)S(1)} %constant_dynamic-slice_fusion), channel_id=1, source_target_pairs={{0,0},{1,1},{2,482},{3,483},{4,452},{5,453},{6,422},{7,423},{8,392... | collective-permute-start | bytes 614408 | tf_op jit(solution)/shard_map/ppermute | solution.py:80

commit v5 on v4

--- a/solution.py
+++ b/solution.py
@@ -1,6 +1,9 @@
+import functools
+
 import jax
 import jax.numpy as jnp
 from jax import lax
+from jax.experimental import pallas as pl
 from jax.sharding import PartitionSpec as P
 
 
@@ -22,12 +25,52 @@
     return jnp.concatenate([high.astype(jnp.bfloat16), low.astype(jnp.bfloat16)], axis=0)
 
 
-def matern_tile(left_feats, left_sq5, right_side, right_sq5):
-    cross_term = dot_f32(left_feats, right_side, ((0,), (0,)))
-    five_dist = jnp.maximum(left_sq5[:, None] + right_sq5[None, :] + cross_term, 0.0)
-    scaled_dist = jnp.sqrt(five_dist)
-    values = (1.0 + scaled_dist + five_dist * (1.0 / 3.0)) * jnp.exp(-scaled_dist)
-    return values.astype(jnp.bfloat16)
+def matern_kernel(lhs_ref, lsq_ref, rhs_ref, rsq_ref, pr_ref, out_ref, *, sub):
+    @pl.when(pl.program_id(1) == 0)
+    def _():
+        out_ref[...] = jnp.zeros_like(out_ref)
+
+    rhs = rhs_ref[...]
+    rsq = rsq_ref[...]
+    probes = pr_ref[...]
+
+    def body(step, carry):
+        start = pl.multiple_of(step * sub, sub)
+        cross = jnp.dot(lhs_ref[pl.ds(start, sub), :], rhs, preferred_element_type=jnp.float32)
+        five_dist = jnp.maximum(lsq_ref[pl.ds(start, sub), :] + rsq + cross, 0.0)
+        scaled_dist = jnp.sqrt(five_dist)
+        values = (1.0 + scaled_dist + five_dist * (1.0 / 3.0)) * jnp.exp(-scaled_dist)
+        tile = values.astype(jnp.bfloat16)
+        part = lax.dot_general(probes, tile, (((1,), (1,)), ((), ())), preferred_element_type=jnp.float32)
+        out_ref[:, pl.ds(start, sub)] += part
+        return carry
+
+    lax.fori_loop(0, lhs_ref.shape[0] // sub, body, 0)
+
+
+def matern_probes(lhs, lsq, rhs, rsq, probes, rows_tile=640, cols_tile=1280, sub=128):
+    rows = lhs.shape[0]
+    cols = rhs.shape[1]
+    depth = lhs.shape[1]
+    grid = (rows // rows_tile, cols // cols_tile)
+    return pl.pallas_call(
+        functools.partial(matern_kernel, sub=sub),
+        out_shape=jax.ShapeDtypeStruct((probes.shape[0], rows), jnp.float32),
+        grid=grid,
+        in_specs=[
+            pl.BlockSpec((rows_tile, depth), lambda i, j: (i, 0)),
+            pl.BlockSpec((rows_tile, 1), lambda i, j: (i, 0)),
+            pl.BlockSpec((depth, cols_tile), lambda i, j: (0, j)),
+            pl.BlockSpec((1, cols_tile), lambda i, j: (0, j)),
+            pl.BlockSpec((probes.shape[0], cols_tile), lambda i, j: (0, j)),
+        ],
+        out_specs=pl.BlockSpec((probes.shape[0], rows_tile), lambda i, j: (0, i)),
+        cost_estimate=pl.CostEstimate(
+            flops=2 * rows * cols * (depth + probes.shape[0]) + 12 * rows * cols,
+            transcendentals=2 * rows * cols,
+            bytes_accessed=2 * (rows * depth + cols * depth) + 4 * rows * 8,
+        ),
+    )(lhs, lsq, rhs, rsq, probes)
 
 
 def gather_peers(block, axis, peers):
@@ -35,20 +78,6 @@
     arrived = lax.all_to_all(spread, axis, 0, 0, tiled=False)
     rows = block.shape[0]
     return jnp.transpose(arrived, (1, 0, 2)).reshape(rows, peers * block.shape[1])
-
-
-def fold_columns(left_feats, left_sq5, right_side, right_sq5, probes, acc, block_cols):
-    doubled = jnp.concatenate([left_feats, left_feats], axis=0)
-
-    def advance(position, row_acc):
-        column_start = position * block_cols
-        side_block = lax.dynamic_slice_in_dim(right_side, column_start, block_cols, 1)
-        sq_block = lax.dynamic_slice_in_dim(right_sq5, column_start, block_cols, 0)
-        probes_block = lax.dynamic_slice_in_dim(probes, column_start, block_cols, 1)
-        kernel_tile = matern_tile(doubled, left_sq5, side_block, sq_block)
-        return row_acc + dot_f32(probes_block, kernel_tile, ((1,), (1,)))
-
-    return lax.fori_loop(0, right_side.shape[1] // block_cols, advance, acc)
 
 
 def on_device(points, w_in, w_mid, w_out, lengthscale, probes):
@@ -80,13 +109,13 @@
         lax.ppermute(mine[:, k * width:(k + 1) * width], ("row", "col"), pairs)
         for k in range(chunks)
     ]
-    acc = jnp.zeros((probe_rows, block.shape[1]), jnp.float32)
-    for piece in arrived:
-        col_feats = piece[:feat_dim]
-        acc = fold_columns(
-            row_feats, row_sq5, minus_ten(col_feats), five_sq_norm(col_feats),
-            piece[feat_dim:], acc, 256,
-        )
+    (piece,) = arrived
+    col_feats = piece[:feat_dim]
+    lhs = jnp.concatenate([row_feats, row_feats], axis=0).T
+    acc = matern_probes(
+        lhs, row_sq5[:, None], minus_ten(col_feats), five_sq_norm(col_feats)[None, :],
+        piece[feat_dim:],
+    )
     parts = jnp.transpose(acc.reshape(probe_rows, col_peers, local), (1, 0, 2))
     summed = lax.all_to_all(parts, "col", 0, 0, tiled=False)
     return jnp.sum(summed, axis=0)

time: 124 us -> 138 us (1.11)
  Pallas kernels: 0 us -> 52.6 us
  matrix products: 45.4 us -> 1.8 us
  blocking collectives: 36.5 us -> 29.8 us
  local copies, waits for them, and re-layouts: 7.68 us -> 13.9 us
  starting transfers between devices: 12.2 us -> 14.8 us
  other arithmetic: 1.83 us -> 4.39 us
    pallas_call x0 -> x1, Pallas kernels: none -> 52.6 us  [matern_probes(): pl.pallas_call(functools.partial(matern_kernel, sub=sub), out_shape=jax.S...]
    dot_general x12 -> x2, matrix products: 45.4 us -> 1.8 us  [dot_f32(): lax.dot_general(left, right, (dims, ((), ())), preferred_element_type=jnp...]
    all_to_all x1, blocking collectives: 36.5 us -> 29.8 us  [on_device(): summed = lax.all_to_all(parts, 'col', 0, 0, tiled=False)]
    mul x1 -> x2, local copies, waits for them, and re-layouts: 0.08 us -> 4.6 us  [five_sq_norm(): return 5.0 * jnp.sum(wide * wide, axis=0)]
    ppermute x1, starting transfers between devices: 0.81 us -> 3.4 us  [on_device(): lax.ppermute(mine[:, k * width:(k + 1) * width], ('row', 'col'), pairs)]
    transpose x0 -> x1, other arithmetic: none -> 1.8 us  [on_device(): lhs = jnp.concatenate([row_feats, row_feats], axis=0).T]
    slice x1, local copies, waits for them, and re-layouts: 0.01 us -> 1.39 us  [on_device(): piece[feat_dim:]]
    slice x3 -> x2, local copies, waits for them, and re-layouts: 2.92 us -> 2.44 us  [on_device(): row_feats = block[:feat_dim]]
  transfers between devices with their start and end apart: 2 -> 2, of which waited for: 1 -> 1; matrix products, arithmetic and copies ran while one was open for 2% -> 5% of each run, Pallas kernels for 0% -> 0%
where the time goes in v5:
time: 138 us; the launch traced here: 137 us
  Pallas kernels  52.6 us (38%)
  blocking collectives  29.8 us (22%)
  waiting for transfers between devices  19.5 us (14%)
  starting transfers between devices  14.8 us (11%)
  local copies, waits for them, and re-layouts  13.9 us (10%)
  other arithmetic  4.39 us (3%)
  matrix products  1.8 us (1%)
    pallas_call x1, Pallas kernels, matern_probes(): pl.pallas_call(functools.partial(matern_kernel, sub=sub), out_shape=jax.S...  52.6 us
    all_to_all x1, blocking collectives, on_device(): summed = lax.all_to_all(parts, 'col', 0, 0, tiled=False)  29.8 us
    all_to_all x1, waiting for transfers between devices, gather_peers(): arrived = lax.all_to_all(spread, axis, 0, 0, tiled=False)  19.5 us
    all_to_all x1, starting transfers between devices, gather_peers(): arrived = lax.all_to_all(spread, axis, 0, 0, tiled=False)  11.4 us
    mul x2, local copies, waits for them, and re-layouts, five_sq_norm(): return 5.0 * jnp.sum(wide * wide, axis=0)  4.6 us
    ppermute x1, starting transfers between devices, on_device(): lax.ppermute(mine[:, k * width:(k + 1) * width], ('row', 'col'), pairs)  3.4 us
  transfers between devices with their start and end apart: 2, of which 1 were waited for; matrix products, arithmetic and copies ran while one was open for 5% of the time, Pallas kernels for 0%

profile of v5, /device:TPU:1, one launch (start us, length us, event | category | flops | bytes accessed | tf_op | source)
XLA Modules:
  0.0 137.0 jit_solution(14693929649000336785)
XLA Ops:
  0.0 0.0 copy-start
  0.0 0.0 copy-start.3
  0.0 0.0 copy-start.2
  0.0 1.6 %copy-done = bf16[1024,1024]{1,0:T(8,128)(2,1)S(1)} copy-done((bf16[1024,1024]{1,0:T(8,128)(2,1)S(1)}, bf16[1024,1024]{1,0:T(8,128)(2,1)}, u32[]{:S(2)}) %copy-start) | copy-done | bytes 2097176
  1.6 0.0 copy-start.1
  1.6 1.6 %fusion.1 = bf16[160,1024]{1,0:T(8,128)(2,1)S(1)} fusion(bf16[1024,1024]{1,0:T(8,128)(2,1)S(1)} %copy-done, bf16[160,128]{1,0:T(8,128)(2,1)} %param.6, bf16[128,1024]{1,0:T(8,128)(2,1)} %param.7), kind=kOutput, calls=%fused_computation.4 | convolution fusion | flops 378142720 | bytes 2727936 | tf_op jit(solution)/shard_map/dot_general | solution.py:11
  3.2 0.0 copy-done.3
  3.2 0.0 copy-done.2
  3.2 0.2 fusion.3
  3.4 0.0 copy-done.1
  3.5 0.9 broadcast_in_dim.2
  4.3 11.4 %all-to-all-start = ((bf16[32,40,160]{2,1,0:T(8,128)(2,1)}), bf16[32,40,160]{2,1,0:T(8,128)(2,1)S(1)}, u32[]{:S(2)}, u32[]{:S(2)}) async-start(bf16[32,40,160]{2,1,0:T(8,128)(2,1)} %broadcast_in_dim.2), calls=%async_computation | async-start | bytes 1310720 | tf_op jit(solution)/shard_map/all_to_all | solution.py:78
  15.7 19.5 %all-to-all-done = bf16[32,40,160]{2,1,0:T(8,128)(2,1)S(1)} async-done(((bf16[32,40,160]{2,1,0:T(8,128)(2,1)}), bf16[32,40,160]{2,1,0:T(8,128)(2,1)S(1)}, u32[]{:S(2)}, u32[]{:S(2)}) %all-to-all-start) | async-done | bytes 409632 | tf_op jit(solution)/shard_map/all_to_all | solution.py:78
  35.3 0.2 multiply_reduce_fusion
  35.4 0.9 slice.16
  36.3 0.1 copy.11
  36.4 1.0 reshape.32
  37.4 0.7 constant_dynamic-slice_fusion
  38.1 3.4 %collective-permute-start = (bf16[40,2560]{1,0:T(8,128)(2,1)}, bf16[40,2560]{1,0:T(8,128)(2,1)}, u32[]{:S(2)}, u32[]{:S(2)}) collective-permute-start(bf16[40,2560]{1,0:T(8,128)(2,1)} %constant_dynamic-slice_fusion), channel_id=1, source_target_pairs={{0,0},{1,1},{2,482},{3,483},{4,452},{5,453},{6,422},{7,423},{8,392... | collective-permute-start | bytes 614408 | tf_op jit(solution)/shard_map/ppermute | solution.py:109
  41.5 1.6 %copy.10 = bf16[32,32,160]{0,2,1:T(8,128)(2,1)S(1)} copy(bf16[32,32,160]{2,0,1:T(8,128)(2,1)} %slice.16) | data formatting | bytes 655360 | tf_op jit(solution)/shard_map/slice | solution.py:95
  43.1 1.8 %maximum_bitcast_fusion.lhs_ref = bf16[5120,64]{1,0:T(8,128)(2,1)} fusion(bf16[32,5120]{0,1:T(8,128)(2,1)S(1)} %bitcast.17), kind=kLoop, calls=%fused_computation | loop fusion | flops 1310720 | bytes 983040 | tf_op jit(solution)/shard_map/transpose | solution.py:114
  44.9 4.0 %mul.59.lsq_ref = f32[5120,1]{1,0:T(8,128)} reshape(f32[32,160]{1,0:T(8,128)S(1)} %broadcast_multiply_fusion) | data formatting | bytes 40960 | tf_op jit(solution)/shard_map/mul | solution.py:18
  48.9 0.0 collective-permute-done
  48.9 1.0 fusion.4
  50.0 0.6 mul.58.rsq_ref
  50.6 0.7 pad_maximum_fusion.rhs_ref
  51.3 1.4 %slice.18.pr_ref = bf16[8,2560]{1,0:T(8,128)(2,1)} slice(bf16[40,2560]{1,0:T(8,128)(2,1)} %collective-permute-done), slice={[32:40], [0:2560]} | slice | bytes 81920 | tf_op jit(solution)/shard_map/slice | solution.py:117
  52.7 52.6 %shard_map.64 = f32[8,5120]{1,0:T(8,128)} custom-call(bf16[5120,64]{1,0:T(8,128)(2,1)} %maximum_bitcast_fusion.lhs_ref, f32[5120,1]{1,0:T(8,128)} %mul.59.lsq_ref, bf16[64,2560]{1,0:T(8,128)(2,1)} %pad_maximum_fusion.rhs_ref, f32[1,2560]{1,0:T(1,128)} %mul.58.rsq_ref, bf16[8,2560]{1,0:T(8,128)(2,1)} %slice.18.pr_ref), custom_call_target="tpu_custom_call" | custom-call | flops 2044723200 | bytes 1146880 | tf_op jit(solution)/shard_map/pallas_call | solution.py:56
  105.4 1.0 reshape.33
  106.4 0.2 copy.15
  106.6 29.8 %all_to_all.10 = f32[32,8,160]{2,1,0:T(8,128)S(1)} all-to-all(f32[32,8,160]{2,1,0:T(8,128)S(1)} %bitcast.18), channel_id=1, replica_groups=mesh['row'=16,'col'=32] {'col'}, dimensions={0} | all-to-all | bytes 327680 | tf_op jit(solution)/shard_map/all_to_all | solution.py:120
  136.4 0.6 reduce_sum.29
  (3 shorter events, 0.0 us)
Async XLA Ops:
  0.0 1.6 %copy-start = (bf16[1024,1024]{1,0:T(8,128)(2,1)S(1)}, bf16[1024,1024]{1,0:T(8,128)(2,1)}, u32[]{:S(2)}) copy-start(bf16[1024,1024]{1,0:T(8,128)(2,1)} %param.8) | copy-start | bytes 6291460
  0.0 3.2 %copy-start.3 = (f32[32]{0:T(128)S(1)}, f32[32]{0:T(128)}, u32[]{:S(2)}) copy-start(f32[32]{0:T(128)} %param.10) | copy-start | bytes 388
  0.0 3.2 %copy-start.2 = (bf16[1024,32]{0,1:T(8,128)(2,1)S(1)}, bf16[1024,32]{0,1:T(8,128)(2,1)}, u32[]{:S(2)}) copy-start(bf16[1024,32]{0,1:T(8,128)(2,1)} %param.9) | copy-start | bytes 196612
  1.6 1.8 %copy-start.1 = (bf16[8,160]{1,0:T(8,128)(2,1)S(1)}, bf16[8,160]{1,0:T(8,128)(2,1)}, u32[]{:S(2)}) copy-start(bf16[8,160]{1,0:T(8,128)(2,1)} %param.11) | copy-start | bytes 7684
  4.3 30.9 %all-to-all-start = ((bf16[32,40,160]{2,1,0:T(8,128)(2,1)}), bf16[32,40,160]{2,1,0:T(8,128)(2,1)S(1)}, u32[]{:S(2)}, u32[]{:S(2)}) async-start(bf16[32,40,160]{2,1,0:T(8,128)(2,1)} %broadcast_in_dim.2), calls=%async_computation | async-start | bytes 1310720 | tf_op jit(solution)/shard_map/all_to_all | solution.py:78
  38.1 10.8 %collective-permute-start = (bf16[40,2560]{1,0:T(8,128)(2,1)}, bf16[40,2560]{1,0:T(8,128)(2,1)}, u32[]{:S(2)}, u32[]{:S(2)}) collective-permute-start(bf16[40,2560]{1,0:T(8,128)(2,1)} %constant_dynamic-slice_fusion), channel_id=1, source_target_pairs={{0,0},{1,1},{2,482},{3,483},{4,452},{5,453},{6,422},{7,423},{8,392... | collective-permute-start | bytes 614408 | tf_op jit(solution)/shard_map/ppermute | solution.py:109

commit v6 on v5

--- a/solution.py
+++ b/solution.py
@@ -25,52 +25,63 @@
     return jnp.concatenate([high.astype(jnp.bfloat16), low.astype(jnp.bfloat16)], axis=0)
 
 
-def matern_kernel(lhs_ref, lsq_ref, rhs_ref, rsq_ref, pr_ref, out_ref, *, sub):
+def matern_kernel(lhs_ref, lsq_ref, rhs_ref, rsq_ref, prt_ref, out_ref, *, rows_sub, cols_sub):
     @pl.when(pl.program_id(1) == 0)
     def _():
         out_ref[...] = jnp.zeros_like(out_ref)
 
-    rhs = rhs_ref[...]
-    rsq = rsq_ref[...]
-    probes = pr_ref[...]
+    def col_body(col_step, carry):
+        col_start = pl.multiple_of(col_step * cols_sub, cols_sub)
+        rhs = rhs_ref[:, pl.ds(col_start, cols_sub)]
+        rsq = rsq_ref[:, pl.ds(col_start, cols_sub)]
+        probes_t = prt_ref[pl.ds(col_start, cols_sub), :]
 
-    def body(step, carry):
-        start = pl.multiple_of(step * sub, sub)
-        cross = jnp.dot(lhs_ref[pl.ds(start, sub), :], rhs, preferred_element_type=jnp.float32)
-        five_dist = jnp.maximum(lsq_ref[pl.ds(start, sub), :] + rsq + cross, 0.0)
-        scaled_dist = jnp.sqrt(five_dist)
-        values = (1.0 + scaled_dist + five_dist * (1.0 / 3.0)) * jnp.exp(-scaled_dist)
-        tile = values.astype(jnp.bfloat16)
-        part = lax.dot_general(probes, tile, (((1,), (1,)), ((), ())), preferred_element_type=jnp.float32)
-        out_ref[:, pl.ds(start, sub)] += part
+        def row_body(row_step, inner):
+            row_start = pl.multiple_of(row_step * rows_sub, rows_sub)
+            cross = jnp.dot(
+                lhs_ref[pl.ds(row_start, rows_sub), :], rhs,
+                preferred_element_type=jnp.float32,
+            )
+            five_dist = jnp.maximum(lsq_ref[pl.ds(row_start, rows_sub), :] + rsq + cross, 0.0)
+            scaled_dist = jnp.sqrt(five_dist)
+            values = (1.0 + scaled_dist + five_dist * (1.0 / 3.0)) * jnp.exp(-scaled_dist)
+            tile = values.astype(jnp.bfloat16)
+            out_ref[pl.ds(row_start, rows_sub), :] += jnp.dot(
+                tile, probes_t, preferred_element_type=jnp.float32
+            )
+            return inner
+
+        lax.fori_loop(0, lhs_ref.shape[0] // rows_sub, row_body, 0)
         return carry
 
-    lax.fori_loop(0, lhs_ref.shape[0] // sub, body, 0)
+    lax.fori_loop(0, rhs_ref.shape[1] // cols_sub, col_body, 0)
 
 
-def matern_probes(lhs, lsq, rhs, rsq, probes, rows_tile=640, cols_tile=1280, sub=128):
+def matern_probes(lhs, lsq, rhs, rsq, probes_t, rows_tile=1280, cols_tile=1280,
+                  rows_sub=128, cols_sub=256):
     rows = lhs.shape[0]
     cols = rhs.shape[1]
     depth = lhs.shape[1]
+    probe_rows = probes_t.shape[1]
     grid = (rows // rows_tile, cols // cols_tile)
     return pl.pallas_call(
-        functools.partial(matern_kernel, sub=sub),
-        out_shape=jax.ShapeDtypeStruct((probes.shape[0], rows), jnp.float32),
+        functools.partial(matern_kernel, rows_sub=rows_sub, cols_sub=cols_sub),
+        out_shape=jax.ShapeDtypeStruct((rows, probe_rows), jnp.float32),
         grid=grid,
         in_specs=[
             pl.BlockSpec((rows_tile, depth), lambda i, j: (i, 0)),
             pl.BlockSpec((rows_tile, 1), lambda i, j: (i, 0)),
             pl.BlockSpec((depth, cols_tile), lambda i, j: (0, j)),
             pl.BlockSpec((1, cols_tile), lambda i, j: (0, j)),
-            pl.BlockSpec((probes.shape[0], cols_tile), lambda i, j: (0, j)),
+            pl.BlockSpec((cols_tile, probe_rows), lambda i, j: (j, 0)),
         ],
-        out_specs=pl.BlockSpec((probes.shape[0], rows_tile), lambda i, j: (0, i)),
+        out_specs=pl.BlockSpec((rows_tile, probe_rows), lambda i, j: (i, 0)),
         cost_estimate=pl.CostEstimate(
-            flops=2 * rows * cols * (depth + probes.shape[0]) + 12 * rows * cols,
+            flops=2 * rows * cols * (depth + probe_rows) + 12 * rows * cols,
             transcendentals=2 * rows * cols,
-            bytes_accessed=2 * (rows * depth + cols * depth) + 4 * rows * 8,
+            bytes_accessed=2 * (rows * depth + cols * depth) + 4 * rows * probe_rows,
         ),
-    )(lhs, lsq, rhs, rsq, probes)
+    )(lhs, lsq, rhs, rsq, probes_t)
 
 
 def gather_peers(block, axis, peers):
@@ -114,9 +125,9 @@
     lhs = jnp.concatenate([row_feats, row_feats], axis=0).T
     acc = matern_probes(
         lhs, row_sq5[:, None], minus_ten(col_feats), five_sq_norm(col_feats)[None, :],
-        piece[feat_dim:],
+        piece[feat_dim:].T,
     )
-    parts = jnp.transpose(acc.reshape(probe_rows, col_peers, local), (1, 0, 2))
+    parts = jnp.transpose(acc.reshape(col_peers, local, probe_rows), (0, 2, 1))
     summed = lax.all_to_all(parts, "col", 0, 0, tiled=False)
     return jnp.sum(summed, axis=0)
 

time: 138 us -> 220 us (1.59)
  Pallas kernels: 52.6 us -> 132 us
  local copies, waits for them, and re-layouts: 13.9 us -> 16.1 us
    pallas_call x1, Pallas kernels: 52.6 us -> 132 us  [matern_probes(): pl.pallas_call(functools.partial(matern_kernel, rows_sub=rows_sub, cols_s...]
  transfers between devices with their start and end apart: 2 -> 2, of which waited for: 1 -> 1; matrix products, arithmetic and copies ran while one was open for 5% -> 3% of each run, Pallas kernels for 0% -> 0%
where the time goes in v6:
time: 220 us; the launch traced here: 219 us
  Pallas kernels  132 us (60%)
  blocking collectives  29.8 us (14%)
  waiting for transfers between devices  19.5 us (9%)
  local copies, waits for them, and re-layouts  16.1 us (7%)
  starting transfers between devices  14.8 us (7%)
  other arithmetic  4.41 us (2%)
    pallas_call x1, Pallas kernels, matern_probes(): pl.pallas_call(functools.partial(matern_kernel, rows_sub=rows_sub, cols_s...  132 us
    all_to_all x1, blocking collectives, on_device(): summed = lax.all_to_all(parts, 'col', 0, 0, tiled=False)  29.8 us
    all_to_all x1, waiting for transfers between devices, gather_peers(): arrived = lax.all_to_all(spread, axis, 0, 0, tiled=False)  19.5 us
    all_to_all x1, starting transfers between devices, gather_peers(): arrived = lax.all_to_all(spread, axis, 0, 0, tiled=False)  11.4 us
    mul x2, local copies, waits for them, and re-layouts, five_sq_norm(): return 5.0 * jnp.sum(wide * wide, axis=0)  4.61 us
  transfers between devices with their start and end apart: 2, of which 1 were waited for; matrix products, arithmetic and copies ran while one was open for 3% of the time, Pallas kernels for 0%

profile of v6, /device:TPU:1, one launch (start us, length us, event | category | flops | bytes accessed | tf_op | source)
XLA Modules:
  0.0 218.9 jit_solution(15821763776075006166)
XLA Ops:
  0.0 0.0 copy-start
  0.0 0.0 copy-start.3
  0.0 0.0 copy-start.2
  0.0 1.6 copy-done
  1.6 0.0 copy-start.1
  1.6 1.6 fusion.1
  3.2 0.0 copy-done.3
  3.2 0.0 copy-done.2
  3.2 0.2 fusion.3
  3.4 0.0 copy-done.1
  3.5 0.9 broadcast_in_dim.2
  4.3 11.4 %all-to-all-start = ((bf16[32,40,160]{2,1,0:T(8,128)(2,1)}), bf16[32,40,160]{2,1,0:T(8,128)(2,1)S(1)}, u32[]{:S(2)}, u32[]{:S(2)}) async-start(bf16[32,40,160]{2,1,0:T(8,128)(2,1)} %broadcast_in_dim.2), calls=%async_computation | async-start | bytes 1310720 | tf_op jit(solution)/shard_map/all_to_all | solution.py:89
  15.7 19.5 %all-to-all-done = bf16[32,40,160]{2,1,0:T(8,128)(2,1)S(1)} async-done(((bf16[32,40,160]{2,1,0:T(8,128)(2,1)}), bf16[32,40,160]{2,1,0:T(8,128)(2,1)S(1)}, u32[]{:S(2)}, u32[]{:S(2)}) %all-to-all-start) | async-done | bytes 409632 | tf_op jit(solution)/shard_map/all_to_all | solution.py:89
  35.3 0.2 multiply_reduce_fusion
  35.4 0.9 slice.16
  36.3 0.1 copy.19
  36.4 1.0 reshape.32
  37.4 0.7 constant_dynamic-slice_fusion
  38.1 3.4 %collective-permute-start = (bf16[40,2560]{1,0:T(8,128)(2,1)}, bf16[40,2560]{1,0:T(8,128)(2,1)}, u32[]{:S(2)}, u32[]{:S(2)}) collective-permute-start(bf16[40,2560]{1,0:T(8,128)(2,1)} %constant_dynamic-slice_fusion), channel_id=1, source_target_pairs={{0,0},{1,1},{2,482},{3,483},{4,452},{5,453},{6,422},{7,423},{8,392... | collective-permute-start | bytes 614408 | tf_op jit(solution)/shard_map/ppermute | solution.py:120
  41.5 1.6 copy.18
  43.1 1.8 maximum_bitcast_fusion.lhs_ref
  45.0 4.0 %mul.59.lsq_ref = f32[5120,1]{1,0:T(8,128)} reshape(f32[32,160]{1,0:T(8,128)S(1)} %broadcast_multiply_fusion) | data formatting | bytes 40960 | tf_op jit(solution)/shard_map/mul | solution.py:18
  49.0 0.0 collective-permute-done
  49.0 1.0 fusion.4
  50.0 0.6 mul.58.rsq_ref
  50.6 0.8 slice.18
  51.4 1.1 copy.20
  52.5 0.8 pad_maximum_fusion.rhs_ref
  53.2 132.5 %shard_map.64 = f32[5120,8]{1,0:T(8,128)} custom-call(bf16[5120,64]{1,0:T(8,128)(2,1)} %maximum_bitcast_fusion.lhs_ref, f32[5120,1]{1,0:T(8,128)} %mul.59.lsq_ref, bf16[64,2560]{1,0:T(8,128)(2,1)} %pad_maximum_fusion.rhs_ref, f32[1,2560]{1,0:T(1,128)} %mul.58.rsq_ref, bf16[2560,8]{1,0:T(8,128)(2,1)} %bitcast.20), custom_call_target="tpu_custom_call" | custom-call | flops 2044723200 | bytes 1146880 | tf_op jit(solution)/shard_map/pallas_call | solution.py:67
  185.7 2.8 %copy.22 = f32[32,160,8]{1,2,0:T(8,128)S(1)} copy(f32[32,160,8]{2,1,0:T(8,128)} %bitcast.18) | data formatting | bytes 327680 | tf_op jit(solution)/shard_map/reshape | solution.py:130
  188.5 29.8 %all_to_all.10 = f32[32,8,160]{2,1,0:T(8,128)S(1)} all-to-all(f32[32,8,160]{2,1,0:T(8,128)S(1)} %bitcast.19), channel_id=1, replica_groups=mesh['row'=16,'col'=32] {'col'}, dimensions={0} | all-to-all | bytes 327680 | tf_op jit(solution)/shard_map/all_to_all | solution.py:131
  218.3 0.6 reduce_sum.29
  (3 shorter events, 0.0 us)
Async XLA Ops:
  0.0 1.6 copy-start
  0.0 3.2 %copy-start.3 = (f32[32]{0:T(128)S(1)}, f32[32]{0:T(128)}, u32[]{:S(2)}) copy-start(f32[32]{0:T(128)} %param.10) | copy-start | bytes 388
  0.0 3.2 %copy-start.2 = (bf16[1024,32]{0,1:T(8,128)(2,1)S(1)}, bf16[1024,32]{0,1:T(8,128)(2,1)}, u32[]{:S(2)}) copy-start(bf16[1024,32]{0,1:T(8,128)(2,1)} %param.9) | copy-start | bytes 196612
  1.6 1.8 copy-start.1
  4.3 30.9 %all-to-all-start = ((bf16[32,40,160]{2,1,0:T(8,128)(2,1)}), bf16[32,40,160]{2,1,0:T(8,128)(2,1)S(1)}, u32[]{:S(2)}, u32[]{:S(2)}) async-start(bf16[32,40,160]{2,1,0:T(8,128)(2,1)} %broadcast_in_dim.2), calls=%async_computation | async-start | bytes 1310720 | tf_op jit(solution)/shard_map/all_to_all | solution.py:89
  38.1 10.8 %collective-permute-start = (bf16[40,2560]{1,0:T(8,128)(2,1)}, bf16[40,2560]{1,0:T(8,128)(2,1)}, u32[]{:S(2)}, u32[]{:S(2)}) collective-permute-start(bf16[40,2560]{1,0:T(8,128)(2,1)} %constant_dynamic-slice_fusion), channel_id=1, source_target_pairs={{0,0},{1,1},{2,482},{3,483},{4,452},{5,453},{6,422},{7,423},{8,392... | collective-permute-start | bytes 614408 | tf_op jit(solution)/shard_map/ppermute | solution.py:120

commit v7 on v2

--- a/solution.py
+++ b/solution.py
@@ -10,11 +10,30 @@
     )
 
 
-def matern_tile(left_feats, left_sq, right_feats):
-    cross_term = dot_f32(left_feats, right_feats, ((0,), (0,)))
-    right_wide = right_feats.astype(jnp.float32)
-    right_sq = jnp.sum(right_wide * right_wide, axis=0)
-    dist_sq = jnp.maximum(left_sq[:, None] + right_sq[None, :] - 2.0 * cross_term, 0.0)
+def split_three(value):
+    high = lax.reduce_precision(value, exponent_bits=8, mantissa_bits=7)
+    rest = value - high
+    middle = lax.reduce_precision(rest, exponent_bits=8, mantissa_bits=7)
+    low = rest - middle
+    return jnp.stack([high, middle, low]).astype(jnp.bfloat16)
+
+
+def augmented(feats):
+    wide = feats.astype(jnp.float32)
+    sq_norm = jnp.sum(wide * wide, axis=0)
+    ones = jnp.ones((3, feats.shape[1]), jnp.bfloat16)
+    return jnp.concatenate([feats, split_three(sq_norm), ones], axis=0)
+
+
+def column_side(side, feat_dim):
+    doubled = (side[:feat_dim].astype(jnp.float32) * -2.0).astype(jnp.bfloat16)
+    return jnp.concatenate(
+        [doubled, side[feat_dim + 3:feat_dim + 6], side[feat_dim:feat_dim + 3]], axis=0
+    )
+
+
+def matern_tile(left_side, right_side):
+    dist_sq = jnp.maximum(dot_f32(left_side, right_side, ((0,), (0,))), 0.0)
     scaled_dist = jnp.sqrt(5.0 * dist_sq)
     values = (1.0 + scaled_dist + scaled_dist * scaled_dist / 3.0) * jnp.exp(-scaled_dist)
     return values.astype(jnp.bfloat16)
@@ -27,15 +46,15 @@
     return jnp.transpose(arrived, (1, 0, 2)).reshape(rows, peers * block.shape[1])
 
 
-def fold_columns(row_feats, row_sq, feats, probes, acc, block_cols):
+def fold_columns(left_side, right_side, probes, acc, block_cols):
     def advance(position, row_acc):
         column_start = position * block_cols
-        feats_block = lax.dynamic_slice_in_dim(feats, column_start, block_cols, 1)
+        side_block = lax.dynamic_slice_in_dim(right_side, column_start, block_cols, 1)
         probes_block = lax.dynamic_slice_in_dim(probes, column_start, block_cols, 1)
-        kernel_tile = matern_tile(row_feats, row_sq, feats_block)
+        kernel_tile = matern_tile(left_side, side_block)
         return row_acc + dot_f32(probes_block, kernel_tile, ((1,), (1,)))
 
-    return lax.fori_loop(0, feats.shape[1] // block_cols, advance, acc)
+    return lax.fori_loop(0, right_side.shape[1] // block_cols, advance, acc)
 
 
 def on_device(points, w_in, w_mid, w_out, lengthscale, probes):
@@ -48,11 +67,11 @@
     local = scaled.shape[1]
     feat_dim = scaled.shape[0]
     probe_rows = probes.shape[0]
-    joined = jnp.concatenate([scaled, probes], axis=0)
+    side = augmented(scaled)
+    side_rows = side.shape[0]
+    joined = jnp.concatenate([side, probes], axis=0)
     block = gather_peers(joined, "col", col_peers)
-    row_feats = block[:feat_dim]
-    row_wide = row_feats.astype(jnp.float32)
-    row_sq = jnp.sum(row_wide * row_wide, axis=0)
+    left_side = block[:side_rows]
     halves = col_peers // row_peers
     span = block.shape[1] // halves
     col = lax.axis_index("col")
@@ -70,7 +89,8 @@
     ]
     acc = jnp.zeros((probe_rows, block.shape[1]), jnp.float32)
     for piece in arrived:
-        acc = fold_columns(row_feats, row_sq, piece[:feat_dim], piece[feat_dim:], acc, 256)
+        right_side = column_side(piece[:side_rows], feat_dim)
+        acc = fold_columns(left_side, right_side, piece[side_rows:], acc, 256)
     parts = jnp.transpose(acc.reshape(probe_rows, col_peers, local), (1, 0, 2))
     summed = lax.all_to_all(parts, "col", 0, 0, tiled=False)
     return jnp.sum(summed, axis=0)

time: 113 us -> 114 us (level)
  matrix products: 39.2 us -> 35.7 us
  waiting for transfers between devices: 19.5 us -> 22.3 us
  starting transfers between devices: 12.7 us -> 14.5 us
    dot_general x12, matrix products: 39.2 us -> 35.7 us  [dot_f32(): lax.dot_general(left, right, (dims, ((), ())), preferred_element_type=jnp...]
    all_to_all x1, waiting for transfers between devices: 19.5 us -> 22.3 us  [gather_peers(): arrived = lax.all_to_all(spread, axis, 0, 0, tiled=False)]
    ppermute x2, starting transfers between devices: 1.33 us -> 3.11 us  [on_device(): lax.ppermute(mine[:, k * width:(k + 1) * width], ('row', 'col'), pairs)]
    slice x7, local copies, waits for them, and re-layouts: 2.95 us -> 1.2 us  [the longest x3 1.15 us: on_device(): left_side = block[:side_rows]]
  transfers between devices with their start and end apart: 3 -> 3, of which waited for: 1 -> 1; matrix products, arithmetic and copies ran while one was open for 19% -> 16% of each run, Pallas kernels for 0% -> 0%
where the time goes in v7:
time: 114 us; the launch traced here: 113 us
  matrix products  35.7 us (31%)
  blocking collectives  31.7 us (28%)
  waiting for transfers between devices  22.3 us (20%)
  starting transfers between devices  14.5 us (13%)
  local copies, waits for them, and re-layouts  8.28 us (7%)
    dot_general x12, matrix products, dot_f32(): lax.dot_general(left, right, (dims, ((), ())), preferred_element_type=jnp...  35.7 us
    all_to_all x1, blocking collectives, on_device(): summed = lax.all_to_all(parts, 'col', 0, 0, tiled=False)  31.7 us
    all_to_all x1, waiting for transfers between devices, gather_peers(): arrived = lax.all_to_all(spread, axis, 0, 0, tiled=False)  22.3 us
    all_to_all x1, starting transfers between devices, gather_peers(): arrived = lax.all_to_all(spread, axis, 0, 0, tiled=False)  11.4 us
    ppermute x2, starting transfers between devices, on_device(): lax.ppermute(mine[:, k * width:(k + 1) * width], ('row', 'col'), pairs)  3.11 us
    reshape x1, local copies, waits for them, and re-layouts, gather_peers(): jnp.transpose(arrived, (1, 0, 2)).reshape(rows, peers * block.shape[1])  2.31 us
  transfers between devices with their start and end apart: 3, of which 1 were waited for; matrix products, arithmetic and copies ran while one was open for 16% of the time, Pallas kernels for 0%

profile of v7, /device:TPU:1, one launch (start us, length us, event | category | flops | bytes accessed | tf_op | source)
XLA Modules:
  0.0 113.4 jit_solution(14938394501390630671)
XLA Ops:
  0.0 1.6 %copy-done = bf16[1024,1024]{1,0:T(8,128)(2,1)S(1)} copy-done((bf16[1024,1024]{1,0:T(8,128)(2,1)S(1)}, bf16[1024,1024]{1,0:T(8,128)(2,1)}, u32[]{:S(2)}) %copy-start) | copy-done | bytes 2097176
  1.6 1.6 %fusion.23 = bf16[160,1024]{1,0:T(8,128)(2,1)S(1)} fusion(bf16[1024,1024]{1,0:T(8,128)(2,1)S(1)} %copy-done, bf16[160,128]{1,0:T(8,128)(2,1)} %param.10, bf16[128,1024]{1,0:T(8,128)(2,1)} %param.11), kind=kOutput, calls=%fused_computation.27 | convolution fusion | flops 378142720 | bytes 2727936 | tf_op jit(solution)/shard_map/dot_general | solution.py:8
  3.2 0.2 multiply_reduce_fusion
  3.5 0.1 concatenate.10
  3.6 0.9 broadcast_in_dim.15
  4.5 11.4 %all-to-all-start = ((bf16[32,46,160]{2,1,0:T(8,128)(2,1)}), bf16[32,46,160]{2,1,0:T(8,128)(2,1)S(1)}, u32[]{:S(2)}, u32[]{:S(2)}) async-start(bf16[32,46,160]{2,1,0:T(8,128)(2,1)} %broadcast_in_dim.15), calls=%async_computation | async-start | bytes 1572864 | tf_op jit(solution)/shard_map/all_to_all | solution.py:44
  15.9 22.3 %all-to-all-done = bf16[32,46,160]{2,1,0:T(8,128)(2,1)S(1)} async-done(((bf16[32,46,160]{2,1,0:T(8,128)(2,1)}), bf16[32,46,160]{2,1,0:T(8,128)(2,1)S(1)}, u32[]{:S(2)}, u32[]{:S(2)}) %all-to-all-start) | async-done | bytes 471072 | tf_op jit(solution)/shard_map/all_to_all | solution.py:44
  38.2 1.1 copy.7
  39.3 2.3 %reshape.33 = bf16[46,5120]{1,0:T(8,128)(2,1)S(1)} reshape(bf16[46,32,160]{2,1,0:T(8,128)(2,1)} %copy.7) | data formatting | bytes 942080 | tf_op jit(solution)/shard_map/reshape | solution.py:46
  41.7 0.7 constant_dynamic-slice_fusion.1
  42.4 1.5 %collective-permute-start = (bf16[46,1280]{1,0:T(8,128)(2,1)}, bf16[46,1280]{1,0:T(8,128)(2,1)S(1)}, u32[]{:S(2)}, u32[]{:S(2)}) collective-permute-start(bf16[46,1280]{1,0:T(8,128)(2,1)} %get-tuple-element.234), channel_id=1, source_target_pairs={{0,0},{1,1},{2,482},{3,483},{4,452},{5,453},{6,422},{7,423},{8,392... | collective-permute-start | bytes 353288 | tf_op jit(solution)/shard_map/ppermute | solution.py:87
  44.0 1.6 %collective-permute-start.1 = (bf16[46,1280]{1,0:T(8,128)(2,1)}, bf16[46,1280]{1,0:T(8,128)(2,1)S(1)}, u32[]{:S(2)}, u32[]{:S(2)}) collective-permute-start(bf16[46,1280]{1,0:T(8,128)(2,1)} %get-tuple-element.233), channel_id=1, source_target_pairs={{0,0},{1,1},{2,482},{3,483},{4,452},{5,453},{6,422},{7,423},{8,392... | collective-permute-start | bytes 353288 | tf_op jit(solution)/shard_map/ppermute | solution.py:87
  45.5 0.1 copy.8
  45.7 1.0 slice.50
  46.7 0.0 collective-permute-done
  46.8 16.9 %while.28 = (s32[]{:T(128)}, f32[8,5120]{1,0:T(8,128)S(1)}, bf16[8,1280]{1,0:T(8,128)(2,1)S(1)}, bf16[38,1280]{1,0:T(8,128)(2,1)S(1)}, bf16[38,5120]{1,0:T(8,128...) while((s32[]{:T(128)}, f32[8,5120]{1,0:T(8,128)S(1)}, ...), condition=%wide.region_2.3_spmd.clone, body=%wide.region_1.2_spmd.clone.sunk | while | flops 132464648 | bytes 763540 | solution.py:57
  46.8 3.4 %convolution_add_fusion.5 = f32[8,5120]{1,0:T(8,128)S(1)} fusion(bf16[38,5120]{1,0:T(8,128)(2,1)S(1)} %get-tuple-element.328, f32[8,5120]{1,0:T(8,128)S(1)} %get-tuple-element.316, pred[]{:T(512)S(6)} %compare.4, bf16[38,1280]{1,0:T(8,128)(2,1)S(1)} %get-tuple-element.327, s32[]{:T(128)S(6)} %select_n.32, bf16[8,1280]{1,0:T(8,128)(2,1)S(1)} %get-tuple-element.326), kind=kOutput, calls=%fused_computation.15.clone.1 | convolution fusion | flops 132464640 | bytes 763392 | tf_op jit(solution)/shard_map/while/body/eval_jaxpr/dot_general | solution.py:8
  50.2 3.4 %convolution_add_fusion.5 = f32[8,5120]{1,0:T(8,128)S(1)} fusion(bf16[38,5120]{1,0:T(8,128)(2,1)S(1)} %get-tuple-element.328, f32[8,5120]{1,0:T(8,128)S(1)} %get-tuple-element.316, pred[]{:T(512)S(6)} %compare.4, bf16[38,1280]{1,0:T(8,128)(2,1)S(1)} %get-tuple-element.327, s32[]{:T(128)S(6)} %select_n.32, bf16[8,1280]{1,0:T(8,128)(2,1)S(1)} %get-tuple-element.326), kind=kOutput, calls=%fused_computation.15.clone.1 | convolution fusion | flops 132464640 | bytes 763392 | tf_op jit(solution)/shard_map/while/body/eval_jaxpr/dot_general | solution.py:8
  53.5 3.4 %convolution_add_fusion.5 = f32[8,5120]{1,0:T(8,128)S(1)} fusion(bf16[38,5120]{1,0:T(8,128)(2,1)S(1)} %get-tuple-element.328, f32[8,5120]{1,0:T(8,128)S(1)} %get-tuple-element.316, pred[]{:T(512)S(6)} %compare.4, bf16[38,1280]{1,0:T(8,128)(2,1)S(1)} %get-tuple-element.327, s32[]{:T(128)S(6)} %select_n.32, bf16[8,1280]{1,0:T(8,128)(2,1)S(1)} %get-tuple-element.326), kind=kOutput, calls=%fused_computation.15.clone.1 | convolution fusion | flops 132464640 | bytes 763392 | tf_op jit(solution)/shard_map/while/body/eval_jaxpr/dot_general | solution.py:8
  56.9 3.4 %convolution_add_fusion.5 = f32[8,5120]{1,0:T(8,128)S(1)} fusion(bf16[38,5120]{1,0:T(8,128)(2,1)S(1)} %get-tuple-element.328, f32[8,5120]{1,0:T(8,128)S(1)} %get-tuple-element.316, pred[]{:T(512)S(6)} %compare.4, bf16[38,1280]{1,0:T(8,128)(2,1)S(1)} %get-tuple-element.327, s32[]{:T(128)S(6)} %select_n.32, bf16[8,1280]{1,0:T(8,128)(2,1)S(1)} %get-tuple-element.326), kind=kOutput, calls=%fused_computation.15.clone.1 | convolution fusion | flops 132464640 | bytes 763392 | tf_op jit(solution)/shard_map/while/body/eval_jaxpr/dot_general | solution.py:8
  60.3 3.4 %convolution_add_fusion.5 = f32[8,5120]{1,0:T(8,128)S(1)} fusion(bf16[38,5120]{1,0:T(8,128)(2,1)S(1)} %get-tuple-element.328, f32[8,5120]{1,0:T(8,128)S(1)} %get-tuple-element.316, pred[]{:T(512)S(6)} %compare.4, bf16[38,1280]{1,0:T(8,128)(2,1)S(1)} %get-tuple-element.327, s32[]{:T(128)S(6)} %select_n.32, bf16[8,1280]{1,0:T(8,128)(2,1)S(1)} %get-tuple-element.326), kind=kOutput, calls=%fused_computation.15.clone.1 | convolution fusion | flops 132464640 | bytes 763392 | tf_op jit(solution)/shard_map/while/body/eval_jaxpr/dot_general | solution.py:8
  63.7 0.0 collective-permute-done.1
  63.8 16.9 %while.27 = (s32[]{:T(128)}, f32[8,5120]{1,0:T(8,128)S(1)}, bf16[8,1280]{1,0:T(8,128)(2,1)S(1)}, bf16[38,1280]{1,0:T(8,128)(2,1)S(1)}, bf16[38,5120]{1,0:T(8,128...) while((s32[]{:T(128)}, f32[8,5120]{1,0:T(8,128)S(1)}, bf16[8,1280]{1,0:T(8,128)(2,1)S(1)}, ...), condition=%wide.region_4.5_spmd, body=%wide.region_3.4_spmd.sunk | while | flops 132423688 | bytes 763019 | solution.py:57
  63.8 3.4 %convolution_add_fusion.4 = f32[8,5120]{1,0:T(8,128)S(1)} fusion(f32[8,5120]{1,0:T(8,128)S(1)} %get-tuple-element.343, bf16[38,5120]{1,0:T(8,128)(2,1)S(1)} %get-tuple-element.355, bf16[38,1280]{1,0:T(8,128)(2,1)S(1)} %get-tuple-element.354, s32[]{:T(128)S(6)} %select_n.31, bf16[8,1280]{1,0:T(8,128)(2,1)S(1)} %get-tuple-element.353), kind=kOutput, calls=%fused_computation.3.clone.1 | convolution fusion | flops 132423680 | bytes 762880 | tf_op jit(solution)/shard_map/while/body/eval_jaxpr/dot_general | solution.py:8
  67.2 3.4 %convolution_add_fusion.4 = f32[8,5120]{1,0:T(8,128)S(1)} fusion(f32[8,5120]{1,0:T(8,128)S(1)} %get-tuple-element.343, bf16[38,5120]{1,0:T(8,128)(2,1)S(1)} %get-tuple-element.355, bf16[38,1280]{1,0:T(8,128)(2,1)S(1)} %get-tuple-element.354, s32[]{:T(128)S(6)} %select_n.31, bf16[8,1280]{1,0:T(8,128)(2,1)S(1)} %get-tuple-element.353), kind=kOutput, calls=%fused_computation.3.clone.1 | convolution fusion | flops 132423680 | bytes 762880 | tf_op jit(solution)/shard_map/while/body/eval_jaxpr/dot_general | solution.py:8
  70.6 3.4 %convolution_add_fusion.4 = f32[8,5120]{1,0:T(8,128)S(1)} fusion(f32[8,5120]{1,0:T(8,128)S(1)} %get-tuple-element.343, bf16[38,5120]{1,0:T(8,128)(2,1)S(1)} %get-tuple-element.355, bf16[38,1280]{1,0:T(8,128)(2,1)S(1)} %get-tuple-element.354, s32[]{:T(128)S(6)} %select_n.31, bf16[8,1280]{1,0:T(8,128)(2,1)S(1)} %get-tuple-element.353), kind=kOutput, calls=%fused_computation.3.clone.1 | convolution fusion | flops 132423680 | bytes 762880 | tf_op jit(solution)/shard_map/while/body/eval_jaxpr/dot_general | solution.py:8
  74.0 3.4 %convolution_add_fusion.4 = f32[8,5120]{1,0:T(8,128)S(1)} fusion(f32[8,5120]{1,0:T(8,128)S(1)} %get-tuple-element.343, bf16[38,5120]{1,0:T(8,128)(2,1)S(1)} %get-tuple-element.355, bf16[38,1280]{1,0:T(8,128)(2,1)S(1)} %get-tuple-element.354, s32[]{:T(128)S(6)} %select_n.31, bf16[8,1280]{1,0:T(8,128)(2,1)S(1)} %get-tuple-element.353), kind=kOutput, calls=%fused_computation.3.clone.1 | convolution fusion | flops 132423680 | bytes 762880 | tf_op jit(solution)/shard_map/while/body/eval_jaxpr/dot_general | solution.py:8
  77.3 3.4 %convolution_add_fusion.4 = f32[8,5120]{1,0:T(8,128)S(1)} fusion(f32[8,5120]{1,0:T(8,128)S(1)} %get-tuple-element.343, bf16[38,5120]{1,0:T(8,128)(2,1)S(1)} %get-tuple-element.355, bf16[38,1280]{1,0:T(8,128)(2,1)S(1)} %get-tuple-element.354, s32[]{:T(128)S(6)} %select_n.31, bf16[8,1280]{1,0:T(8,128)(2,1)S(1)} %get-tuple-element.353), kind=kOutput, calls=%fused_computation.3.clone.1 | convolution fusion | flops 132423680 | bytes 762880 | tf_op jit(solution)/shard_map/while/body/eval_jaxpr/dot_general | solution.py:8
  80.7 0.1 reshape.34
  80.9 0.2 copy.9
  81.0 31.7 %all_to_all.10 = f32[32,8,160]{2,1,0:T(8,128)S(1)} all-to-all(f32[32,8,160]{2,1,0:T(8,128)S(1)} %copy.9), channel_id=1, replica_groups=mesh['row'=16,'col'=32] {'col'}, dimensions={0} | all-to-all | bytes 327680 | tf_op jit(solution)/shard_map/all_to_all | solution.py:95
  112.7 0.6 reduce_sum.22
  (19 shorter events, 0.2 us)
Async XLA Ops:
  0.0 1.6 %copy-start = (bf16[1024,1024]{1,0:T(8,128)(2,1)S(1)}, bf16[1024,1024]{1,0:T(8,128)(2,1)}, u32[]{:S(2)}) copy-start(bf16[1024,1024]{1,0:T(8,128)(2,1)} %param.12) | copy-start | bytes 6291460
  0.0 3.2 %copy-start.2 = (bf16[1024,32]{0,1:T(8,128)(2,1)S(1)}, bf16[1024,32]{0,1:T(8,128)(2,1)}, u32[]{:S(2)}) copy-start(bf16[1024,32]{0,1:T(8,128)(2,1)} %param.13) | copy-start | bytes 196612
  0.0 3.2 %copy-start.3 = (f32[32]{0:T(128)S(1)}, f32[32]{0:T(128)}, u32[]{:S(2)}) copy-start(f32[32]{0:T(128)} %param.14) | copy-start | bytes 388
  1.6 1.9 %copy-start.1 = (bf16[8,160]{1,0:T(8,128)(2,1)S(1)}, bf16[8,160]{1,0:T(8,128)(2,1)}, u32[]{:S(2)}) copy-start(bf16[8,160]{1,0:T(8,128)(2,1)} %param.15) | copy-start | bytes 7684
  4.5 33.7 %all-to-all-start = ((bf16[32,46,160]{2,1,0:T(8,128)(2,1)}), bf16[32,46,160]{2,1,0:T(8,128)(2,1)S(1)}, u32[]{:S(2)}, u32[]{:S(2)}) async-start(bf16[32,46,160]{2,1,0:T(8,128)(2,1)} %broadcast_in_dim.15), calls=%async_computation | async-start | bytes 1572864 | tf_op jit(solution)/shard_map/all_to_all | solution.py:44
  42.4 4.3 %collective-permute-start = (bf16[46,1280]{1,0:T(8,128)(2,1)}, bf16[46,1280]{1,0:T(8,128)(2,1)S(1)}, u32[]{:S(2)}, u32[]{:S(2)}) collective-permute-start(bf16[46,1280]{1,0:T(8,128)(2,1)} %get-tuple-element.234), channel_id=1, source_target_pairs={{0,0},{1,1},{2,482},{3,483},{4,452},{5,453},{6,422},{7,423},{8,392... | collective-permute-start | bytes 353288 | tf_op jit(solution)/shard_map/ppermute | solution.py:87
  44.0 19.7 %collective-permute-start.1 = (bf16[46,1280]{1,0:T(8,128)(2,1)}, bf16[46,1280]{1,0:T(8,128)(2,1)S(1)}, u32[]{:S(2)}, u32[]{:S(2)}) collective-permute-start(bf16[46,1280]{1,0:T(8,128)(2,1)} %get-tuple-element.233), channel_id=1, source_target_pairs={{0,0},{1,1},{2,482},{3,483},{4,452},{5,453},{6,422},{7,423},{8,392... | collective-permute-start | bytes 353288 | tf_op jit(solution)/shard_map/ppermute | solution.py:87

commit v8 on v2

--- a/solution.py
+++ b/solution.py
@@ -10,11 +10,9 @@
     )
 
 
-def matern_tile(left_feats, left_sq, right_feats):
-    cross_term = dot_f32(left_feats, right_feats, ((0,), (0,)))
-    right_wide = right_feats.astype(jnp.float32)
-    right_sq = jnp.sum(right_wide * right_wide, axis=0)
-    dist_sq = jnp.maximum(left_sq[:, None] + right_sq[None, :] - 2.0 * cross_term, 0.0)
+def matern_tile(left_feats, left_sq, right_doubled, right_sq):
+    cross_term = dot_f32(left_feats, right_doubled, ((0,), (0,)))
+    dist_sq = jnp.maximum(left_sq[:, None] + right_sq[None, :] + cross_term, 0.0)
     scaled_dist = jnp.sqrt(5.0 * dist_sq)
     values = (1.0 + scaled_dist + scaled_dist * scaled_dist / 3.0) * jnp.exp(-scaled_dist)
     return values.astype(jnp.bfloat16)
@@ -28,11 +26,16 @@
 
 
 def fold_columns(row_feats, row_sq, feats, probes, acc, block_cols):
+    wide = feats.astype(jnp.float32)
+    sq_norm = jnp.sum(wide * wide, axis=0)
+    doubled = (wide * -2.0).astype(jnp.bfloat16)
+
     def advance(position, row_acc):
         column_start = position * block_cols
-        feats_block = lax.dynamic_slice_in_dim(feats, column_start, block_cols, 1)
+        feats_block = lax.dynamic_slice_in_dim(doubled, column_start, block_cols, 1)
+        sq_block = lax.dynamic_slice_in_dim(sq_norm, column_start, block_cols, 0)
         probes_block = lax.dynamic_slice_in_dim(probes, column_start, block_cols, 1)
-        kernel_tile = matern_tile(row_feats, row_sq, feats_block)
+        kernel_tile = matern_tile(row_feats, row_sq, feats_block, sq_block)
         return row_acc + dot_f32(probes_block, kernel_tile, ((1,), (1,)))
 
     return lax.fori_loop(0, feats.shape[1] // block_cols, advance, acc)
@@ -70,7 +73,7 @@
     ]
     acc = jnp.zeros((probe_rows, block.shape[1]), jnp.float32)
     for piece in arrived:
-        acc = fold_columns(row_feats, row_sq, piece[:feat_dim], piece[feat_dim:], acc, 256)
+        acc = fold_columns(row_feats, row_sq, piece[:feat_dim], piece[feat_dim:], acc, 640)
     parts = jnp.transpose(acc.reshape(probe_rows, col_peers, local), (1, 0, 2))
     summed = lax.all_to_all(parts, "col", 0, 0, tiled=False)
     return jnp.sum(summed, axis=0)

time: 113 us -> 110 us (0.973)
  matrix products: 39.2 us -> 35.9 us
    dot_general x12 -> x6, matrix products: 39.2 us -> 35.9 us  [dot_f32(): lax.dot_general(left, right, (dims, ((), ())), preferred_element_type=jnp...]
  transfers between devices with their start and end apart: 3 -> 3, of which waited for: 1 -> 1; matrix products, arithmetic and copies ran while one was open for 19% -> 18% of each run, Pallas kernels for 0% -> 0%
where the time goes in v8:
time: 110 us
  matrix products  35.9 us (33%)
  blocking collectives  30.8 us (28%)
  waiting for transfers between devices  19.5 us (18%)
  starting transfers between devices  12.9 us (12%)
  local copies, waits for them, and re-layouts  8.99 us (8%)
    dot_general x6, matrix products, dot_f32(): lax.dot_general(left, right, (dims, ((), ())), preferred_element_type=jnp...  35.9 us
    all_to_all x1, blocking collectives, on_device(): summed = lax.all_to_all(parts, 'col', 0, 0, tiled=False)  30.8 us
    all_to_all x1, waiting for transfers between devices, gather_peers(): arrived = lax.all_to_all(spread, axis, 0, 0, tiled=False)  19.5 us
    all_to_all x1, starting transfers between devices, gather_peers(): arrived = lax.all_to_all(spread, axis, 0, 0, tiled=False)  11.4 us
    slice x3, local copies, waits for them, and re-layouts, on_device(): row_feats = block[:feat_dim]  2.94 us
  transfers between devices with their start and end apart: 3, of which 1 were waited for; matrix products, arithmetic and copies ran while one was open for 18% of the time, Pallas kernels for 0%

profile of v8, /device:TPU:1, one launch (start us, length us, event | category | flops | bytes accessed | tf_op | source)
XLA Modules:
  0.0 109.5 jit_solution(5332856318225083495)
XLA Ops:
  0.0 1.6 %copy-done = bf16[1024,1024]{1,0:T(8,128)(2,1)S(1)} copy-done((bf16[1024,1024]{1,0:T(8,128)(2,1)S(1)}, bf16[1024,1024]{1,0:T(8,128)(2,1)}, u32[]{:S(2)}) %copy-start) | copy-done | bytes 2097176
  1.6 1.6 %fusion.25 = bf16[160,1024]{1,0:T(8,128)(2,1)S(1)} fusion(bf16[1024,1024]{1,0:T(8,128)(2,1)S(1)} %copy-done, bf16[160,128]{1,0:T(8,128)(2,1)} %param.10, bf16[128,1024]{1,0:T(8,128)(2,1)} %param.11), kind=kOutput, calls=%fused_computation.29 | convolution fusion | flops 378142720 | bytes 2727936 | tf_op jit(solution)/shard_map/dot_general | solution.py:8
  3.2 0.2 fusion.27
  3.4 0.0 copy-done.2
  3.5 0.9 broadcast_in_dim.23
  4.4 11.4 %all-to-all-start = ((bf16[32,40,160]{2,1,0:T(8,128)(2,1)}), bf16[32,40,160]{2,1,0:T(8,128)(2,1)S(1)}, u32[]{:S(2)}, u32[]{:S(2)}) async-start(bf16[32,40,160]{2,1,0:T(8,128)(2,1)} %broadcast_in_dim.23), calls=%async_computation | async-start | bytes 1310720 | tf_op jit(solution)/shard_map/all_to_all | solution.py:23
  15.8 19.5 %all-to-all-done = bf16[32,40,160]{2,1,0:T(8,128)(2,1)S(1)} async-done(((bf16[32,40,160]{2,1,0:T(8,128)(2,1)}), bf16[32,40,160]{2,1,0:T(8,128)(2,1)S(1)}, u32[]{:S(2)}, u32[]{:S(2)}) %all-to-all-start) | async-done | bytes 409632 | tf_op jit(solution)/shard_map/all_to_all | solution.py:23
  35.3 0.1 copy.7
  35.4 0.9 slice.33
  36.3 1.7 %reshape.14 = bf16[40,5120]{1,0:T(8,128)(2,1)} reshape(bf16[40,32,160]{2,1,0:T(8,128)(2,1)S(1)} %copy.7) | data formatting | bytes 819200 | tf_op jit(solution)/shard_map/reshape | solution.py:25
  38.0 1.0 constant_dynamic-slice_fusion.1
  39.0 0.7 collective-permute-start
  39.7 0.2 multiply_reduce_fusion
  39.9 0.1 reduce_sum.39
  40.0 1.3 %copy.8 = bf16[32,32,160]{2,1,0:T(8,128)(2,1)S(1)} copy(bf16[32,32,160]{2,0,1:T(8,128)(2,1)} %slice.33) | data formatting | bytes 655360 | tf_op jit(solution)/shard_map/slice | solution.py:56
  41.3 0.7 slice.28
  42.1 0.8 collective-permute-start.1
  42.9 0.0 collective-permute-done
  43.0 17.2 %while.28 = (s32[]{:T(128)}, f32[8,5120]{1,0:T(8,128)S(1)}, bf16[8,1280]{1,0:T(8,128)(2,1)S(1)}, f32[5120]{0:T(1024)S(1)}, f32[1280]{0:T(1024)S(1)}, /*index=5*/...) while((s32[]{:T(128)}, f32[8,5120]{1,0:T(8,128)S(1)}, ...), condition=%wide.region_3.4_spmd.clone, body=%wide.region_2.3_spmd.clone.sunk | while | flops 298270720 | bytes 737968 | solution.py:41
  43.0 0.1 dynamic_slice.70
  43.1 8.5 %convolution_add_fusion.5 = f32[8,5120]{1,0:T(8,128)S(1)} fusion(bf16[32,5120]{1,0:T(8,128)(2,1)S(1)} %get-tuple-element.427, f32[640]{0:T(1024)S(1)} %dynamic_slice.70, f32[5120]{0:T(1024)S(1)} %get-tuple-element.424, f32[8,5120]{1,0:T(8,128)S(1)} %get-tuple-element.411, pred[]{:T(512)S(6)} %compare.4, ...), kind=kOutput, calls=%fused_computation.18.clone.1 | convolution fusion | flops 298270720 | bytes 732672 | tf_op jit(solution)/shard_map/while/body/eval_jaxpr/dot_general | solution.py:8
  51.6 0.1 dynamic_slice.70
  51.7 8.5 %convolution_add_fusion.5 = f32[8,5120]{1,0:T(8,128)S(1)} fusion(bf16[32,5120]{1,0:T(8,128)(2,1)S(1)} %get-tuple-element.427, f32[640]{0:T(1024)S(1)} %dynamic_slice.70, f32[5120]{0:T(1024)S(1)} %get-tuple-element.424, f32[8,5120]{1,0:T(8,128)S(1)} %get-tuple-element.411, pred[]{:T(512)S(6)} %compare.4, ...), kind=kOutput, calls=%fused_computation.18.clone.1 | convolution fusion | flops 298270720 | bytes 732672 | tf_op jit(solution)/shard_map/while/body/eval_jaxpr/dot_general | solution.py:8
  60.3 17.5 %while.27 = (s32[]{:T(128)}, f32[8,5120]{1,0:T(8,128)S(1)}, bf16[8,1280]{1,0:T(8,128)(2,1)S(1)}, f32[5120]{0:T(1024)S(1)}, f32[1280]{0:T(1024)S(1)}, /*index=5*/...) while((s32[]{:T(128)}, f32[8,5120]{1,0:T(8,128)S(1)}, ...), condition=%wide.region_6.7_spmd, body=%wide.region_5.6_spmd.sunk | while | flops 298229760 | bytes 737447 | solution.py:41
  60.5 0.1 dynamic_slice.67
  60.6 8.5 %convolution_add_fusion.4 = f32[8,5120]{1,0:T(8,128)S(1)} fusion(f32[8,5120]{1,0:T(8,128)S(1)} %get-tuple-element.444, bf16[32,5120]{1,0:T(8,128)(2,1)S(1)} %get-tuple-element.460, f32[640]{0:T(1024)S(1)} %dynamic_slice.67, f32[5120]{0:T(1024)S(1)} %get-tuple-element.457, bf16[32,1280]{1,0:T(8,128)(2,1)S(1)} %get-tuple-element.459, ...), kind=kOutput, calls=%fused_computation.5.clone.1 | convolution fusion | flops 298229760 | bytes 732160 | tf_op jit(solution)/shard_map/while/body/eval_jaxpr/dot_general | solution.py:8
  69.1 0.1 dynamic_slice.67
  69.2 8.5 %convolution_add_fusion.4 = f32[8,5120]{1,0:T(8,128)S(1)} fusion(f32[8,5120]{1,0:T(8,128)S(1)} %get-tuple-element.444, bf16[32,5120]{1,0:T(8,128)(2,1)S(1)} %get-tuple-element.460, f32[640]{0:T(1024)S(1)} %dynamic_slice.67, f32[5120]{0:T(1024)S(1)} %get-tuple-element.457, bf16[32,1280]{1,0:T(8,128)(2,1)S(1)} %get-tuple-element.459, ...), kind=kOutput, calls=%fused_computation.5.clone.1 | convolution fusion | flops 298229760 | bytes 732160 | tf_op jit(solution)/shard_map/while/body/eval_jaxpr/dot_general | solution.py:8
  77.7 0.1 reshape.15
  77.9 0.2 copy.9
  78.0 30.8 %all_to_all.10 = f32[32,8,160]{2,1,0:T(8,128)S(1)} all-to-all(f32[32,8,160]{2,1,0:T(8,128)S(1)} %copy.9), channel_id=1, replica_groups=mesh['row'=16,'col'=32] {'col'}, dimensions={0} | all-to-all | bytes 327680 | tf_op jit(solution)/shard_map/all_to_all | solution.py:78
  108.9 0.6 reduce_sum.42
  (15 shorter events, 0.1 us)
Async XLA Ops:
  0.0 1.6 %copy-start = (bf16[1024,1024]{1,0:T(8,128)(2,1)S(1)}, bf16[1024,1024]{1,0:T(8,128)(2,1)}, u32[]{:S(2)}) copy-start(bf16[1024,1024]{1,0:T(8,128)(2,1)} %param.12) | copy-start | bytes 6291460
  0.0 3.2 %copy-start.3 = (bf16[1024,32]{0,1:T(8,128)(2,1)S(1)}, bf16[1024,32]{0,1:T(8,128)(2,1)}, u32[]{:S(2)}) copy-start(bf16[1024,32]{0,1:T(8,128)(2,1)} %param.13) | copy-start | bytes 196612
  0.0 3.2 %copy-start.4 = (f32[32]{0:T(128)S(1)}, f32[32]{0:T(128)}, u32[]{:S(2)}) copy-start(f32[32]{0:T(128)} %param.14) | copy-start | bytes 388
  1.6 1.9 %copy-start.2 = (bf16[8,160]{1,0:T(8,128)(2,1)S(1)}, bf16[8,160]{1,0:T(8,128)(2,1)}, u32[]{:S(2)}) copy-start(bf16[8,160]{1,0:T(8,128)(2,1)} %param.15) | copy-start | bytes 7684
  4.4 30.9 %all-to-all-start = ((bf16[32,40,160]{2,1,0:T(8,128)(2,1)}), bf16[32,40,160]{2,1,0:T(8,128)(2,1)S(1)}, u32[]{:S(2)}, u32[]{:S(2)}) async-start(bf16[32,40,160]{2,1,0:T(8,128)(2,1)} %broadcast_in_dim.23), calls=%async_computation | async-start | bytes 1310720 | tf_op jit(solution)/shard_map/all_to_all | solution.py:23
  38.0 5.0 %copy-start.1 = (f32[8,5120]{1,0:T(8,128)S(1)}, f32[8,5120]{1,0:T(8,128)}, u32[]{:S(2)}) copy-start(f32[8,5120]{1,0:T(8,128)} %custom-call) | copy-start | bytes 491524
  39.0 3.9 %collective-permute-start = (bf16[40,1280]{1,0:T(8,128)(2,1)S(1)}, bf16[40,1280]{1,0:T(8,128)(2,1)S(1)}, u32[]{:S(2)}, u32[]{:S(2)}) collective-permute-start(bf16[40,1280]{1,0:T(8,128)(2,1)S(1)} %get-tuple-element.308), channel_id=1, source_target_pairs={{0,0},{1,1},{2,482},{3,483},{4,452},{5,453},{6,422},{7,423},{8,392... | collective-permute-start | bytes 307208 | tf_op jit(solution)/shard_map/ppermute | solution.py:71
  42.1 18.2 %collective-permute-start.1 = (bf16[40,1280]{1,0:T(8,128)(2,1)S(1)}, bf16[40,1280]{1,0:T(8,128)(2,1)S(1)}, u32[]{:S(2)}, u32[]{:S(2)}) collective-permute-start(bf16[40,1280]{1,0:T(8,128)(2,1)S(1)} %get-tuple-element.307), channel_id=1, source_target_pairs={{0,0},{1,1},{2,482},{3,483},{4,452},{5,453},{6,422},{7,423},{8,392... | collective-permute-start | bytes 307208 | tf_op jit(solution)/shard_map/ppermute | solution.py:71

commit v9 on v8

--- a/solution.py
+++ b/solution.py
@@ -65,7 +65,7 @@
         for c in range(col_peers):
             target = (r - c // halves) % row_peers
             pairs.append((r * col_peers + c, target * col_peers + c))
-    chunks = 2
+    chunks = 1
     width = span // chunks
     arrived = [
         lax.ppermute(mine[:, k * width:(k + 1) * width], ("row", "col"), pairs)

time: 110 us -> 121 us (1.10)
  blocking collectives: 30.8 us -> 37.5 us
  matrix products: 35.9 us -> 41.3 us
    all_to_all x1, blocking collectives: 30.8 us -> 37.5 us  [on_device(): summed = lax.all_to_all(parts, 'col', 0, 0, tiled=False)]
    dot_general x6, matrix products: 35.9 us -> 41.3 us  [dot_f32(): lax.dot_general(left, right, (dims, ((), ())), preferred_element_type=jnp...]
    slice x3, local copies, waits for them, and re-layouts: 2.94 us -> 1.09 us  [on_device(): row_feats = block[:feat_dim]]
    dynamic_slice x0 -> x1, local copies, waits for them, and re-layouts: none -> 1.62 us  [on_device(): mine = lax.dynamic_slice_in_dim(block, col % halves * span, span, 1)]
  transfers between devices with their start and end apart: 3 -> 2, of which waited for: 1 -> 1; matrix products, arithmetic and copies ran while one was open for 18% -> 1% of each run, Pallas kernels for 0% -> 0%
where the time goes in v9:
time: 121 us
  matrix products  41.3 us (34%)
  blocking collectives  37.5 us (31%)
  waiting for transfers between devices  19.5 us (16%)
  starting transfers between devices  12.9 us (11%)
  local copies, waits for them, and re-layouts  8.67 us (7%)
    dot_general x6, matrix products, dot_f32(): lax.dot_general(left, right, (dims, ((), ())), preferred_element_type=jnp...  41.3 us
    all_to_all x1, blocking collectives, on_device(): summed = lax.all_to_all(parts, 'col', 0, 0, tiled=False)  37.5 us
    all_to_all x1, waiting for transfers between devices, gather_peers(): arrived = lax.all_to_all(spread, axis, 0, 0, tiled=False)  19.5 us
    all_to_all x1, starting transfers between devices, gather_peers(): arrived = lax.all_to_all(spread, axis, 0, 0, tiled=False)  11.4 us
  transfers between devices with their start and end apart: 2, of which 1 were waited for; matrix products, arithmetic and copies ran while one was open for 1% of the time, Pallas kernels for 0%

profile of v9, /device:TPU:1, one launch (start us, length us, event | category | flops | bytes accessed | tf_op | source)
XLA Modules:
  0.0 121.0 jit_solution(14774999458429739470)
XLA Ops:
  0.0 0.0 copy-start
  0.0 1.6 %copy-done = bf16[1024,1024]{1,0:T(8,128)(2,1)S(1)} copy-done((bf16[1024,1024]{1,0:T(8,128)(2,1)S(1)}, bf16[1024,1024]{1,0:T(8,128)(2,1)}, u32[]{:S(2)}) %copy-start) | copy-done | bytes 2097176
  1.6 1.6 %fusion.13 = bf16[160,1024]{1,0:T(8,128)(2,1)S(1)} fusion(bf16[1024,1024]{1,0:T(8,128)(2,1)S(1)} %copy-done, bf16[160,128]{1,0:T(8,128)(2,1)} %param.8, bf16[128,1024]{1,0:T(8,128)(2,1)} %param.9), kind=kOutput, calls=%fused_computation.16 | convolution fusion | flops 378142720 | bytes 2727936 | tf_op jit(solution)/shard_map/dot_general | solution.py:8
  3.2 0.2 fusion.15
  3.4 0.0 copy-done.1
  3.5 0.9 broadcast_in_dim.17
  4.4 11.4 %all-to-all-start = ((bf16[32,40,160]{2,1,0:T(8,128)(2,1)}), bf16[32,40,160]{2,1,0:T(8,128)(2,1)S(1)}, u32[]{:S(2)}, u32[]{:S(2)}) async-start(bf16[32,40,160]{2,1,0:T(8,128)(2,1)} %broadcast_in_dim.17), calls=%async_computation | async-start | bytes 1310720 | tf_op jit(solution)/shard_map/all_to_all | solution.py:23
  15.8 19.5 %all-to-all-done = bf16[32,40,160]{2,1,0:T(8,128)(2,1)S(1)} async-done(((bf16[32,40,160]{2,1,0:T(8,128)(2,1)}), bf16[32,40,160]{2,1,0:T(8,128)(2,1)S(1)}, u32[]{:S(2)}, u32[]{:S(2)}) %all-to-all-start) | async-done | bytes 409632 | tf_op jit(solution)/shard_map/all_to_all | solution.py:23
  35.3 0.1 copy.7
  35.4 1.7 %reshape.12 = bf16[40,5120]{1,0:T(8,128)(2,1)} reshape(bf16[40,32,160]{2,1,0:T(8,128)(2,1)S(1)} %copy.7) | data formatting | bytes 819200 | tf_op jit(solution)/shard_map/reshape | solution.py:25
  37.2 1.6 %constant_dynamic-slice_fusion = bf16[40,2560]{1,0:T(8,128)(2,1)} fusion(bf16[40,5120]{1,0:T(8,128)(2,1)} %reshape.12, s32[]{:T(128)S(6)} %select_n.20), kind=kLoop, calls=%fused_computation.27 | loop fusion | bytes 409604 | tf_op jit(solution)/shard_map/dynamic_slice | solution.py:62
  38.8 1.6 %collective-permute-start = (bf16[40,2560]{1,0:T(8,128)(2,1)}, bf16[40,2560]{1,0:T(8,128)(2,1)S(1)}, u32[]{:S(2)}, u32[]{:S(2)}) collective-permute-start(bf16[40,2560]{1,0:T(8,128)(2,1)} %constant_dynamic-slice_fusion), channel_id=1, source_target_pairs={{0,0},{1,1},{2,482},{3,483},{4,452},{5,453},{6,422},{7,423},{8,392... | collective-permute-start | bytes 614408 | tf_op jit(solution)/shard_map/ppermute | solution.py:71
  40.4 0.1 slice.17
  40.4 0.2 multiply_reduce_fusion
  40.6 0.1 reduce_sum.30
  40.7 0.3 copy.8
  41.0 0.7 slice.15
  41.8 0.0 collective-permute-done
  41.8 0.1 fusion.17
  41.9 39.8 %while.14 = (s32[]{:T(128)}, f32[8,5120]{1,0:T(8,128)}, bf16[8,2560]{1,0:T(8,128)(2,1)S(1)}, f32[5120]{0:T(1024)S(1)}, f32[2560]{0:T(1024)S(1)}, /*index=5*/bf16...) while((s32[]{:T(128)}, f32[8,5120]{1,0:T(8,128)}, ...), condition=%wide.region_3.4_spmd.clone, body=%wide.region_2.3_spmd.clone.sunk | while | flops 298270720 | bytes 737968 | solution.py:41
  41.9 0.1 dynamic_slice.39
  42.0 9.2 %convolution_add_fusion.2 = f32[8,5120]{1,0:T(8,128)} fusion(bf16[32,5120]{1,0:T(8,128)(2,1)S(1)} %get-tuple-element.241, f32[640]{0:T(1024)S(1)} %dynamic_slice.39, f32[5120]{0:T(1024)S(1)} %get-tuple-element.238, f32[8,5120]{1,0:T(8,128)} %get-tuple-element.225, pred[]{:T(512)S(6)} %compare.4, bf16[32,2560]{1,0:T(8,128)(2,1)S(1)} %get-tuple-element.240, ...), kind=kOutput, calls=%fused_computation.5.clone.1 | convolution fusion | flops 298270720 | bytes 732672 | tf_op jit(solution)/shard_map/while/body/eval_jaxpr/dot_general | solution.py:8
  51.1 0.1 dynamic_slice.39
  51.2 10.1 %convolution_add_fusion.2 = f32[8,5120]{1,0:T(8,128)} fusion(bf16[32,5120]{1,0:T(8,128)(2,1)S(1)} %get-tuple-element.241, f32[640]{0:T(1024)S(1)} %dynamic_slice.39, f32[5120]{0:T(1024)S(1)} %get-tuple-element.238, f32[8,5120]{1,0:T(8,128)} %get-tuple-element.225, pred[]{:T(512)S(6)} %compare.4, bf16[32,2560]{1,0:T(8,128)(2,1)S(1)} %get-tuple-element.240, ...), kind=kOutput, calls=%fused_computation.5.clone.1 | convolution fusion | flops 298270720 | bytes 732672 | tf_op jit(solution)/shard_map/while/body/eval_jaxpr/dot_general | solution.py:8
  61.3 0.1 dynamic_slice.39
  61.4 10.1 %convolution_add_fusion.2 = f32[8,5120]{1,0:T(8,128)} fusion(bf16[32,5120]{1,0:T(8,128)(2,1)S(1)} %get-tuple-element.241, f32[640]{0:T(1024)S(1)} %dynamic_slice.39, f32[5120]{0:T(1024)S(1)} %get-tuple-element.238, f32[8,5120]{1,0:T(8,128)} %get-tuple-element.225, pred[]{:T(512)S(6)} %compare.4, bf16[32,2560]{1,0:T(8,128)(2,1)S(1)} %get-tuple-element.240, ...), kind=kOutput, calls=%fused_computation.5.clone.1 | convolution fusion | flops 298270720 | bytes 732672 | tf_op jit(solution)/shard_map/while/body/eval_jaxpr/dot_general | solution.py:8
  71.5 0.1 dynamic_slice.39
  71.5 10.1 %convolution_add_fusion.2 = f32[8,5120]{1,0:T(8,128)} fusion(bf16[32,5120]{1,0:T(8,128)(2,1)S(1)} %get-tuple-element.241, f32[640]{0:T(1024)S(1)} %dynamic_slice.39, f32[5120]{0:T(1024)S(1)} %get-tuple-element.238, f32[8,5120]{1,0:T(8,128)} %get-tuple-element.225, pred[]{:T(512)S(6)} %compare.4, bf16[32,2560]{1,0:T(8,128)(2,1)S(1)} %get-tuple-element.240, ...), kind=kOutput, calls=%fused_computation.5.clone.1 | convolution fusion | flops 298270720 | bytes 732672 | tf_op jit(solution)/shard_map/while/body/eval_jaxpr/dot_general | solution.py:8
  81.6 1.0 reshape.13
  82.7 0.2 copy.9
  82.9 37.5 %all_to_all.10 = f32[32,8,160]{2,1,0:T(8,128)S(1)} all-to-all(f32[32,8,160]{2,1,0:T(8,128)S(1)} %copy.9), channel_id=1, replica_groups=mesh['row'=16,'col'=32] {'col'}, dimensions={0} | all-to-all | bytes 327680 | tf_op jit(solution)/shard_map/all_to_all | solution.py:78
  120.4 0.6 reduce_sum.32
  (8 shorter events, 0.0 us)
Async XLA Ops:
  0.0 1.6 %copy-start = (bf16[1024,1024]{1,0:T(8,128)(2,1)S(1)}, bf16[1024,1024]{1,0:T(8,128)(2,1)}, u32[]{:S(2)}) copy-start(bf16[1024,1024]{1,0:T(8,128)(2,1)} %param.10) | copy-start | bytes 6291460
  0.0 3.2 %copy-start.2 = (bf16[1024,32]{0,1:T(8,128)(2,1)S(1)}, bf16[1024,32]{0,1:T(8,128)(2,1)}, u32[]{:S(2)}) copy-start(bf16[1024,32]{0,1:T(8,128)(2,1)} %param.11) | copy-start | bytes 196612
  0.0 3.2 %copy-start.3 = (f32[32]{0:T(128)S(1)}, f32[32]{0:T(128)}, u32[]{:S(2)}) copy-start(f32[32]{0:T(128)} %param.12) | copy-start | bytes 388
  1.6 1.9 %copy-start.1 = (bf16[8,160]{1,0:T(8,128)(2,1)S(1)}, bf16[8,160]{1,0:T(8,128)(2,1)}, u32[]{:S(2)}) copy-start(bf16[8,160]{1,0:T(8,128)(2,1)} %param.13) | copy-start | bytes 7684
  4.4 30.9 %all-to-all-start = ((bf16[32,40,160]{2,1,0:T(8,128)(2,1)}), bf16[32,40,160]{2,1,0:T(8,128)(2,1)S(1)}, u32[]{:S(2)}, u32[]{:S(2)}) async-start(bf16[32,40,160]{2,1,0:T(8,128)(2,1)} %broadcast_in_dim.17), calls=%async_computation | async-start | bytes 1310720 | tf_op jit(solution)/shard_map/all_to_all | solution.py:23
  38.8 3.0 %collective-permute-start = (bf16[40,2560]{1,0:T(8,128)(2,1)}, bf16[40,2560]{1,0:T(8,128)(2,1)S(1)}, u32[]{:S(2)}, u32[]{:S(2)}) collective-permute-start(bf16[40,2560]{1,0:T(8,128)(2,1)} %constant_dynamic-slice_fusion), channel_id=1, source_target_pairs={{0,0},{1,1},{2,482},{3,483},{4,452},{5,453},{6,422},{7,423},{8,392... | collective-permute-start | bytes 614408 | tf_op jit(solution)/shard_map/ppermute | solution.py:71

commit v10 on v8

--- a/solution.py
+++ b/solution.py
@@ -71,12 +71,21 @@
         lax.ppermute(mine[:, k * width:(k + 1) * width], ("row", "col"), pairs)
         for k in range(chunks)
     ]
-    acc = jnp.zeros((probe_rows, block.shape[1]), jnp.float32)
-    for piece in arrived:
-        acc = fold_columns(row_feats, row_sq, piece[:feat_dim], piece[feat_dim:], acc, 640)
-    parts = jnp.transpose(acc.reshape(probe_rows, col_peers, local), (1, 0, 2))
-    summed = lax.all_to_all(parts, "col", 0, 0, tiled=False)
-    return jnp.sum(summed, axis=0)
+    row_halves = 2
+    part = local // row_halves
+    feats_split = row_feats.reshape(feat_dim, col_peers, row_halves, part)
+    sq_split = row_sq.reshape(col_peers, row_halves, part)
+    results = []
+    for h in range(row_halves):
+        half_feats = feats_split[:, :, h, :].reshape(feat_dim, col_peers * part)
+        half_sq = sq_split[:, h, :].reshape(col_peers * part)
+        acc = jnp.zeros((probe_rows, col_peers * part), jnp.float32)
+        for piece in arrived:
+            acc = fold_columns(half_feats, half_sq, piece[:feat_dim], piece[feat_dim:], acc, 640)
+        parts = jnp.transpose(acc.reshape(probe_rows, col_peers, part), (1, 0, 2))
+        summed = lax.all_to_all(parts, "col", 0, 0, tiled=False)
+        results.append(jnp.sum(summed, axis=0))
+    return jnp.concatenate(results, axis=1)
 
 
 def solution(mesh):

time: 110 us -> 130 us (1.18)
  blocking collectives: 30.8 us -> 0 us
  starting transfers between devices: 12.9 us -> 39.8 us
  waiting for transfers between devices: 19.5 us -> 28.2 us
  local copies, waits for them, and re-layouts: 8.99 us -> 16.8 us
  other arithmetic: 0.9 us -> 6.4 us
    all_to_all x1 -> x0, blocking collectives: 30.8 us -> none  [on_device(): summed = lax.all_to_all(parts, 'col', 0, 0, tiled=False)]
    all_to_all x0 -> x2, starting transfers between devices: none -> 26.9 us  [on_device(): summed = lax.all_to_all(parts, 'col', 0, 0, tiled=False)]
    all_to_all x0 -> x2, waiting for transfers between devices: none -> 8.65 us  [on_device(): summed = lax.all_to_all(parts, 'col', 0, 0, tiled=False)]
    slice x0 -> x2, local copies, waits for them, and re-layouts: none -> 2.99 us  [the longest x1 2.96 us: on_device(): half_feats = feats_split[:, :, h, :].reshape(feat_dim, col_peers * part)]
    another operation x0 -> x6, local copies, waits for them, and re-layouts: none -> 2.74 us
    another operation x0 -> x4, other arithmetic: none -> 2.69 us
    while x0 -> x4, other arithmetic: none -> 2.69 us
    slice x3 -> x1, local copies, waits for them, and re-layouts: 2.94 us -> 0.85 us  [on_device(): row_feats = block[:feat_dim]]
  transfers between devices with their start and end apart: 3 -> 5, of which waited for: 1 -> 2; matrix products, arithmetic and copies ran while one was open for 18% -> 32% of each run, Pallas kernels for 0% -> 0%
where the time goes in v10:
time: 130 us; the launch traced here: 128 us
  starting transfers between devices  39.8 us (31%)
  matrix products  36.7 us (28%)
  waiting for transfers between devices  28.2 us (22%)
  local copies, waits for them, and re-layouts  16.8 us (13%)
  other arithmetic  6.4 us (5%)
    dot_general x10, matrix products, dot_f32(): lax.dot_general(left, right, (dims, ((), ())), preferred_element_type=jnp...  36.7 us
    all_to_all x2, starting transfers between devices, on_device(): summed = lax.all_to_all(parts, 'col', 0, 0, tiled=False)  26.9 us
    all_to_all x1, waiting for transfers between devices, gather_peers(): arrived = lax.all_to_all(spread, axis, 0, 0, tiled=False)  19.5 us
    all_to_all x1, starting transfers between devices, gather_peers(): arrived = lax.all_to_all(spread, axis, 0, 0, tiled=False)  11.4 us
    all_to_all x2, waiting for transfers between devices, on_device(): summed = lax.all_to_all(parts, 'col', 0, 0, tiled=False)  8.65 us
    slice x1, local copies, waits for them, and re-layouts, on_device(): half_feats = feats_split[:, :, h, :].reshape(feat_dim, col_peers * part)  2.96 us
    another operation x4, other arithmetic  2.69 us
    while x4, other arithmetic  2.69 us
  transfers between devices with their start and end apart: 5, of which 2 were waited for; matrix products, arithmetic and copies ran while one was open for 32% of the time, Pallas kernels for 0%

profile of v10, /device:TPU:1, one launch (start us, length us, event | category | flops | bytes accessed | tf_op | source)
XLA Modules:
  0.0 128.3 jit_solution(16592722586272334810)
XLA Ops:
  0.0 1.6 %copy-done = bf16[1024,1024]{1,0:T(8,128)(2,1)S(1)} copy-done((bf16[1024,1024]{1,0:T(8,128)(2,1)S(1)}, bf16[1024,1024]{1,0:T(8,128)(2,1)}, u32[]{:S(2)}) %copy-start) | copy-done | bytes 2097176
  1.6 1.6 %fusion.49 = bf16[160,1024]{1,0:T(8,128)(2,1)S(1)} fusion(bf16[1024,1024]{1,0:T(8,128)(2,1)S(1)} %copy-done, bf16[160,128]{1,0:T(8,128)(2,1)} %param.14, bf16[128,1024]{1,0:T(8,128)(2,1)} %param.15), kind=kOutput, calls=%fused_computation.55 | convolution fusion | flops 378142720 | bytes 2727936 | tf_op jit(solution)/shard_map/dot_general | solution.py:8
  3.5 0.9 broadcast_in_dim.19
  4.3 11.4 %all-to-all-start = ((bf16[32,40,160]{2,1,0:T(8,128)(2,1)}), bf16[32,40,160]{2,1,0:T(8,128)(2,1)S(1)}, u32[]{:S(2)}, u32[]{:S(2)}) async-start(bf16[32,40,160]{2,1,0:T(8,128)(2,1)} %broadcast_in_dim.19), calls=%async_computation | async-start | bytes 1310720 | tf_op jit(solution)/shard_map/all_to_all | solution.py:23
  15.8 19.5 %all-to-all-done = bf16[32,40,160]{2,1,0:T(8,128)(2,1)S(1)} async-done(((bf16[32,40,160]{2,1,0:T(8,128)(2,1)}), bf16[32,40,160]{2,1,0:T(8,128)(2,1)S(1)}, u32[]{:S(2)}, u32[]{:S(2)}) %all-to-all-start) | async-done | bytes 409632 | tf_op jit(solution)/shard_map/all_to_all | solution.py:23
  35.6 0.9 slice.50
  36.5 1.0 reshape.29
  38.2 1.3 %reshape.34 = bf16[32,32,2,80]{3,2,0,1:T(2,128)(2,1)S(1)} reshape(bf16[32,32,160]{2,0,1:T(8,128)(2,1)} %slice.50) | data formatting | bytes 655360 | tf_op jit(solution)/shard_map/reshape | solution.py:76
  39.6 3.0 %slice_reduce_fusion.1 = (bf16[32,32,80]{2,0,1:T(8,128)(2,1)S(1)}, bf16[32,32,80]{2,0,1:T(8,128)(2,1)S(1)}) fusion(bf16[32,32,2,80]{3,2,0,1:T(2,128)(2,1)S(1)} %reshape.34), kind=kLoop, calls=%fused_computation.61 | loop fusion | bytes 655360 | tf_op jit(solution)/shard_map/slice | solution.py:80
  43.0 0.8 collective-permute-start.1
  44.4 11.4 %while.57 = (s32[]{:T(128)}, f32[8,2560]{1,0:T(8,128)S(1)}, bf16[8,1280]{1,0:T(8,128)(2,1)S(1)}, f32[32,1,80]{2,1,0:T(1,128)S(1)}, f32[1280]{0:T(1024)S(1)}, /*i...) while((s32[]{:T(128)}, f32[8,2560]{1,0:T(8,128)S(1)}, ...), condition=%wide.region_9.10_spmd.clone, body=%wide.region_8.9_spmd.clone.sunk | while | flops 149135360 | bytes 443076 | solution.py:41
  45.8 4.4 %convolution_add_fusion.11 = f32[8,2560]{1,0:T(8,128)S(1)} fusion(bf16[32,2560]{1,0:T(8,128)(2,1)S(1)} %get-tuple-element.821, f32[640]{0:T(1024)S(1)} %dynamic_slice.137, f32[2560]{0:T(1024)S(1)} %add.595, f32[8,2560]{1,0:T(8,128)S(1)} %get-tuple-element.804, bf16[32,1280]{1,0:T(8,128)(2,1)S(1)} %get-tuple-element.820, s32[]{:T(128)S(6)} %select_n.57, ...), kind=kOutput, calls=%fused_computation.44.clone.1 | convolution fusion | flops 149135360 | bytes 396800 | tf_op jit(solution)/shard_map/while/body/eval_jaxpr/dot_general | solution.py:8
  51.5 4.4 %convolution_add_fusion.11 = f32[8,2560]{1,0:T(8,128)S(1)} fusion(bf16[32,2560]{1,0:T(8,128)(2,1)S(1)} %get-tuple-element.821, f32[640]{0:T(1024)S(1)} %dynamic_slice.137, f32[2560]{0:T(1024)S(1)} %add.595, f32[8,2560]{1,0:T(8,128)S(1)} %get-tuple-element.804, bf16[32,1280]{1,0:T(8,128)(2,1)S(1)} %get-tuple-element.820, s32[]{:T(128)S(6)} %select_n.57, ...), kind=kOutput, calls=%fused_computation.44.clone.1 | convolution fusion | flops 149135360 | bytes 396800 | tf_op jit(solution)/shard_map/while/body/eval_jaxpr/dot_general | solution.py:8
  55.9 11.4 %while.55 = (s32[]{:T(128)}, f32[8,2560]{1,0:T(8,128)S(1)}, bf16[8,1280]{1,0:T(8,128)(2,1)S(1)}, f32[32,1,80]{2,1,0:T(1,128)S(1)}, f32[1280]{0:T(1024)S(1)}, /*i...) while((s32[]{:T(128)}, f32[8,2560]{1,0:T(8,128)S(1)}, ...), condition=%wide.region_11.12_spmd, body=%wide.region_10.11_spmd.sunk | while | flops 149114880 | bytes 442555 | solution.py:41
  57.3 4.3 %convolution_add_fusion.9 = f32[8,2560]{1,0:T(8,128)S(1)} fusion(f32[8,2560]{1,0:T(8,128)S(1)} %get-tuple-element.840, bf16[32,2560]{1,0:T(8,128)(2,1)S(1)} %get-tuple-element.857, f32[640]{0:T(1024)S(1)} %dynamic_slice.131, f32[2560]{0:T(1024)S(1)} %add.575, bf16[32,1280]{1,0:T(8,128)(2,1)S(1)} %get-tuple-element.856, s32[]{:T(128)S(6)} %select_n.55, ...), kind=kOutput, calls=%fused_computation.18.clone.1 | convolution fusion | flops 149114880 | bytes 396288 | tf_op jit(solution)/shard_map/while/body/eval_jaxpr/dot_general | solution.py:8
  63.0 4.4 %convolution_add_fusion.9 = f32[8,2560]{1,0:T(8,128)S(1)} fusion(f32[8,2560]{1,0:T(8,128)S(1)} %get-tuple-element.840, bf16[32,2560]{1,0:T(8,128)(2,1)S(1)} %get-tuple-element.857, f32[640]{0:T(1024)S(1)} %dynamic_slice.131, f32[2560]{0:T(1024)S(1)} %add.575, bf16[32,1280]{1,0:T(8,128)(2,1)S(1)} %get-tuple-element.856, s32[]{:T(128)S(6)} %select_n.55, ...), kind=kOutput, calls=%fused_computation.18.clone.1 | convolution fusion | flops 149114880 | bytes 396288 | tf_op jit(solution)/shard_map/while/body/eval_jaxpr/dot_general | solution.py:8
  67.5 0.7 copy.11
  68.2 19.2 %all-to-all-start.2 = ((f32[32,8,80]{2,1,0:T(8,128)}), f32[32,8,80]{2,1,0:T(8,128)S(1)}, u32[]{:S(2)}, u32[]{:S(2)}) async-start(f32[32,8,80]{2,1,0:T(8,128)} %copy.11), calls=%async_computation.2 | async-start | bytes 262144 | tf_op jit(solution)/shard_map/all_to_all | solution.py:86
  87.4 11.5 %while.56 = (s32[]{:T(128)}, f32[8,2560]{1,0:T(8,128)S(1)}, bf16[8,1280]{1,0:T(8,128)(2,1)S(1)}, f32[32,1,80]{2,1,0:T(1,128)S(1)}, f32[1280]{0:T(1024)S(1)}, /*i...) while((s32[]{:T(128)}, f32[8,2560]{1,0:T(8,128)S(1)}, ...), condition=%wide.region_3.4_spmd.clone, body=%wide.region_2.3_spmd.clone.sunk | while | flops 149135360 | bytes 443076 | solution.py:41
  88.0 0.7 reduce.27
  88.8 4.4 %convolution_add_fusion.10 = f32[8,2560]{1,0:T(8,128)S(1)} fusion(bf16[32,2560]{1,0:T(8,128)(2,1)S(1)} %get-tuple-element.893, f32[640]{0:T(1024)S(1)} %dynamic_slice.134, f32[2560]{0:T(1024)S(1)} %add.585, f32[8,2560]{1,0:T(8,128)S(1)} %get-tuple-element.876, bf16[32,1280]{1,0:T(8,128)(2,1)S(1)} %get-tuple-element.892, s32[]{:T(128)S(6)} %select_n.56, ...), kind=kOutput, calls=%fused_computation.31.clone.1 | convolution fusion | flops 149135360 | bytes 396800 | tf_op jit(solution)/shard_map/while/body/eval_jaxpr/dot_general | solution.py:8
  93.8 0.7 reduce.27
  94.5 4.4 %convolution_add_fusion.10 = f32[8,2560]{1,0:T(8,128)S(1)} fusion(bf16[32,2560]{1,0:T(8,128)(2,1)S(1)} %get-tuple-element.893, f32[640]{0:T(1024)S(1)} %dynamic_slice.134, f32[2560]{0:T(1024)S(1)} %add.585, f32[8,2560]{1,0:T(8,128)S(1)} %get-tuple-element.876, bf16[32,1280]{1,0:T(8,128)(2,1)S(1)} %get-tuple-element.892, s32[]{:T(128)S(6)} %select_n.56, ...), kind=kOutput, calls=%fused_computation.31.clone.1 | convolution fusion | flops 149135360 | bytes 396800 | tf_op jit(solution)/shard_map/while/body/eval_jaxpr/dot_general | solution.py:8
  98.9 11.5 %while.54 = (s32[]{:T(128)}, f32[8,2560]{1,0:T(8,128)S(1)}, bf16[8,1280]{1,0:T(8,128)(2,1)S(1)}, f32[32,1,80]{2,1,0:T(1,128)S(1)}, f32[1280]{0:T(1024)S(1)}, /*i...) while((s32[]{:T(128)}, f32[8,2560]{1,0:T(8,128)S(1)}, ...), condition=%wide.region_6.7_spmd, body=%wide.region_5.6_spmd.sunk | while | flops 149114880 | bytes 442555 | solution.py:41
  99.5 0.7 reduce.25
  100.2 4.4 %convolution_add_fusion.8 = f32[8,2560]{1,0:T(8,128)S(1)} fusion(f32[8,2560]{1,0:T(8,128)S(1)} %get-tuple-element.912, bf16[32,2560]{1,0:T(8,128)(2,1)S(1)} %get-tuple-element.929, f32[640]{0:T(1024)S(1)} %dynamic_slice.128, f32[2560]{0:T(1024)S(1)} %add.565, bf16[32,1280]{1,0:T(8,128)(2,1)S(1)} %get-tuple-element.928, s32[]{:T(128)S(6)} %select_n.54, ...), kind=kOutput, calls=%fused_computation.5.clone.1 | convolution fusion | flops 149114880 | bytes 396288 | tf_op jit(solution)/shard_map/while/body/eval_jaxpr/dot_general | solution.py:8
  105.2 0.7 reduce.25
  106.0 4.4 %convolution_add_fusion.8 = f32[8,2560]{1,0:T(8,128)S(1)} fusion(f32[8,2560]{1,0:T(8,128)S(1)} %get-tuple-element.912, bf16[32,2560]{1,0:T(8,128)(2,1)S(1)} %get-tuple-element.929, f32[640]{0:T(1024)S(1)} %dynamic_slice.128, f32[2560]{0:T(1024)S(1)} %add.565, bf16[32,1280]{1,0:T(8,128)(2,1)S(1)} %get-tuple-element.928, s32[]{:T(128)S(6)} %select_n.54, ...), kind=kOutput, calls=%fused_computation.5.clone.1 | convolution fusion | flops 149114880 | bytes 396288 | tf_op jit(solution)/shard_map/while/body/eval_jaxpr/dot_general | solution.py:8
  110.5 0.7 copy.10
  111.2 7.7 %all-to-all-start.1 = ((f32[32,8,80]{2,1,0:T(8,128)}), f32[32,8,80]{2,1,0:T(8,128)S(1)}, u32[]{:S(2)}, u32[]{:S(2)}) async-start(f32[32,8,80]{2,1,0:T(8,128)} %copy.10), calls=%async_computation.1 | async-start | bytes 262144 | tf_op jit(solution)/shard_map/all_to_all | solution.py:86
  118.9 8.6 %all-to-all-done.1 = f32[32,8,80]{2,1,0:T(8,128)S(1)} async-done(((f32[32,8,80]{2,1,0:T(8,128)}), f32[32,8,80]{2,1,0:T(8,128)S(1)}, u32[]{:S(2)}, u32[]{:S(2)}) %all-to-all-start.1) | async-done | bytes 81952 | tf_op jit(solution)/shard_map/all_to_all | solution.py:86
  127.6 0.7 pad_maximum_fusion.1
  (64 shorter events, 10.6 us)
Async XLA Ops:
  0.0 1.6 %copy-start = (bf16[1024,1024]{1,0:T(8,128)(2,1)S(1)}, bf16[1024,1024]{1,0:T(8,128)(2,1)}, u32[]{:S(2)}) copy-start(bf16[1024,1024]{1,0:T(8,128)(2,1)} %param.16) | copy-start | bytes 6291460
  0.0 3.2 %copy-start.4 = (bf16[1024,32]{0,1:T(8,128)(2,1)S(1)}, bf16[1024,32]{0,1:T(8,128)(2,1)}, u32[]{:S(2)}) copy-start(bf16[1024,32]{0,1:T(8,128)(2,1)} %param.17) | copy-start | bytes 196612
  0.0 3.2 %copy-start.5 = (f32[32]{0:T(128)S(1)}, f32[32]{0:T(128)}, u32[]{:S(2)}) copy-start(f32[32]{0:T(128)} %param.18) | copy-start | bytes 388
  1.6 1.9 %copy-start.3 = (bf16[8,160]{1,0:T(8,128)(2,1)S(1)}, bf16[8,160]{1,0:T(8,128)(2,1)}, u32[]{:S(2)}) copy-start(bf16[8,160]{1,0:T(8,128)(2,1)} %param.19) | copy-start | bytes 7684
  4.3 30.9 %all-to-all-start = ((bf16[32,40,160]{2,1,0:T(8,128)(2,1)}), bf16[32,40,160]{2,1,0:T(8,128)(2,1)S(1)}, u32[]{:S(2)}, u32[]{:S(2)}) async-start(bf16[32,40,160]{2,1,0:T(8,128)(2,1)} %broadcast_in_dim.19), calls=%async_computation | async-start | bytes 1310720 | tf_op jit(solution)/shard_map/all_to_all | solution.py:23
  37.5 6.9 %collective-permute-start = (bf16[40,1280]{1,0:T(8,128)(2,1)S(1)}, bf16[40,1280]{1,0:T(8,128)(2,1)S(1)}, u32[]{:S(2)}, u32[]{:S(2)}) collective-permute-start(bf16[40,1280]{1,0:T(8,128)(2,1)S(1)} %get-tuple-element.612), channel_id=1, source_target_pairs={{0,0},{1,1},{2,482},{3,483},{4,452},{5,453},{6,422},{7,423},{8,392... | collective-permute-start | bytes 307208 | tf_op jit(solution)/shard_map/ppermute | solution.py:71
  39.6 4.8 %copy-start.2 = (f32[8,2560]{1,0:T(8,128)S(1)}, f32[8,2560]{1,0:T(8,128)}, u32[]{:S(2)}) copy-start(f32[8,2560]{1,0:T(8,128)} %custom-call.1) | copy-start | bytes 245764
  43.0 12.8 %collective-permute-start.1 = (bf16[40,1280]{1,0:T(8,128)(2,1)S(1)}, bf16[40,1280]{1,0:T(8,128)(2,1)S(1)}, u32[]{:S(2)}, u32[]{:S(2)}) collective-permute-start(bf16[40,1280]{1,0:T(8,128)(2,1)S(1)} %get-tuple-element.611), channel_id=1, source_target_pairs={{0,0},{1,1},{2,482},{3,483},{4,452},{5,453},{6,422},{7,423},{8,392... | collective-permute-start | bytes 307208 | tf_op jit(solution)/shard_map/ppermute | solution.py:71
  55.9 31.5 %copy-start.1 = (f32[8,2560]{1,0:T(8,128)S(1)}, f32[8,2560]{1,0:T(8,128)}, u32[]{:S(2)}) copy-start(f32[8,2560]{1,0:T(8,128)} %custom-call) | copy-start | bytes 245764
  68.2 43.0 %all-to-all-start.2 = ((f32[32,8,80]{2,1,0:T(8,128)}), f32[32,8,80]{2,1,0:T(8,128)S(1)}, u32[]{:S(2)}, u32[]{:S(2)}) async-start(f32[32,8,80]{2,1,0:T(8,128)} %copy.11), calls=%async_computation.2 | async-start | bytes 262144 | tf_op jit(solution)/shard_map/all_to_all | solution.py:86
  111.2 16.4 %all-to-all-start.1 = ((f32[32,8,80]{2,1,0:T(8,128)}), f32[32,8,80]{2,1,0:T(8,128)S(1)}, u32[]{:S(2)}, u32[]{:S(2)}) async-start(f32[32,8,80]{2,1,0:T(8,128)} %copy.10), calls=%async_computation.1 | async-start | bytes 262144 | tf_op jit(solution)/shard_map/all_to_all | solution.py:86

commit v11 on v8

--- a/solution.py
+++ b/solution.py
@@ -11,8 +11,8 @@
 
 
 def matern_tile(left_feats, left_sq, right_doubled, right_sq):
-    cross_term = dot_f32(left_feats, right_doubled, ((0,), (0,)))
-    dist_sq = jnp.maximum(left_sq[:, None] + right_sq[None, :] + cross_term, 0.0)
+    cross_term = dot_f32(right_doubled, left_feats, ((0,), (0,)))
+    dist_sq = jnp.maximum(left_sq[None, :] + right_sq[:, None] + cross_term, 0.0)
     scaled_dist = jnp.sqrt(5.0 * dist_sq)
     values = (1.0 + scaled_dist + scaled_dist * scaled_dist / 3.0) * jnp.exp(-scaled_dist)
     return values.astype(jnp.bfloat16)
@@ -36,7 +36,7 @@
         sq_block = lax.dynamic_slice_in_dim(sq_norm, column_start, block_cols, 0)
         probes_block = lax.dynamic_slice_in_dim(probes, column_start, block_cols, 1)
         kernel_tile = matern_tile(row_feats, row_sq, feats_block, sq_block)
-        return row_acc + dot_f32(probes_block, kernel_tile, ((1,), (1,)))
+        return row_acc + dot_f32(probes_block, kernel_tile, ((1,), (0,)))
 
     return lax.fori_loop(0, feats.shape[1] // block_cols, advance, acc)
 

time: 110 us -> 110 us (level)
  no operation moved by 1% of the time
where the time goes in v11:
time: 110 us
  matrix products  35.9 us (33%)
  blocking collectives  30.8 us (28%)
  waiting for transfers between devices  19.5 us (18%)
  starting transfers between devices  12.9 us (12%)
  local copies, waits for them, and re-layouts  8.99 us (8%)
    dot_general x6, matrix products, dot_f32(): lax.dot_general(left, right, (dims, ((), ())), preferred_element_type=jnp...  35.9 us
    all_to_all x1, blocking collectives, on_device(): summed = lax.all_to_all(parts, 'col', 0, 0, tiled=False)  30.8 us
    all_to_all x1, waiting for transfers between devices, gather_peers(): arrived = lax.all_to_all(spread, axis, 0, 0, tiled=False)  19.5 us
    all_to_all x1, starting transfers between devices, gather_peers(): arrived = lax.all_to_all(spread, axis, 0, 0, tiled=False)  11.4 us
    slice x3, local copies, waits for them, and re-layouts, on_device(): row_feats = block[:feat_dim]  2.94 us
  transfers between devices with their start and end apart: 3, of which 1 were waited for; matrix products, arithmetic and copies ran while one was open for 18% of the time, Pallas kernels for 0%

profile of v11, /device:TPU:1, one launch (start us, length us, event | category | flops | bytes accessed | tf_op | source)
XLA Modules:
  0.0 109.5 jit_solution(5332856318225083495)
XLA Ops:
  0.0 1.6 %copy-done = bf16[1024,1024]{1,0:T(8,128)(2,1)S(1)} copy-done((bf16[1024,1024]{1,0:T(8,128)(2,1)S(1)}, bf16[1024,1024]{1,0:T(8,128)(2,1)}, u32[]{:S(2)}) %copy-start) | copy-done | bytes 2097176
  1.6 1.6 %fusion.19 = bf16[160,1024]{1,0:T(8,128)(2,1)S(1)} fusion(bf16[1024,1024]{1,0:T(8,128)(2,1)S(1)} %copy-done, bf16[160,128]{1,0:T(8,128)(2,1)} %param.10, bf16[128,1024]{1,0:T(8,128)(2,1)} %param.11), kind=kOutput, calls=%fused_computation.21 | convolution fusion | flops 378142720 | bytes 2727936 | tf_op jit(solution)/shard_map/dot_general | solution.py:8
  3.2 0.2 fusion.21
  3.4 0.0 copy-done.2
  3.5 0.9 broadcast_in_dim.23
  4.4 11.4 %all-to-all-start = ((bf16[32,40,160]{2,1,0:T(8,128)(2,1)}), bf16[32,40,160]{2,1,0:T(8,128)(2,1)S(1)}, u32[]{:S(2)}, u32[]{:S(2)}) async-start(bf16[32,40,160]{2,1,0:T(8,128)(2,1)} %broadcast_in_dim.23), calls=%async_computation | async-start | bytes 1310720 | tf_op jit(solution)/shard_map/all_to_all | solution.py:23
  15.8 19.5 %all-to-all-done = bf16[32,40,160]{2,1,0:T(8,128)(2,1)S(1)} async-done(((bf16[32,40,160]{2,1,0:T(8,128)(2,1)}), bf16[32,40,160]{2,1,0:T(8,128)(2,1)S(1)}, u32[]{:S(2)}, u32[]{:S(2)}) %all-to-all-start) | async-done | bytes 409632 | tf_op jit(solution)/shard_map/all_to_all | solution.py:23
  35.3 0.1 copy.7
  35.4 0.9 slice.33
  36.3 1.7 %reshape.14 = bf16[40,5120]{1,0:T(8,128)(2,1)} reshape(bf16[40,32,160]{2,1,0:T(8,128)(2,1)S(1)} %copy.7) | data formatting | bytes 819200 | tf_op jit(solution)/shard_map/reshape | solution.py:25
  38.0 1.0 constant_dynamic-slice_fusion.1
  39.0 0.7 collective-permute-start
  39.7 0.2 multiply_reduce_fusion
  39.9 0.1 reduce_sum.39
  40.0 1.3 %copy.8 = bf16[32,32,160]{2,1,0:T(8,128)(2,1)S(1)} copy(bf16[32,32,160]{2,0,1:T(8,128)(2,1)} %slice.33) | data formatting | bytes 655360 | tf_op jit(solution)/shard_map/slice | solution.py:56
  41.3 0.7 slice.28
  42.1 0.8 collective-permute-start.1
  42.9 0.0 collective-permute-done
  43.0 17.2 %while.28 = (s32[]{:T(128)}, f32[8,5120]{1,0:T(8,128)S(1)}, bf16[8,1280]{1,0:T(8,128)(2,1)S(1)}, f32[5120]{0:T(1024)S(1)}, f32[1280]{0:T(1024)S(1)}, /*index=5*/...) while((s32[]{:T(128)}, f32[8,5120]{1,0:T(8,128)S(1)}, ...), condition=%wide.region_3.4_spmd.clone, body=%wide.region_2.3_spmd.clone.sunk | while | flops 298270720 | bytes 737968 | solution.py:41
  43.0 0.1 dynamic_slice.70
  43.1 8.5 %convolution_add_fusion.5 = f32[8,5120]{1,0:T(8,128)S(1)} fusion(bf16[32,5120]{1,0:T(8,128)(2,1)S(1)} %get-tuple-element.427, f32[640]{0:T(1024)S(1)} %dynamic_slice.70, f32[5120]{0:T(1024)S(1)} %get-tuple-element.424, f32[8,5120]{1,0:T(8,128)S(1)} %get-tuple-element.411, pred[]{:T(512)S(6)} %compare.4, ...), kind=kOutput, calls=%fused_computation.10.clone.1 | convolution fusion | flops 298270720 | bytes 732672 | tf_op jit(solution)/shard_map/while/body/eval_jaxpr/dot_general | solution.py:8
  51.6 0.1 dynamic_slice.70
  51.7 8.5 %convolution_add_fusion.5 = f32[8,5120]{1,0:T(8,128)S(1)} fusion(bf16[32,5120]{1,0:T(8,128)(2,1)S(1)} %get-tuple-element.427, f32[640]{0:T(1024)S(1)} %dynamic_slice.70, f32[5120]{0:T(1024)S(1)} %get-tuple-element.424, f32[8,5120]{1,0:T(8,128)S(1)} %get-tuple-element.411, pred[]{:T(512)S(6)} %compare.4, ...), kind=kOutput, calls=%fused_computation.10.clone.1 | convolution fusion | flops 298270720 | bytes 732672 | tf_op jit(solution)/shard_map/while/body/eval_jaxpr/dot_general | solution.py:8
  60.3 17.5 %while.27 = (s32[]{:T(128)}, f32[8,5120]{1,0:T(8,128)S(1)}, bf16[8,1280]{1,0:T(8,128)(2,1)S(1)}, f32[5120]{0:T(1024)S(1)}, f32[1280]{0:T(1024)S(1)}, /*index=5*/...) while((s32[]{:T(128)}, f32[8,5120]{1,0:T(8,128)S(1)}, ...), condition=%wide.region_6.7_spmd, body=%wide.region_5.6_spmd.sunk | while | flops 298229760 | bytes 737447 | solution.py:41
  60.5 0.1 dynamic_slice.67
  60.6 8.5 %convolution_add_fusion.4 = f32[8,5120]{1,0:T(8,128)S(1)} fusion(f32[8,5120]{1,0:T(8,128)S(1)} %get-tuple-element.444, bf16[32,5120]{1,0:T(8,128)(2,1)S(1)} %get-tuple-element.460, f32[640]{0:T(1024)S(1)} %dynamic_slice.67, f32[5120]{0:T(1024)S(1)} %get-tuple-element.457, bf16[32,1280]{1,0:T(8,128)(2,1)S(1)} %get-tuple-element.459, ...), kind=kOutput, calls=%fused_computation.1.clone.1 | convolution fusion | flops 298229760 | bytes 732160 | tf_op jit(solution)/shard_map/while/body/eval_jaxpr/dot_general | solution.py:8
  69.1 0.1 dynamic_slice.67
  69.2 8.5 %convolution_add_fusion.4 = f32[8,5120]{1,0:T(8,128)S(1)} fusion(f32[8,5120]{1,0:T(8,128)S(1)} %get-tuple-element.444, bf16[32,5120]{1,0:T(8,128)(2,1)S(1)} %get-tuple-element.460, f32[640]{0:T(1024)S(1)} %dynamic_slice.67, f32[5120]{0:T(1024)S(1)} %get-tuple-element.457, bf16[32,1280]{1,0:T(8,128)(2,1)S(1)} %get-tuple-element.459, ...), kind=kOutput, calls=%fused_computation.1.clone.1 | convolution fusion | flops 298229760 | bytes 732160 | tf_op jit(solution)/shard_map/while/body/eval_jaxpr/dot_general | solution.py:8
  77.7 0.1 reshape.15
  77.9 0.2 copy.9
  78.0 30.8 %all_to_all.10 = f32[32,8,160]{2,1,0:T(8,128)S(1)} all-to-all(f32[32,8,160]{2,1,0:T(8,128)S(1)} %copy.9), channel_id=1, replica_groups=mesh['row'=16,'col'=32] {'col'}, dimensions={0} | all-to-all | bytes 327680 | tf_op jit(solution)/shard_map/all_to_all | solution.py:78
  108.9 0.6 reduce_sum.42
  (15 shorter events, 0.1 us)
Async XLA Ops:
  0.0 1.6 %copy-start = (bf16[1024,1024]{1,0:T(8,128)(2,1)S(1)}, bf16[1024,1024]{1,0:T(8,128)(2,1)}, u32[]{:S(2)}) copy-start(bf16[1024,1024]{1,0:T(8,128)(2,1)} %param.12) | copy-start | bytes 6291460
  0.0 3.2 %copy-start.3 = (bf16[1024,32]{0,1:T(8,128)(2,1)S(1)}, bf16[1024,32]{0,1:T(8,128)(2,1)}, u32[]{:S(2)}) copy-start(bf16[1024,32]{0,1:T(8,128)(2,1)} %param.13) | copy-start | bytes 196612
  0.0 3.2 %copy-start.4 = (f32[32]{0:T(128)S(1)}, f32[32]{0:T(128)}, u32[]{:S(2)}) copy-start(f32[32]{0:T(128)} %param.14) | copy-start | bytes 388
  1.6 1.9 %copy-start.2 = (bf16[8,160]{1,0:T(8,128)(2,1)S(1)}, bf16[8,160]{1,0:T(8,128)(2,1)}, u32[]{:S(2)}) copy-start(bf16[8,160]{1,0:T(8,128)(2,1)} %param.15) | copy-start | bytes 7684
  4.4 30.9 %all-to-all-start = ((bf16[32,40,160]{2,1,0:T(8,128)(2,1)}), bf16[32,40,160]{2,1,0:T(8,128)(2,1)S(1)}, u32[]{:S(2)}, u32[]{:S(2)}) async-start(bf16[32,40,160]{2,1,0:T(8,128)(2,1)} %broadcast_in_dim.23), calls=%async_computation | async-start | bytes 1310720 | tf_op jit(solution)/shard_map/all_to_all | solution.py:23
  38.0 5.0 %copy-start.1 = (f32[8,5120]{1,0:T(8,128)S(1)}, f32[8,5120]{1,0:T(8,128)}, u32[]{:S(2)}) copy-start(f32[8,5120]{1,0:T(8,128)} %custom-call) | copy-start | bytes 491524
  39.0 3.9 %collective-permute-start = (bf16[40,1280]{1,0:T(8,128)(2,1)S(1)}, bf16[40,1280]{1,0:T(8,128)(2,1)S(1)}, u32[]{:S(2)}, u32[]{:S(2)}) collective-permute-start(bf16[40,1280]{1,0:T(8,128)(2,1)S(1)} %get-tuple-element.308), channel_id=1, source_target_pairs={{0,0},{1,1},{2,482},{3,483},{4,452},{5,453},{6,422},{7,423},{8,392... | collective-permute-start | bytes 307208 | tf_op jit(solution)/shard_map/ppermute | solution.py:71
  42.1 18.2 %collective-permute-start.1 = (bf16[40,1280]{1,0:T(8,128)(2,1)S(1)}, bf16[40,1280]{1,0:T(8,128)(2,1)S(1)}, u32[]{:S(2)}, u32[]{:S(2)}) collective-permute-start(bf16[40,1280]{1,0:T(8,128)(2,1)S(1)} %get-tuple-element.307), channel_id=1, source_target_pairs={{0,0},{1,1},{2,482},{3,483},{4,452},{5,453},{6,422},{7,423},{8,392... | collective-permute-start | bytes 307208 | tf_op jit(solution)/shard_map/ppermute | solution.py:71

commit v12 on v8

--- a/solution.py
+++ b/solution.py
@@ -60,11 +60,15 @@
     span = block.shape[1] // halves
     col = lax.axis_index("col")
     mine = lax.dynamic_slice_in_dim(block, (col % halves) * span, span, 1)
+    z_run = 4
+    swap = [0, 3, 2, 1]
     pairs = []
     for r in range(row_peers):
         for c in range(col_peers):
-            target = (r - c // halves) % row_peers
-            pairs.append((r * col_peers + c, target * col_peers + c))
+            chip, core = divmod(c, halves)
+            source_chip = (chip // z_run) * z_run + swap[chip % z_run]
+            source = ((r + chip) % row_peers) * col_peers + source_chip * halves + core
+            pairs.append((source, r * col_peers + c))
     chunks = 2
     width = span // chunks
     arrived = [

time: 110 us -> 110 us (level)
  no operation moved by 1% of the time
where the time goes in v12:
time: 110 us; the launch traced here: 109 us
  matrix products  35.9 us (33%)
  blocking collectives  30.6 us (28%)
  waiting for transfers between devices  19.5 us (18%)
  starting transfers between devices  12.9 us (12%)
  local copies, waits for them, and re-layouts  8.99 us (8%)
    dot_general x6, matrix products, dot_f32(): lax.dot_general(left, right, (dims, ((), ())), preferred_element_type=jnp...  35.9 us
    all_to_all x1, blocking collectives, on_device(): summed = lax.all_to_all(parts, 'col', 0, 0, tiled=False)  30.6 us
    all_to_all x1, waiting for transfers between devices, gather_peers(): arrived = lax.all_to_all(spread, axis, 0, 0, tiled=False)  19.5 us
    all_to_all x1, starting transfers between devices, gather_peers(): arrived = lax.all_to_all(spread, axis, 0, 0, tiled=False)  11.4 us
    slice x3, local copies, waits for them, and re-layouts, on_device(): row_feats = block[:feat_dim]  2.94 us
  transfers between devices with their start and end apart: 3, of which 1 were waited for; matrix products, arithmetic and copies ran while one was open for 18% of the time, Pallas kernels for 0%

profile of v12, /device:TPU:1, one launch (start us, length us, event | category | flops | bytes accessed | tf_op | source)
XLA Modules:
  0.0 109.2 jit_solution(8264944031007687294)
XLA Ops:
  0.0 1.6 %copy-done = bf16[1024,1024]{1,0:T(8,128)(2,1)S(1)} copy-done((bf16[1024,1024]{1,0:T(8,128)(2,1)S(1)}, bf16[1024,1024]{1,0:T(8,128)(2,1)}, u32[]{:S(2)}) %copy-start) | copy-done | bytes 2097176
  1.6 1.6 %fusion.25 = bf16[160,1024]{1,0:T(8,128)(2,1)S(1)} fusion(bf16[1024,1024]{1,0:T(8,128)(2,1)S(1)} %copy-done, bf16[160,128]{1,0:T(8,128)(2,1)} %param.10, bf16[128,1024]{1,0:T(8,128)(2,1)} %param.11), kind=kOutput, calls=%fused_computation.29 | convolution fusion | flops 378142720 | bytes 2727936 | tf_op jit(solution)/shard_map/dot_general | solution.py:8
  3.2 0.2 fusion.27
  3.4 0.0 copy-done.2
  3.5 0.9 broadcast_in_dim.23
  4.4 11.4 %all-to-all-start = ((bf16[32,40,160]{2,1,0:T(8,128)(2,1)}), bf16[32,40,160]{2,1,0:T(8,128)(2,1)S(1)}, u32[]{:S(2)}, u32[]{:S(2)}) async-start(bf16[32,40,160]{2,1,0:T(8,128)(2,1)} %broadcast_in_dim.23), calls=%async_computation | async-start | bytes 1310720 | tf_op jit(solution)/shard_map/all_to_all | solution.py:23
  15.8 19.5 %all-to-all-done = bf16[32,40,160]{2,1,0:T(8,128)(2,1)S(1)} async-done(((bf16[32,40,160]{2,1,0:T(8,128)(2,1)}), bf16[32,40,160]{2,1,0:T(8,128)(2,1)S(1)}, u32[]{:S(2)}, u32[]{:S(2)}) %all-to-all-start) | async-done | bytes 409632 | tf_op jit(solution)/shard_map/all_to_all | solution.py:23
  35.3 0.1 copy.7
  35.4 0.9 slice.33
  36.3 1.7 %reshape.14 = bf16[40,5120]{1,0:T(8,128)(2,1)} reshape(bf16[40,32,160]{2,1,0:T(8,128)(2,1)S(1)} %copy.7) | data formatting | bytes 819200 | tf_op jit(solution)/shard_map/reshape | solution.py:25
  38.0 1.0 constant_dynamic-slice_fusion.1
  39.0 0.7 collective-permute-start
  39.7 0.2 multiply_reduce_fusion
  39.9 0.1 reduce_sum.39
  40.0 1.3 %copy.8 = bf16[32,32,160]{2,1,0:T(8,128)(2,1)S(1)} copy(bf16[32,32,160]{2,0,1:T(8,128)(2,1)} %slice.33) | data formatting | bytes 655360 | tf_op jit(solution)/shard_map/slice | solution.py:56
  41.3 0.7 slice.28
  42.1 0.8 collective-permute-start.1
  42.9 0.0 collective-permute-done
  43.0 17.2 %while.28 = (s32[]{:T(128)}, f32[8,5120]{1,0:T(8,128)S(1)}, bf16[8,1280]{1,0:T(8,128)(2,1)S(1)}, f32[5120]{0:T(1024)S(1)}, f32[1280]{0:T(1024)S(1)}, /*index=5*/...) while((s32[]{:T(128)}, f32[8,5120]{1,0:T(8,128)S(1)}, ...), condition=%wide.region_3.4_spmd.clone, body=%wide.region_2.3_spmd.clone.sunk | while | flops 298270720 | bytes 737968 | solution.py:41
  43.0 0.1 dynamic_slice.70
  43.1 8.5 %convolution_add_fusion.5 = f32[8,5120]{1,0:T(8,128)S(1)} fusion(bf16[32,5120]{1,0:T(8,128)(2,1)S(1)} %get-tuple-element.427, f32[640]{0:T(1024)S(1)} %dynamic_slice.70, f32[5120]{0:T(1024)S(1)} %get-tuple-element.424, f32[8,5120]{1,0:T(8,128)S(1)} %get-tuple-element.411, pred[]{:T(512)S(6)} %compare.4, ...), kind=kOutput, calls=%fused_computation.18.clone.1 | convolution fusion | flops 298270720 | bytes 732672 | tf_op jit(solution)/shard_map/while/body/eval_jaxpr/dot_general | solution.py:8
  51.6 0.1 dynamic_slice.70
  51.7 8.5 %convolution_add_fusion.5 = f32[8,5120]{1,0:T(8,128)S(1)} fusion(bf16[32,5120]{1,0:T(8,128)(2,1)S(1)} %get-tuple-element.427, f32[640]{0:T(1024)S(1)} %dynamic_slice.70, f32[5120]{0:T(1024)S(1)} %get-tuple-element.424, f32[8,5120]{1,0:T(8,128)S(1)} %get-tuple-element.411, pred[]{:T(512)S(6)} %compare.4, ...), kind=kOutput, calls=%fused_computation.18.clone.1 | convolution fusion | flops 298270720 | bytes 732672 | tf_op jit(solution)/shard_map/while/body/eval_jaxpr/dot_general | solution.py:8
  60.3 17.5 %while.27 = (s32[]{:T(128)}, f32[8,5120]{1,0:T(8,128)S(1)}, bf16[8,1280]{1,0:T(8,128)(2,1)S(1)}, f32[5120]{0:T(1024)S(1)}, f32[1280]{0:T(1024)S(1)}, /*index=5*/...) while((s32[]{:T(128)}, f32[8,5120]{1,0:T(8,128)S(1)}, ...), condition=%wide.region_6.7_spmd, body=%wide.region_5.6_spmd.sunk | while | flops 298229760 | bytes 737447 | solution.py:41
  60.5 0.1 dynamic_slice.67
  60.6 8.5 %convolution_add_fusion.4 = f32[8,5120]{1,0:T(8,128)S(1)} fusion(f32[8,5120]{1,0:T(8,128)S(1)} %get-tuple-element.444, bf16[32,5120]{1,0:T(8,128)(2,1)S(1)} %get-tuple-element.460, f32[640]{0:T(1024)S(1)} %dynamic_slice.67, f32[5120]{0:T(1024)S(1)} %get-tuple-element.457, bf16[32,1280]{1,0:T(8,128)(2,1)S(1)} %get-tuple-element.459, ...), kind=kOutput, calls=%fused_computation.5.clone.1 | convolution fusion | flops 298229760 | bytes 732160 | tf_op jit(solution)/shard_map/while/body/eval_jaxpr/dot_general | solution.py:8
  69.1 0.1 dynamic_slice.67
  69.2 8.5 %convolution_add_fusion.4 = f32[8,5120]{1,0:T(8,128)S(1)} fusion(f32[8,5120]{1,0:T(8,128)S(1)} %get-tuple-element.444, bf16[32,5120]{1,0:T(8,128)(2,1)S(1)} %get-tuple-element.460, f32[640]{0:T(1024)S(1)} %dynamic_slice.67, f32[5120]{0:T(1024)S(1)} %get-tuple-element.457, bf16[32,1280]{1,0:T(8,128)(2,1)S(1)} %get-tuple-element.459, ...), kind=kOutput, calls=%fused_computation.5.clone.1 | convolution fusion | flops 298229760 | bytes 732160 | tf_op jit(solution)/shard_map/while/body/eval_jaxpr/dot_general | solution.py:8
  77.7 0.1 reshape.15
  77.9 0.2 copy.9
  78.0 30.6 %all_to_all.10 = f32[32,8,160]{2,1,0:T(8,128)S(1)} all-to-all(f32[32,8,160]{2,1,0:T(8,128)S(1)} %copy.9), channel_id=1, replica_groups=mesh['row'=16,'col'=32] {'col'}, dimensions={0} | all-to-all | bytes 327680 | tf_op jit(solution)/shard_map/all_to_all | solution.py:82
  108.6 0.6 reduce_sum.42
  (15 shorter events, 0.1 us)
Async XLA Ops:
  0.0 1.6 %copy-start = (bf16[1024,1024]{1,0:T(8,128)(2,1)S(1)}, bf16[1024,1024]{1,0:T(8,128)(2,1)}, u32[]{:S(2)}) copy-start(bf16[1024,1024]{1,0:T(8,128)(2,1)} %param.12) | copy-start | bytes 6291460
  0.0 3.2 %copy-start.3 = (bf16[1024,32]{0,1:T(8,128)(2,1)S(1)}, bf16[1024,32]{0,1:T(8,128)(2,1)}, u32[]{:S(2)}) copy-start(bf16[1024,32]{0,1:T(8,128)(2,1)} %param.13) | copy-start | bytes 196612
  0.0 3.2 %copy-start.4 = (f32[32]{0:T(128)S(1)}, f32[32]{0:T(128)}, u32[]{:S(2)}) copy-start(f32[32]{0:T(128)} %param.14) | copy-start | bytes 388
  1.6 1.9 %copy-start.2 = (bf16[8,160]{1,0:T(8,128)(2,1)S(1)}, bf16[8,160]{1,0:T(8,128)(2,1)}, u32[]{:S(2)}) copy-start(bf16[8,160]{1,0:T(8,128)(2,1)} %param.15) | copy-start | bytes 7684
  4.4 30.9 %all-to-all-start = ((bf16[32,40,160]{2,1,0:T(8,128)(2,1)}), bf16[32,40,160]{2,1,0:T(8,128)(2,1)S(1)}, u32[]{:S(2)}, u32[]{:S(2)}) async-start(bf16[32,40,160]{2,1,0:T(8,128)(2,1)} %broadcast_in_dim.23), calls=%async_computation | async-start | bytes 1310720 | tf_op jit(solution)/shard_map/all_to_all | solution.py:23
  38.0 5.0 %copy-start.1 = (f32[8,5120]{1,0:T(8,128)S(1)}, f32[8,5120]{1,0:T(8,128)}, u32[]{:S(2)}) copy-start(f32[8,5120]{1,0:T(8,128)} %custom-call) | copy-start | bytes 491524
  39.0 3.9 %collective-permute-start = (bf16[40,1280]{1,0:T(8,128)(2,1)S(1)}, bf16[40,1280]{1,0:T(8,128)(2,1)S(1)}, u32[]{:S(2)}, u32[]{:S(2)}) collective-permute-start(bf16[40,1280]{1,0:T(8,128)(2,1)S(1)} %get-tuple-element.308), channel_id=1, source_target_pairs={{0,0},{1,1},{38,2},{39,3},{68,4},{69,5},{98,6},{99,7},{136,8},{137... | collective-permute-start | bytes 307208 | tf_op jit(solution)/shard_map/ppermute | solution.py:75
  42.1 18.2 %collective-permute-start.1 = (bf16[40,1280]{1,0:T(8,128)(2,1)S(1)}, bf16[40,1280]{1,0:T(8,128)(2,1)S(1)}, u32[]{:S(2)}, u32[]{:S(2)}) collective-permute-start(bf16[40,1280]{1,0:T(8,128)(2,1)S(1)} %get-tuple-element.307), channel_id=1, source_target_pairs={{0,0},{1,1},{38,2},{39,3},{68,4},{69,5},{98,6},{99,7},{136,8},{137... | collective-permute-start | bytes 307208 | tf_op jit(solution)/shard_map/ppermute | solution.py:75

commit v13 on v12

--- a/solution.py
+++ b/solution.py
@@ -59,22 +59,23 @@
     halves = col_peers // row_peers
     span = block.shape[1] // halves
     col = lax.axis_index("col")
-    mine = lax.dynamic_slice_in_dim(block, (col % halves) * span, span, 1)
     z_run = 4
     swap = [0, 3, 2, 1]
-    pairs = []
-    for r in range(row_peers):
-        for c in range(col_peers):
-            chip, core = divmod(c, halves)
-            source_chip = (chip // z_run) * z_run + swap[chip % z_run]
-            source = ((r + chip) % row_peers) * col_peers + source_chip * halves + core
-            pairs.append((source, r * col_peers + c))
-    chunks = 2
+    chunks = halves
     width = span // chunks
-    arrived = [
-        lax.ppermute(mine[:, k * width:(k + 1) * width], ("row", "col"), pairs)
-        for k in range(chunks)
-    ]
+    arrived = []
+    for k in range(chunks):
+        pairs = []
+        for r in range(row_peers):
+            for c in range(col_peers):
+                chip, core = divmod(c, halves)
+                source_chip = (chip // z_run) * z_run + swap[chip % z_run]
+                sender = source_chip * halves + (core + k) % halves
+                source = ((r + chip) % row_peers) * col_peers + sender
+                pairs.append((source, r * col_peers + c))
+        wanted = (col % halves + halves - k) % halves
+        mine = lax.dynamic_slice_in_dim(block, wanted * span + k * width, width, 1)
+        arrived.append(lax.ppermute(mine, ("row", "col"), pairs))
     acc = jnp.zeros((probe_rows, block.shape[1]), jnp.float32)
     for piece in arrived:
         acc = fold_columns(row_feats, row_sq, piece[:feat_dim], piece[feat_dim:], acc, 640)

time: 110 us -> 109 us (level)
  blocking collectives: 30.6 us -> 28.3 us
  starting transfers between devices: 12.9 us -> 14.2 us
    all_to_all x1, blocking collectives: 30.6 us -> 28.3 us  [on_device(): summed = lax.all_to_all(parts, 'col', 0, 0, tiled=False)]
    ppermute x2, starting transfers between devices: 1.52 us -> 2.86 us  [on_device(): arrived.append(lax.ppermute(mine, ('row', 'col'), pairs))]
where the time goes in v13:
time: 109 us; the launch traced here: 108 us
  matrix products  35.9 us (33%)
  blocking collectives  28.3 us (26%)
  waiting for transfers between devices  19.5 us (18%)
  starting transfers between devices  14.2 us (13%)
  local copies, waits for them, and re-layouts  8.99 us (8%)
    dot_general x6, matrix products, dot_f32(): lax.dot_general(left, right, (dims, ((), ())), preferred_element_type=jnp...  35.9 us
    all_to_all x1, blocking collectives, on_device(): summed = lax.all_to_all(parts, 'col', 0, 0, tiled=False)  28.3 us
    all_to_all x1, waiting for transfers between devices, gather_peers(): arrived = lax.all_to_all(spread, axis, 0, 0, tiled=False)  19.5 us
    all_to_all x1, starting transfers between devices, gather_peers(): arrived = lax.all_to_all(spread, axis, 0, 0, tiled=False)  11.4 us
    slice x3, local copies, waits for them, and re-layouts, on_device(): row_feats = block[:feat_dim]  2.94 us
    ppermute x2, starting transfers between devices, on_device(): arrived.append(lax.ppermute(mine, ('row', 'col'), pairs))  2.86 us
  transfers between devices with their start and end apart: 3, of which 1 were waited for; matrix products, arithmetic and copies ran while one was open for 18% of the time, Pallas kernels for 0%

profile of v13, /device:TPU:1, one launch (start us, length us, event | category | flops | bytes accessed | tf_op | source)
XLA Modules:
  0.0 108.4 jit_solution(14908480773721873011)
XLA Ops:
  0.0 1.6 %copy-done = bf16[1024,1024]{1,0:T(8,128)(2,1)S(1)} copy-done((bf16[1024,1024]{1,0:T(8,128)(2,1)S(1)}, bf16[1024,1024]{1,0:T(8,128)(2,1)}, u32[]{:S(2)}) %copy-start) | copy-done | bytes 2097176
  1.6 1.6 %fusion.25 = bf16[160,1024]{1,0:T(8,128)(2,1)S(1)} fusion(bf16[1024,1024]{1,0:T(8,128)(2,1)S(1)} %copy-done, bf16[160,128]{1,0:T(8,128)(2,1)} %param.10, bf16[128,1024]{1,0:T(8,128)(2,1)} %param.11), kind=kOutput, calls=%fused_computation.29 | convolution fusion | flops 378142720 | bytes 2727936 | tf_op jit(solution)/shard_map/dot_general | solution.py:8
  3.2 0.2 fusion.27
  3.4 0.0 copy-done.2
  3.5 0.9 broadcast_in_dim.23
  4.4 11.4 %all-to-all-start = ((bf16[32,40,160]{2,1,0:T(8,128)(2,1)}), bf16[32,40,160]{2,1,0:T(8,128)(2,1)S(1)}, u32[]{:S(2)}, u32[]{:S(2)}) async-start(bf16[32,40,160]{2,1,0:T(8,128)(2,1)} %broadcast_in_dim.23), calls=%async_computation | async-start | bytes 1310720 | tf_op jit(solution)/shard_map/all_to_all | solution.py:23
  15.8 19.5 %all-to-all-done = bf16[32,40,160]{2,1,0:T(8,128)(2,1)S(1)} async-done(((bf16[32,40,160]{2,1,0:T(8,128)(2,1)}), bf16[32,40,160]{2,1,0:T(8,128)(2,1)S(1)}, u32[]{:S(2)}, u32[]{:S(2)}) %all-to-all-start) | async-done | bytes 409632 | tf_op jit(solution)/shard_map/all_to_all | solution.py:23
  35.3 0.1 copy.7
  35.4 0.9 slice.25
  36.3 1.7 %reshape.14 = bf16[40,5120]{1,0:T(8,128)(2,1)} reshape(bf16[40,32,160]{2,1,0:T(8,128)(2,1)S(1)} %copy.7) | data formatting | bytes 819200 | tf_op jit(solution)/shard_map/reshape | solution.py:25
  38.0 1.0 constant_dynamic-slice_fusion
  39.0 0.7 collective-permute-start
  39.7 0.2 multiply_reduce_fusion
  39.9 0.1 reduce_sum.39
  40.0 1.3 %copy.8 = bf16[32,32,160]{2,1,0:T(8,128)(2,1)S(1)} copy(bf16[32,32,160]{2,0,1:T(8,128)(2,1)} %slice.25) | data formatting | bytes 655360 | tf_op jit(solution)/shard_map/slice | solution.py:56
  41.3 0.7 slice.21
  42.1 2.2 %collective-permute-start.1 = (bf16[40,1280]{1,0:T(8,128)(2,1)S(1)}, bf16[40,1280]{1,0:T(8,128)(2,1)S(1)}, u32[]{:S(2)}, u32[]{:S(2)}) collective-permute-start(bf16[40,1280]{1,0:T(8,128)(2,1)S(1)} %get-tuple-element.307), channel_id=1, source_target_pairs={{1,0},{0,1},{39,2},{38,3},{69,4},{68,5},{99,6},{98,7},{137,8},{136... | collective-permute-start | bytes 307208 | tf_op jit(solution)/shard_map/ppermute | solution.py:78
  44.3 0.0 collective-permute-done
  44.3 17.2 %while.28 = (s32[]{:T(128)}, f32[8,5120]{1,0:T(8,128)S(1)}, bf16[8,1280]{1,0:T(8,128)(2,1)S(1)}, f32[5120]{0:T(1024)S(1)}, f32[1280]{0:T(1024)S(1)}, /*index=5*/...) while((s32[]{:T(128)}, f32[8,5120]{1,0:T(8,128)S(1)}, ...), condition=%wide.region_3.4_spmd.clone, body=%wide.region_2.3_spmd.clone.sunk | while | flops 298270720 | bytes 737968 | solution.py:41
  44.4 0.1 dynamic_slice.76
  44.4 8.5 %convolution_add_fusion.5 = f32[8,5120]{1,0:T(8,128)S(1)} fusion(bf16[32,5120]{1,0:T(8,128)(2,1)S(1)} %get-tuple-element.427, f32[640]{0:T(1024)S(1)} %dynamic_slice.76, f32[5120]{0:T(1024)S(1)} %get-tuple-element.424, f32[8,5120]{1,0:T(8,128)S(1)} %get-tuple-element.411, pred[]{:T(512)S(6)} %compare.6, ...), kind=kOutput, calls=%fused_computation.18.clone.1 | convolution fusion | flops 298270720 | bytes 732672 | tf_op jit(solution)/shard_map/while/body/eval_jaxpr/dot_general | solution.py:8
  53.0 0.1 dynamic_slice.76
  53.0 8.5 %convolution_add_fusion.5 = f32[8,5120]{1,0:T(8,128)S(1)} fusion(bf16[32,5120]{1,0:T(8,128)(2,1)S(1)} %get-tuple-element.427, f32[640]{0:T(1024)S(1)} %dynamic_slice.76, f32[5120]{0:T(1024)S(1)} %get-tuple-element.424, f32[8,5120]{1,0:T(8,128)S(1)} %get-tuple-element.411, pred[]{:T(512)S(6)} %compare.6, ...), kind=kOutput, calls=%fused_computation.18.clone.1 | convolution fusion | flops 298270720 | bytes 732672 | tf_op jit(solution)/shard_map/while/body/eval_jaxpr/dot_general | solution.py:8
  61.6 17.5 %while.27 = (s32[]{:T(128)}, f32[8,5120]{1,0:T(8,128)S(1)}, bf16[8,1280]{1,0:T(8,128)(2,1)S(1)}, f32[5120]{0:T(1024)S(1)}, f32[1280]{0:T(1024)S(1)}, /*index=5*/...) while((s32[]{:T(128)}, f32[8,5120]{1,0:T(8,128)S(1)}, ...), condition=%wide.region_6.7_spmd, body=%wide.region_5.6_spmd.sunk | while | flops 298229760 | bytes 737447 | solution.py:41
  61.9 0.1 dynamic_slice.73
  62.0 8.5 %convolution_add_fusion.4 = f32[8,5120]{1,0:T(8,128)S(1)} fusion(f32[8,5120]{1,0:T(8,128)S(1)} %get-tuple-element.444, bf16[32,5120]{1,0:T(8,128)(2,1)S(1)} %get-tuple-element.460, f32[640]{0:T(1024)S(1)} %dynamic_slice.73, f32[5120]{0:T(1024)S(1)} %get-tuple-element.457, bf16[32,1280]{1,0:T(8,128)(2,1)S(1)} %get-tuple-element.459, ...), kind=kOutput, calls=%fused_computation.5.clone.1 | convolution fusion | flops 298229760 | bytes 732160 | tf_op jit(solution)/shard_map/while/body/eval_jaxpr/dot_general | solution.py:8
  70.5 0.1 dynamic_slice.73
  70.6 8.5 %convolution_add_fusion.4 = f32[8,5120]{1,0:T(8,128)S(1)} fusion(f32[8,5120]{1,0:T(8,128)S(1)} %get-tuple-element.444, bf16[32,5120]{1,0:T(8,128)(2,1)S(1)} %get-tuple-element.460, f32[640]{0:T(1024)S(1)} %dynamic_slice.73, f32[5120]{0:T(1024)S(1)} %get-tuple-element.457, bf16[32,1280]{1,0:T(8,128)(2,1)S(1)} %get-tuple-element.459, ...), kind=kOutput, calls=%fused_computation.5.clone.1 | convolution fusion | flops 298229760 | bytes 732160 | tf_op jit(solution)/shard_map/while/body/eval_jaxpr/dot_general | solution.py:8
  79.1 0.1 reshape.15
  79.2 0.2 copy.9
  79.4 28.3 %all_to_all.10 = f32[32,8,160]{2,1,0:T(8,128)S(1)} all-to-all(f32[32,8,160]{2,1,0:T(8,128)S(1)} %copy.9), channel_id=1, replica_groups=mesh['row'=16,'col'=32] {'col'}, dimensions={0} | all-to-all | bytes 327680 | tf_op jit(solution)/shard_map/all_to_all | solution.py:83
  107.7 0.6 reduce_sum.42
  (15 shorter events, 0.1 us)
Async XLA Ops:
  0.0 1.6 %copy-start = (bf16[1024,1024]{1,0:T(8,128)(2,1)S(1)}, bf16[1024,1024]{1,0:T(8,128)(2,1)}, u32[]{:S(2)}) copy-start(bf16[1024,1024]{1,0:T(8,128)(2,1)} %param.12) | copy-start | bytes 6291460
  0.0 3.2 %copy-start.3 = (bf16[1024,32]{0,1:T(8,128)(2,1)S(1)}, bf16[1024,32]{0,1:T(8,128)(2,1)}, u32[]{:S(2)}) copy-start(bf16[1024,32]{0,1:T(8,128)(2,1)} %param.13) | copy-start | bytes 196612
  0.0 3.2 %copy-start.4 = (f32[32]{0:T(128)S(1)}, f32[32]{0:T(128)}, u32[]{:S(2)}) copy-start(f32[32]{0:T(128)} %param.14) | copy-start | bytes 388
  1.6 1.9 %copy-start.2 = (bf16[8,160]{1,0:T(8,128)(2,1)S(1)}, bf16[8,160]{1,0:T(8,128)(2,1)}, u32[]{:S(2)}) copy-start(bf16[8,160]{1,0:T(8,128)(2,1)} %param.15) | copy-start | bytes 7684
  4.4 30.9 %all-to-all-start = ((bf16[32,40,160]{2,1,0:T(8,128)(2,1)}), bf16[32,40,160]{2,1,0:T(8,128)(2,1)S(1)}, u32[]{:S(2)}, u32[]{:S(2)}) async-start(bf16[32,40,160]{2,1,0:T(8,128)(2,1)} %broadcast_in_dim.23), calls=%async_computation | async-start | bytes 1310720 | tf_op jit(solution)/shard_map/all_to_all | solution.py:23
  38.0 6.3 %copy-start.1 = (f32[8,5120]{1,0:T(8,128)S(1)}, f32[8,5120]{1,0:T(8,128)}, u32[]{:S(2)}) copy-start(f32[8,5120]{1,0:T(8,128)} %custom-call) | copy-start | bytes 491524
  39.0 5.2 %collective-permute-start = (bf16[40,1280]{1,0:T(8,128)(2,1)S(1)}, bf16[40,1280]{1,0:T(8,128)(2,1)S(1)}, u32[]{:S(2)}, u32[]{:S(2)}) collective-permute-start(bf16[40,1280]{1,0:T(8,128)(2,1)S(1)} %get-tuple-element.308), channel_id=1, source_target_pairs={{0,0},{1,1},{38,2},{39,3},{68,4},{69,5},{98,6},{99,7},{136,8},{137... | collective-permute-start | bytes 307208 | tf_op jit(solution)/shard_map/ppermute | solution.py:78
  42.1 19.5 %collective-permute-start.1 = (bf16[40,1280]{1,0:T(8,128)(2,1)S(1)}, bf16[40,1280]{1,0:T(8,128)(2,1)S(1)}, u32[]{:S(2)}, u32[]{:S(2)}) collective-permute-start(bf16[40,1280]{1,0:T(8,128)(2,1)S(1)} %get-tuple-element.307), channel_id=1, source_target_pairs={{1,0},{0,1},{39,2},{38,3},{69,4},{68,5},{99,6},{98,7},{137,8},{136... | collective-permute-start | bytes 307208 | tf_op jit(solution)/shard_map/ppermute | solution.py:78

commit v14 on v13

--- a/solution.py
+++ b/solution.py
@@ -61,7 +61,8 @@
     col = lax.axis_index("col")
     z_run = 4
     swap = [0, 3, 2, 1]
-    chunks = halves
+    swaps = [swap, [1, 2, 3, 0]]
+    chunks = 2 * halves
     width = span // chunks
     arrived = []
     for k in range(chunks):
@@ -69,7 +70,7 @@
         for r in range(row_peers):
             for c in range(col_peers):
                 chip, core = divmod(c, halves)
-                source_chip = (chip // z_run) * z_run + swap[chip % z_run]
+                source_chip = (chip // z_run) * z_run + swaps[k // halves][chip % z_run]
                 sender = source_chip * halves + (core + k) % halves
                 source = ((r + chip) % row_peers) * col_peers + sender
                 pairs.append((source, r * col_peers + c))
@@ -78,7 +79,7 @@
         arrived.append(lax.ppermute(mine, ("row", "col"), pairs))
     acc = jnp.zeros((probe_rows, block.shape[1]), jnp.float32)
     for piece in arrived:
-        acc = fold_columns(row_feats, row_sq, piece[:feat_dim], piece[feat_dim:], acc, 640)
+        acc = fold_columns(row_feats, row_sq, piece[:feat_dim], piece[feat_dim:], acc, 320)
     parts = jnp.transpose(acc.reshape(probe_rows, col_peers, local), (1, 0, 2))
     summed = lax.all_to_all(parts, "col", 0, 0, tiled=False)
     return jnp.sum(summed, axis=0)

time: 109 us -> 124 us (1.14)
  starting transfers between devices: 14.2 us -> 32.4 us
  blocking collectives: 28.3 us -> 21.8 us
  matrix products: 35.9 us -> 38.4 us
    ppermute x2 -> x4, starting transfers between devices: 2.86 us -> 21 us  [on_device(): arrived.append(lax.ppermute(mine, ('row', 'col'), pairs))]
    all_to_all x1, blocking collectives: 28.3 us -> 21.8 us  [on_device(): summed = lax.all_to_all(parts, 'col', 0, 0, tiled=False)]
    dot_general x6 -> x10, matrix products: 35.9 us -> 38.4 us  [dot_f32(): lax.dot_general(left, right, (dims, ((), ())), preferred_element_type=jnp...]
    slice x3, local copies, waits for them, and re-layouts: 2.94 us -> 1.09 us  [on_device(): row_feats = block[:feat_dim]]
  transfers between devices with their start and end apart: 3 -> 5, of which waited for: 1 -> 1; matrix products, arithmetic and copies ran while one was open for 18% -> 25% of each run, Pallas kernels for 0% -> 0%
where the time goes in v14:
time: 124 us; the launch traced here: 123 us
  matrix products  38.4 us (31%)
  starting transfers between devices  32.4 us (26%)
  blocking collectives  21.8 us (18%)
  waiting for transfers between devices  19.5 us (16%)
  local copies, waits for them, and re-layouts  8.75 us (7%)
  other arithmetic  1.69 us (1%)
    dot_general x10, matrix products, dot_f32(): lax.dot_general(left, right, (dims, ((), ())), preferred_element_type=jnp...  38.4 us
    all_to_all x1, blocking collectives, on_device(): summed = lax.all_to_all(parts, 'col', 0, 0, tiled=False)  21.8 us
    ppermute x4, starting transfers between devices, on_device(): arrived.append(lax.ppermute(mine, ('row', 'col'), pairs))  21 us
    all_to_all x1, waiting for transfers between devices, gather_peers(): arrived = lax.all_to_all(spread, axis, 0, 0, tiled=False)  19.5 us
    all_to_all x1, starting transfers between devices, gather_peers(): arrived = lax.all_to_all(spread, axis, 0, 0, tiled=False)  11.4 us
  transfers between devices with their start and end apart: 5, of which 1 were waited for; matrix products, arithmetic and copies ran while one was open for 25% of the time, Pallas kernels for 0%

profile of v14, /device:TPU:1, one launch (start us, length us, event | category | flops | bytes accessed | tf_op | source)
XLA Modules:
  0.0 123.1 jit_solution(14602051779343852986)
XLA Ops:
  0.0 1.6 %copy-done = bf16[1024,1024]{1,0:T(8,128)(2,1)S(1)} copy-done((bf16[1024,1024]{1,0:T(8,128)(2,1)S(1)}, bf16[1024,1024]{1,0:T(8,128)(2,1)}, u32[]{:S(2)}) %copy-start) | copy-done | bytes 2097176
  1.6 1.6 %fusion.53 = bf16[160,1024]{1,0:T(8,128)(2,1)S(1)} fusion(bf16[1024,1024]{1,0:T(8,128)(2,1)S(1)} %copy-done, bf16[160,128]{1,0:T(8,128)(2,1)} %param.14, bf16[128,1024]{1,0:T(8,128)(2,1)} %param.15), kind=kOutput, calls=%fused_computation.59 | convolution fusion | flops 378142720 | bytes 2727936 | tf_op jit(solution)/shard_map/dot_general | solution.py:8
  3.2 0.2 fusion.55
  3.5 0.9 broadcast_in_dim.35
  4.4 11.4 %all-to-all-start = ((bf16[32,40,160]{2,1,0:T(8,128)(2,1)}), bf16[32,40,160]{2,1,0:T(8,128)(2,1)S(1)}, u32[]{:S(2)}, u32[]{:S(2)}) async-start(bf16[32,40,160]{2,1,0:T(8,128)(2,1)} %broadcast_in_dim.35), calls=%async_computation | async-start | bytes 1310720 | tf_op jit(solution)/shard_map/all_to_all | solution.py:23
  15.8 19.5 %all-to-all-done = bf16[32,40,160]{2,1,0:T(8,128)(2,1)S(1)} async-done(((bf16[32,40,160]{2,1,0:T(8,128)(2,1)}), bf16[32,40,160]{2,1,0:T(8,128)(2,1)S(1)}, u32[]{:S(2)}, u32[]{:S(2)}) %all-to-all-start) | async-done | bytes 409632 | tf_op jit(solution)/shard_map/all_to_all | solution.py:23
  35.4 1.7 %reshape.18 = bf16[40,5120]{1,0:T(8,128)(2,1)} reshape(bf16[40,32,160]{2,1,0:T(8,128)(2,1)S(1)} %copy.7) | data formatting | bytes 819200 | tf_op jit(solution)/shard_map/reshape | solution.py:25
  37.2 1.6 %constant_dynamic-slice_fusion = (bf16[40,640]{1,0:T(8,128)(2,1)S(1)}, bf16[40,640]{1,0:T(8,128)(2,1)}, bf16[40,640]{1,0:T(8,128)(2,1)}, bf16[40,640]{1,0:T(8,128)(2,1)}) fusion(bf16[40,5120]{1,0:T(8,128)(2,1)} %reshape.18, s32[]{:T(128)S(6)} %select_n.85, s32[]{:T(128)S(6)} %select_n.83, s32[]{:T(128)S(6)} %select_n.81, s32[]{:T(128)S(6)} %select_n.79), kind=kLoop, calls=%fused_computation.82 | loop fusion | bytes 409616 | tf_op jit(solution)/shard_map/dynamic_slice | solution.py:78
  38.8 2.1 %collective-permute-start = (bf16[40,640]{1,0:T(8,128)(2,1)}, bf16[40,640]{1,0:T(8,128)(2,1)}, u32[]{:S(2)}, u32[]{:S(2)}) collective-permute-start(bf16[40,640]{1,0:T(8,128)(2,1)} %get-tuple-element.588), channel_id=1, source_target_pairs={{0,0},{1,1},{38,2},{39,3},{68,4},{69,5},{98,6},{99,7},{136,8},{137... | collective-permute-start | bytes 153608 | tf_op jit(solution)/shard_map/ppermute | solution.py:79
  40.8 0.2 multiply_reduce_fusion
  41.1 0.3 copy.8
  41.4 0.7 slice.33
  42.2 2.0 %collective-permute-start.1 = (bf16[40,640]{1,0:T(8,128)(2,1)}, bf16[40,640]{1,0:T(8,128)(2,1)S(1)}, u32[]{:S(2)}, u32[]{:S(2)}) collective-permute-start(bf16[40,640]{1,0:T(8,128)(2,1)} %get-tuple-element.587), channel_id=1, source_target_pairs={{1,0},{0,1},{39,2},{38,3},{69,4},{68,5},{99,6},{98,7},{137,8},{136... | collective-permute-start | bytes 153608 | tf_op jit(solution)/shard_map/ppermute | solution.py:79
  44.2 13.1 %collective-permute-start.2 = (bf16[40,640]{1,0:T(8,128)(2,1)}, bf16[40,640]{1,0:T(8,128)(2,1)S(1)}, u32[]{:S(2)}, u32[]{:S(2)}) collective-permute-start(bf16[40,640]{1,0:T(8,128)(2,1)} %get-tuple-element.586), channel_id=1, source_target_pairs={{2,0},{3,1},{36,2},{37,3},{70,4},{71,5},{96,6},{97,7},{138,8},{139... | collective-permute-start | bytes 153608 | tf_op jit(solution)/shard_map/ppermute | solution.py:79
  57.4 3.8 %collective-permute-start.3 = (bf16[40,640]{1,0:T(8,128)(2,1)S(1)}, bf16[40,640]{1,0:T(8,128)(2,1)S(1)}, u32[]{:S(2)}, u32[]{:S(2)}) collective-permute-start(bf16[40,640]{1,0:T(8,128)(2,1)S(1)} %get-tuple-element.585), channel_id=1, source_target_pairs={{3,0},{2,1},{37,2},{36,3},{71,4},{70,5},{97,6},{96,7},{139,8},{138... | collective-permute-start | bytes 153608 | tf_op jit(solution)/shard_map/ppermute | solution.py:79
  61.2 0.7 slice.40
  61.9 0.8 fusion.58
  62.7 9.2 %while.56 = (s32[]{:T(128)}, f32[8,5120]{1,0:T(8,128)S(1)}, bf16[8,640]{1,0:T(8,128)(2,1)S(1)}, f32[5120]{0:T(1024)S(1)}, f32[640]{0:T(1024)S(1)}, /*index=5*/bf...) while((s32[]{:T(128)}, f32[8,5120]{1,0:T(8,128)S(1)}, ...), condition=%wide.region_3.4_spmd.clone, body=%wide.region_2.3_spmd.clone.sunk | while | flops 149176320 | bytes 712880 | solution.py:41
  62.8 4.5 %convolution_add_fusion.11 = f32[8,5120]{1,0:T(8,128)S(1)} fusion(bf16[32,5120]{1,0:T(8,128)(2,1)S(1)} %get-tuple-element.797, f32[320]{0:T(512)S(1)} %dynamic_slice.150, f32[5120]{0:T(1024)S(1)} %get-tuple-element.794, f32[8,5120]{1,0:T(8,128)S(1)} %get-tuple-element.781, pred[]{:T(512)S(6)} %compare.8, ...), kind=kOutput, calls=%fused_computation.48.clone.1 | convolution fusion | flops 149176320 | bytes 710144 | tf_op jit(solution)/shard_map/while/body/eval_jaxpr/dot_general | solution.py:8
  67.4 4.5 %convolution_add_fusion.11 = f32[8,5120]{1,0:T(8,128)S(1)} fusion(bf16[32,5120]{1,0:T(8,128)(2,1)S(1)} %get-tuple-element.797, f32[320]{0:T(512)S(1)} %dynamic_slice.150, f32[5120]{0:T(1024)S(1)} %get-tuple-element.794, f32[8,5120]{1,0:T(8,128)S(1)} %get-tuple-element.781, pred[]{:T(512)S(6)} %compare.8, ...), kind=kOutput, calls=%fused_computation.48.clone.1 | convolution fusion | flops 149176320 | bytes 710144 | tf_op jit(solution)/shard_map/while/body/eval_jaxpr/dot_general | solution.py:8
  72.0 9.3 %while.53 = (s32[]{:T(128)}, f32[8,5120]{1,0:T(8,128)S(1)}, bf16[8,640]{1,0:T(8,128)(2,1)S(1)}, f32[5120]{0:T(1024)S(1)}, f32[640]{0:T(1024)S(1)}, /*index=5*/bf...) while((s32[]{:T(128)}, f32[8,5120]{1,0:T(8,128)S(1)}, ...), condition=%wide.region_6.7_spmd, body=%wide.region_5.6_spmd.sunk | while | flops 149135360 | bytes 712359 | solution.py:41
  72.1 4.6 %convolution_add_fusion.8 = f32[8,5120]{1,0:T(8,128)S(1)} fusion(f32[8,5120]{1,0:T(8,128)S(1)} %get-tuple-element.814, bf16[32,5120]{1,0:T(8,128)(2,1)S(1)} %get-tuple-element.830, f32[320]{0:T(512)S(1)} %dynamic_slice.141, f32[5120]{0:T(1024)S(1)} %get-tuple-element.827, bf16[32,640]{1,0:T(8,128)(2,1)S(1)} %get-tuple-element.829, s32[]{:T(128)S(6)} %select_n.91, ...), kind=kOutput, calls=%fused_computation.6.clone.1 | convolution fusion | flops 149135360 | bytes 709632 | tf_op jit(solution)/shard_map/while/body/eval_jaxpr/dot_general | solution.py:8
  76.7 4.6 %convolution_add_fusion.8 = f32[8,5120]{1,0:T(8,128)S(1)} fusion(f32[8,5120]{1,0:T(8,128)S(1)} %get-tuple-element.814, bf16[32,5120]{1,0:T(8,128)(2,1)S(1)} %get-tuple-element.830, f32[320]{0:T(512)S(1)} %dynamic_slice.141, f32[5120]{0:T(1024)S(1)} %get-tuple-element.827, bf16[32,640]{1,0:T(8,128)(2,1)S(1)} %get-tuple-element.829, s32[]{:T(128)S(6)} %select_n.91, ...), kind=kOutput, calls=%fused_computation.6.clone.1 | convolution fusion | flops 149135360 | bytes 709632 | tf_op jit(solution)/shard_map/while/body/eval_jaxpr/dot_general | solution.py:8
  81.3 9.6 %while.54 = (s32[]{:T(128)}, f32[8,5120]{1,0:T(8,128)S(1)}, bf16[8,640]{1,0:T(8,128)(2,1)S(1)}, f32[5120]{0:T(1024)S(1)}, f32[640]{0:T(1024)S(1)}, /*index=5*/bf...) while((s32[]{:T(128)}, f32[8,5120]{1,0:T(8,128)S(1)}, ...), condition=%wide.region_9.10_spmd, body=%wide.region_8.9_spmd.sunk | while | flops 149135360 | bytes 712359 | solution.py:41
  81.7 4.6 %convolution_add_fusion.9 = f32[8,5120]{1,0:T(8,128)S(1)} fusion(f32[8,5120]{1,0:T(8,128)S(1)} %get-tuple-element.847, bf16[32,5120]{1,0:T(8,128)(2,1)S(1)} %get-tuple-element.863, f32[320]{0:T(512)S(1)} %dynamic_slice.144, f32[5120]{0:T(1024)S(1)} %get-tuple-element.860, bf16[32,640]{1,0:T(8,128)(2,1)S(1)} %get-tuple-element.862, ...), kind=kOutput, calls=%fused_computation.20.clone.1 | convolution fusion | flops 149135360 | bytes 709632 | tf_op jit(solution)/shard_map/while/body/eval_jaxpr/dot_general | solution.py:8
  86.4 4.6 %convolution_add_fusion.9 = f32[8,5120]{1,0:T(8,128)S(1)} fusion(f32[8,5120]{1,0:T(8,128)S(1)} %get-tuple-element.847, bf16[32,5120]{1,0:T(8,128)(2,1)S(1)} %get-tuple-element.863, f32[320]{0:T(512)S(1)} %dynamic_slice.144, f32[5120]{0:T(1024)S(1)} %get-tuple-element.860, bf16[32,640]{1,0:T(8,128)(2,1)S(1)} %get-tuple-element.862, ...), kind=kOutput, calls=%fused_computation.20.clone.1 | convolution fusion | flops 149135360 | bytes 709632 | tf_op jit(solution)/shard_map/while/body/eval_jaxpr/dot_general | solution.py:8
  91.0 9.3 %while.55 = (s32[]{:T(128)}, f32[8,5120]{1,0:T(8,128)S(1)}, bf16[8,640]{1,0:T(8,128)(2,1)S(1)}, f32[5120]{0:T(1024)S(1)}, f32[640]{0:T(1024)S(1)}, /*index=5*/bf...) while((s32[]{:T(128)}, f32[8,5120]{1,0:T(8,128)S(1)}, ...), condition=%wide.region_12.13_spmd, body=%wide.region_11.12_spmd.sunk | while | flops 149135360 | bytes 712359 | solution.py:41
  91.1 4.6 %convolution_add_fusion.10 = f32[8,5120]{1,0:T(8,128)S(1)} fusion(f32[8,5120]{1,0:T(8,128)S(1)} %get-tuple-element.880, bf16[32,5120]{1,0:T(8,128)(2,1)S(1)} %get-tuple-element.896, f32[320]{0:T(512)S(1)} %dynamic_slice.147, f32[5120]{0:T(1024)S(1)} %get-tuple-element.893, bf16[32,640]{1,0:T(8,128)(2,1)S(1)} %get-tuple-element.895, ...), kind=kOutput, calls=%fused_computation.34.clone.1 | convolution fusion | flops 149135360 | bytes 709632 | tf_op jit(solution)/shard_map/while/body/eval_jaxpr/dot_general | solution.py:8
  95.7 4.6 %convolution_add_fusion.10 = f32[8,5120]{1,0:T(8,128)S(1)} fusion(f32[8,5120]{1,0:T(8,128)S(1)} %get-tuple-element.880, bf16[32,5120]{1,0:T(8,128)(2,1)S(1)} %get-tuple-element.896, f32[320]{0:T(512)S(1)} %dynamic_slice.147, f32[5120]{0:T(1024)S(1)} %get-tuple-element.893, bf16[32,640]{1,0:T(8,128)(2,1)S(1)} %get-tuple-element.895, ...), kind=kOutput, calls=%fused_computation.34.clone.1 | convolution fusion | flops 149135360 | bytes 709632 | tf_op jit(solution)/shard_map/while/body/eval_jaxpr/dot_general | solution.py:8
  100.5 0.2 copy.9
  100.6 21.8 %all_to_all.10 = f32[32,8,160]{2,1,0:T(8,128)S(1)} all-to-all(f32[32,8,160]{2,1,0:T(8,128)S(1)} %copy.9), channel_id=1, replica_groups=mesh['row'=16,'col'=32] {'col'}, dimensions={0} | all-to-all | bytes 327680 | tf_op jit(solution)/shard_map/all_to_all | solution.py:84
  122.5 0.6 reduce_sum.62
  (33 shorter events, 1.2 us)
Async XLA Ops:
  0.0 1.6 %copy-start = (bf16[1024,1024]{1,0:T(8,128)(2,1)S(1)}, bf16[1024,1024]{1,0:T(8,128)(2,1)}, u32[]{:S(2)}) copy-start(bf16[1024,1024]{1,0:T(8,128)(2,1)} %param.16) | copy-start | bytes 6291460
  0.0 3.2 %copy-start.3 = (bf16[1024,32]{0,1:T(8,128)(2,1)S(1)}, bf16[1024,32]{0,1:T(8,128)(2,1)}, u32[]{:S(2)}) copy-start(bf16[1024,32]{0,1:T(8,128)(2,1)} %param.17) | copy-start | bytes 196612
  0.0 3.2 %copy-start.4 = (f32[32]{0:T(128)S(1)}, f32[32]{0:T(128)}, u32[]{:S(2)}) copy-start(f32[32]{0:T(128)} %param.18) | copy-start | bytes 388
  1.6 1.9 %copy-start.2 = (bf16[8,160]{1,0:T(8,128)(2,1)S(1)}, bf16[8,160]{1,0:T(8,128)(2,1)}, u32[]{:S(2)}) copy-start(bf16[8,160]{1,0:T(8,128)(2,1)} %param.19) | copy-start | bytes 7684
  4.4 30.9 %all-to-all-start = ((bf16[32,40,160]{2,1,0:T(8,128)(2,1)}), bf16[32,40,160]{2,1,0:T(8,128)(2,1)S(1)}, u32[]{:S(2)}, u32[]{:S(2)}) async-start(bf16[32,40,160]{2,1,0:T(8,128)(2,1)} %broadcast_in_dim.35), calls=%async_computation | async-start | bytes 1310720 | tf_op jit(solution)/shard_map/all_to_all | solution.py:23
  37.2 25.5 %copy-start.1 = (f32[8,5120]{1,0:T(8,128)S(1)}, f32[8,5120]{1,0:T(8,128)}, u32[]{:S(2)}) copy-start(f32[8,5120]{1,0:T(8,128)} %custom-call) | copy-start | bytes 491524
  38.8 22.4 %collective-permute-start = (bf16[40,640]{1,0:T(8,128)(2,1)}, bf16[40,640]{1,0:T(8,128)(2,1)}, u32[]{:S(2)}, u32[]{:S(2)}) collective-permute-start(bf16[40,640]{1,0:T(8,128)(2,1)} %get-tuple-element.588), channel_id=1, source_target_pairs={{0,0},{1,1},{38,2},{39,3},{68,4},{69,5},{98,6},{99,7},{136,8},{137... | collective-permute-start | bytes 153608 | tf_op jit(solution)/shard_map/ppermute | solution.py:79
  42.2 29.7 %collective-permute-start.1 = (bf16[40,640]{1,0:T(8,128)(2,1)}, bf16[40,640]{1,0:T(8,128)(2,1)S(1)}, u32[]{:S(2)}, u32[]{:S(2)}) collective-permute-start(bf16[40,640]{1,0:T(8,128)(2,1)} %get-tuple-element.587), channel_id=1, source_target_pairs={{1,0},{0,1},{39,2},{38,3},{69,4},{68,5},{99,6},{98,7},{137,8},{136... | collective-permute-start | bytes 153608 | tf_op jit(solution)/shard_map/ppermute | solution.py:79
  44.2 37.1 %collective-permute-start.2 = (bf16[40,640]{1,0:T(8,128)(2,1)}, bf16[40,640]{1,0:T(8,128)(2,1)S(1)}, u32[]{:S(2)}, u32[]{:S(2)}) collective-permute-start(bf16[40,640]{1,0:T(8,128)(2,1)} %get-tuple-element.586), channel_id=1, source_target_pairs={{2,0},{3,1},{36,2},{37,3},{70,4},{71,5},{96,6},{97,7},{138,8},{139... | collective-permute-start | bytes 153608 | tf_op jit(solution)/shard_map/ppermute | solution.py:79
  57.4 33.6 %collective-permute-start.3 = (bf16[40,640]{1,0:T(8,128)(2,1)S(1)}, bf16[40,640]{1,0:T(8,128)(2,1)S(1)}, u32[]{:S(2)}, u32[]{:S(2)}) collective-permute-start(bf16[40,640]{1,0:T(8,128)(2,1)S(1)} %get-tuple-element.585), channel_id=1, source_target_pairs={{3,0},{2,1},{37,2},{36,3},{71,4},{70,5},{97,6},{96,7},{139,8},{138... | collective-permute-start | bytes 153608 | tf_op jit(solution)/shard_map/ppermute | solution.py:79
